TPU v7x, 768 devices: a whole 4x8x12 slice. The times are simulated.
768 devices in a mesh: row: 64 (over y, x, core), col: 12 (over z).
Axes of the slice: x: 4, y: 8, z: 12, core: 2. Of those that a mesh axis runs over, the one named last changes fastest.
Arguments:
- qkv: bfloat16 [12, 8192, 1920], P('col', 'row'), may hold values from -20 to 20
- cotangent: bfloat16 [12, 8192, 1280], P('col', 'row'), may hold values from -6 to 6
- out_weight: bfloat16 [640, 1280], replicated, may hold values from -0.25 to 0.25
- live_patches: int32 [12, 64], P('col', 'row'), may hold values from 1 to 128, as said below
Outputs:
- output: bfloat16 [12, 8192, 1280], P('col', 'row')
- d_qkv: bfloat16 [12, 8192, 1920], P('col', 'row')
- d_weight: float32 [640, 1280], P('row')
Inputs may be any that keep to these rules, and one draw needn't show every extreme that they name: `live_patches`: patches beyond a rank's count are padding; some rank holds 128 live patches.
All inputs are finite; a program needn't handle non-finite values.
Results may differ from a plain program's by a relative error of at most 0.007.
Values may be sent and summed in bfloat16 or wider, within the bound.
No kernel may reach another device: no remote copies, remote signals or barrier semaphores. Data moves between devices by JAX's collectives and lax.ppermute only.
A program may use at most 64 MiB of HBM per device.

v0:
```python
import jax
import jax.numpy as jnp
from jax import lax
from jax.sharding import PartitionSpec as P

HD = 80
H = 8
WIN = 64


def unit_attention(unit_block, keys_live):
    head_channels = unit_block.shape[-1] // 3
    window_len = unit_block.shape[1]
    query_matrix = unit_block[..., :head_channels].astype(jnp.float32)
    key_matrix = unit_block[..., head_channels : 2 * head_channels].astype(jnp.float32)
    value_matrix = unit_block[..., 2 * head_channels :].astype(jnp.float32)
    places = jnp.arange(window_len, dtype=jnp.int32)
    key_alive = places[None, :] < keys_live[:, None]
    attention_logits = jnp.einsum(
        "ohc,opc->ohp", query_matrix, key_matrix, precision=lax.Precision.HIGHEST
    ) * head_channels ** (-0.5)
    attention_logits = jnp.where(key_alive[:, None, :], attention_logits, -1e30)
    row_peak = jnp.max(attention_logits, axis=-1, keepdims=True)
    weights = jnp.exp(attention_logits - row_peak)
    row_total = jnp.sum(weights, axis=-1, keepdims=True)
    attention_probabilities = (weights / row_total).astype(jnp.bfloat16)
    attended_values = jnp.einsum(
        "gcn,gnu->gcu",
        attention_probabilities.astype(jnp.float32),
        value_matrix,
        precision=lax.Precision.HIGHEST,
    )
    attended_values = jnp.where(key_alive[:, :, None], attended_values, 0.0)
    return attended_values.astype(jnp.bfloat16)


def unit_gradient(unit_block, keys_live, grad_block):
    ignored, pullback = jax.vjp(
        lambda block_units: unit_attention(block_units, keys_live), unit_block
    )
    return pullback(grad_block)[0]


def tokens_to_units(token_rows, head_channels):
    window_count = token_rows.shape[0] // WIN
    shaped = token_rows.reshape(window_count, WIN, H, head_channels)
    return shaped.transpose(0, 2, 1, 3).reshape(window_count * H, WIN, head_channels)


def units_to_tokens(unit_rows, head_channels):
    window_count = unit_rows.shape[0] // H
    shaped = unit_rows.reshape(window_count, H, WIN, head_channels)
    return shaped.transpose(0, 2, 1, 3).reshape(window_count * WIN, H * head_channels)


def body(qkv, cotangent, out_weight, live_patches):
    token_count = qkv.shape[1]
    unit_count = token_count // WIN * H
    home_units = tokens_to_units(qkv[0], 3 * HD)
    live_count = live_patches[0, 0]
    unit_ids = jnp.arange(unit_count, dtype=jnp.int32)
    home_live = jnp.clip(live_count - unit_ids // H * WIN, 0, WIN)
    live_windows = (live_count + WIN - 1) // WIN
    grad_attended = lax.dot_general(
        cotangent[0], out_weight, (((1,), (1,)), ((), ())), preferred_element_type=jnp.float32
    ).astype(jnp.bfloat16)
    grad_units = tokens_to_units(grad_attended, HD)
    rank_total = lax.axis_size("row")
    my_rank = lax.axis_index("row")
    per_peer = -(-unit_count // rank_total)
    slot_total = rank_total * per_peer
    slot_ids = jnp.arange(slot_total, dtype=jnp.int32)
    target_rank = slot_ids // per_peer
    target_turn = slot_ids % per_peer
    local_id = (target_rank - my_rank * H) % rank_total + target_turn * rank_total
    valid = local_id < live_windows * H
    safe_id = jnp.where(valid, local_id, 0)
    send_units = home_units[safe_id].reshape(slot_total, -1)
    send_live = jnp.where(valid, home_live[safe_id], 0).astype(jnp.bfloat16)
    recv_units, recv_live = (
        lax.all_to_all(send_units, "row", split_axis=0, concat_axis=0, tiled=True),
        lax.all_to_all(send_live, "row", split_axis=0, concat_axis=0, tiled=True),
    )
    live_int = recv_live.astype(jnp.int32)
    arrived = recv_units.reshape(slot_total, WIN, 3 * HD)
    done_units = unit_attention(arrived, live_int)
    send_grads = grad_units[safe_id].reshape(slot_total, -1)
    returned, recv_grads = (
        lax.all_to_all(
            done_units.reshape(slot_total, -1), "row", split_axis=0, concat_axis=0, tiled=True
        ),
        lax.all_to_all(send_grads, "row", split_axis=0, concat_axis=0, tiled=True),
    )
    target_home = jnp.where(valid, local_id, unit_count)
    attended_units = (
        jnp.zeros((unit_count, WIN, HD), jnp.bfloat16)
        .at[target_home]
        .set(returned.reshape(slot_total, WIN, HD), mode="drop")
    )
    grads_arrived = recv_grads.reshape(slot_total, WIN, HD)
    grad_slots = unit_gradient(arrived, live_int, grads_arrived)
    grads_home = lax.all_to_all(
        grad_slots.reshape(slot_total, -1), "row", split_axis=0, concat_axis=0, tiled=True
    )
    d_units = (
        jnp.zeros((unit_count, WIN, 3 * HD), jnp.bfloat16)
        .at[target_home]
        .set(grads_home.reshape(slot_total, WIN, 3 * HD), mode="drop")
    )
    attended_values = units_to_tokens(attended_units, HD)
    output = jnp.dot(attended_values, out_weight, preferred_element_type=jnp.float32).astype(
        jnp.bfloat16
    )
    d_qkv = units_to_tokens(d_units, 3 * HD)
    grad_rows = cotangent[0]
    row_share = lax.psum_scatter(
        lax.dot_general(
            attended_values, grad_rows, (((0,), (0,)), ((), ())), preferred_element_type=jnp.float32
        ),
        "row",
        scatter_dimension=0,
        tiled=True,
    )
    scale = (lax.axis_size("col") * lax.axis_size("row") * token_count) ** (-0.5)
    d_weight = lax.psum(row_share, "col") * scale
    return (output[None], d_qkv[None], d_weight)


def solution(mesh):
    in_specs = (P("col", "row", None), P("col", "row", None), P(), P("col", "row"))
    out_specs = (P("col", "row", None), P("col", "row", None), P("row", None))
    return jax.shard_map(body, mesh=mesh, in_specs=in_specs, out_specs=out_specs, check_vma=False)
```

profile of v0, /device:TPU:2, one launch (start us, length us, event | category | flops | bytes accessed | tf_op | source)
XLA Modules:
  0.0 594.2 jit_solution(11884766811682356621)
XLA Ops:
  8.0 0.8 gather_fusion
  8.8 0.7 copy.29
  9.5 13.6 %all-to-all-start = ((bf16[64,1,1]{2,1,0:T(2,128)(2,1)}), bf16[64,1,1]{2,1,0:T(2,128)(2,1)S(1)}, u32[]{:S(2)}, u32[]{:S(2)}) async-start(bf16[64,1,1]{2,1,0:T(2,128)(2,1)} %copy.29), calls=%async_computation | async-start | bytes 65536 | tf_op jit(solution)/shard_map/all_to_all | solution.py:82
  23.1 1.6 convolution_convert_fusion.3
  24.7 0.3 reshape.244
  25.1 1.7 gather_fusion.2
  26.7 4.6 all_to_all.39
  31.4 0.5 broadcast.387
  31.9 5.4 reduce.9
  37.3 3.0 reshape.300
  40.3 10.7 %all-to-all-start.3 = ((bf16[64,2,2560]{2,1,0:T(2,128)(2,1)}), bf16[64,2,2560]{2,1,0:T(2,128)(2,1)S(1)}, u32[]{:S(2)}, u32[]{:S(2)}) async-start(bf16[64,2,2560]{2,1,0:T(2,128)(2,1)} %reshape.300), calls=%async_computation.3 | async-start | bytes 1310720 | tf_op jit(solution)/shard_map/all_to_all | solution.py:92
  51.1 0.9 reshape_squeeze.3
  52.0 0.1 copy.30
  52.1 2.0 gather_fusion.1
  54.1 11.3 %all_to_all.37 = bf16[64,1,15360]{2,1,0:T(2,128)(2,1)} reshape(bf16[64,64,240]{2,1,0:T(8,128)(2,1)} %gather_fusion.1) | data formatting | bytes 3932160 | tf_op jit(solution)/shard_map/all_to_all | solution.py:81
  65.4 13.8 %reduce.7 = bf16[64,15360]{1,0:T(8,128)(2,1)} reduce(bf16[64,1,15360]{2,1,0:T(2,128)(2,1)} %all_to_all.37, bf16[]{:T(256)} %broadcast.387), dimensions={1}, to_apply=%all_to_all.37.reduce_sub_computation | reduce | bytes 3932162 | tf_op jit(solution)/shard_map/all_to_all | solution.py:81
  79.2 5.6 reshape.296
  84.8 11.0 %all-to-all-start.1 = ((bf16[64,2,7680]{2,1,0:T(2,128)(2,1)}), bf16[64,2,7680]{2,1,0:T(2,128)(2,1)}, u32[]{:S(2)}, u32[]{:S(2)}) async-start(bf16[64,2,7680]{2,1,0:T(2,128)(2,1)} %reshape.296), calls=%async_computation.1 | async-start | bytes 3932160 | tf_op jit(solution)/shard_map/all_to_all | solution.py:81
  95.8 1.2 convert_reduce_fusion.2
  97.1 0.1 iota_compare_fusion
  97.2 4.1 reshape.301
  101.3 4.8 convert_reduce_fusion.1
  106.0 3.2 reshape.249
  109.2 34.8 %all-to-all-done.1 = bf16[64,2,7680]{2,1,0:T(2,128)(2,1)} async-done(((bf16[64,2,7680]{2,1,0:T(2,128)(2,1)}), bf16[64,2,7680]{2,1,0:T(2,128)(2,1)}, u32[]{:S(2)}, u32[]{:S(2)}) %all-to-all-start.1) | async-done | bytes 1966112 | tf_op jit(solution)/shard_map/all_to_all | solution.py:81
  144.0 10.2 %reshape.297 = bf16[64,1,15360]{2,1,0:T(2,128)(2,1)} reshape(bf16[64,2,7680]{2,1,0:T(2,128)(2,1)} %all-to-all-done.1) | data formatting | bytes 3932160
  154.2 13.1 %reduce.1 = bf16[64,15360]{1,0:T(8,128)(2,1)} reduce(bf16[64,1,15360]{2,1,0:T(2,128)(2,1)} %reshape.297, bf16[]{:T(256)} %constant.123), dimensions={1}, to_apply=%all_to_all.30.reduce_sub_computation | reduce | bytes 3932162 | tf_op jit(solution)/shard_map/all_to_all | solution.py:81
  167.3 6.9 %reshape.240 = bf16[64,64,240]{2,1,0:T(8,128)(2,1)} reshape(bf16[64,15360]{1,0:T(8,128)(2,1)} %reduce.1) | data formatting | bytes 3932160 | tf_op jit(solution)/shard_map/reshape | solution.py:85
  174.2 2.5 fusion.54
  176.7 0.5 fusion.15
  177.2 1.8 copy-done.4
  179.0 2.5 select_convert_fusion
  181.6 3.0 fusion.9
  184.6 3.6 fusion.4
  188.2 4.6 all_to_all.38
  192.8 5.4 reduce.8
  198.3 3.1 reshape.298
  201.4 5.8 all-to-all-start.2
  207.2 3.2 convert_reduce_fusion
  210.4 4.7 convolution_convert_fusion.1
  215.1 2.6 convolution_convert_fusion.2
  217.7 2.5 pad_add_fusion
  220.2 11.3 %all_to_all.40 = bf16[64,1,15360]{2,1,0:T(2,128)(2,1)} reshape(bf16[64,64,240]{2,1,0:T(8,128)(2,1)} %pad_add_fusion) | data formatting | bytes 3932160 | tf_op jit(solution)/shard_map/all_to_all | solution.py:102
  231.5 13.8 %reduce.10 = bf16[64,15360]{1,0:T(8,128)(2,1)} reduce(bf16[64,1,15360]{2,1,0:T(2,128)(2,1)} %all_to_all.40, bf16[]{:T(256)} %broadcast.387), dimensions={1}, to_apply=%all_to_all.40.reduce_sub_computation | reduce | bytes 3932162 | tf_op jit(solution)/shard_map/all_to_all | solution.py:102
  245.3 5.7 reshape.302
  251.0 10.5 %all-to-all-start.4 = ((bf16[64,2,7680]{2,1,0:T(2,128)(2,1)}), bf16[64,2,7680]{2,1,0:T(2,128)(2,1)}, u32[]{:S(2)}, u32[]{:S(2)}) async-start(bf16[64,2,7680]{2,1,0:T(2,128)(2,1)} %reshape.302), calls=%async_computation.4 | async-start | bytes 3932160 | tf_op jit(solution)/shard_map/all_to_all | solution.py:102
  261.5 4.3 reshape.299
  265.9 4.8 reduce.2
  270.6 2.3 reshape.278
  273.0 2.8 scatter_fusion
  275.8 0.2 copy.34
  276.0 0.2 reshape.243
  276.2 2.3 fusion.34
  278.6 1.3 dynamic-slice
  280.5 1.2 fusion
  281.7 219.5 %all-reduce.6.cloned.1.call-done = f32[640,1280]{1,0:T(8,128)} async-done(((f32[640,1280]{1,0:T(8,128)}), f32[640,1280]{1,0:T(8,128)}) %all-reduce.6.cloned.1.call-update) | async-done | bytes 3276816
  501.2 0.9 constant_dynamic-slice_fusion
  502.1 45.5 %psum.7 = f32[10,1280]{1,0:T(8,128)S(1)} all-reduce(f32[10,1280]{1,0:T(8,128)S(1)} %constant_dynamic-slice_fusion), channel_id=1, replica_groups=mesh['row'=64,'col'=12] {'col'}, use_global_device_ids=true, to_apply=%region_8.9 | all-reduce | flops 12800 | bytes 102400 | tf_op jit(solution)/shard_map/psum | solution.py:125
  547.6 0.6 broadcast_multiply_fusion
  548.3 10.2 %reshape.303 = bf16[64,1,15360]{2,1,0:T(2,128)(2,1)} reshape(bf16[64,2,7680]{2,1,0:T(2,128)(2,1)} %all-to-all-done.4) | data formatting | bytes 3932160
  558.4 13.1 %reduce.4 = bf16[64,15360]{1,0:T(8,128)(2,1)} reduce(bf16[64,1,15360]{2,1,0:T(2,128)(2,1)} %reshape.303, bf16[]{:T(256)} %constant.123), dimensions={1}, to_apply=%all_to_all.36.reduce_sub_computation | reduce | bytes 3932162 | tf_op jit(solution)/shard_map/all_to_all | solution.py:102
  571.6 6.9 %reshape.286 = bf16[64,64,240]{2,1,0:T(8,128)(2,1)} reshape(bf16[64,15360]{1,0:T(8,128)(2,1)} %reduce.4) | data formatting | bytes 3932160 | tf_op jit(solution)/shard_map/reshape | solution.py:108
  578.5 6.7 %scatter_fusion.1 = bf16[16,64,240]{2,1,0:T(8,128)(2,1)S(1)} fusion(bf16[16,64,240]{2,1,0:T(8,128)(2,1)S(1)} %broadcast_in_dim.90, s32[64]{0:T(128)S(1)} %fusion.42, bf16[64,64,240]{2,1,0:T(8,128)(2,1)} %reshape.286), kind=kCustom, calls=%fused_computation.4 | custom fusion | bytes 5898496 | tf_op jit(solution)/shard_map/scatter | solution.py:108
  585.2 0.3 copy.39
  585.5 1.3 broadcast_in_dim_reshape.3
  (40 shorter events, 0.3 us)
Async XLA Ops:
  7.2 15.9 %copy-start = (bf16[640,1280]{1,0:T(8,128)(2,1)S(1)}, bf16[640,1280]{1,0:T(8,128)(2,1)}, u32[]{:S(2)}) copy-start(bf16[640,1280]{1,0:T(8,128)(2,1)} %param.6) | copy-start | bytes 4915204
  9.5 30.8 %all-to-all-start = ((bf16[64,1,1]{2,1,0:T(2,128)(2,1)}), bf16[64,1,1]{2,1,0:T(2,128)(2,1)S(1)}, u32[]{:S(2)}, u32[]{:S(2)}) async-start(bf16[64,1,1]{2,1,0:T(2,128)(2,1)} %copy.29), calls=%async_computation | async-start | bytes 65536 | tf_op jit(solution)/shard_map/all_to_all | solution.py:82
  37.3 13.8 %copy-start.11 = (bf16[1,128,1920]{2,1,0:T(8,128)(2,1)S(1)}, bf16[1,128,1920]{2,1,0:T(8,128)(2,1)}, u32[]{:S(2)}) copy-start(bf16[1,128,1920]{2,1,0:T(8,128)(2,1)} %param.4) | copy-start | bytes 1474564
  40.3 44.5 %all-to-all-start.3 = ((bf16[64,2,2560]{2,1,0:T(2,128)(2,1)}), bf16[64,2,2560]{2,1,0:T(2,128)(2,1)S(1)}, u32[]{:S(2)}, u32[]{:S(2)}) async-start(bf16[64,2,2560]{2,1,0:T(2,128)(2,1)} %reshape.300), calls=%async_computation.3 | async-start | bytes 1310720 | tf_op jit(solution)/shard_map/all_to_all | solution.py:92
  84.8 12.3 %copy-start.8 = (bf16[64,2,2560]{2,1,0:T(2,128)(2,1)}, bf16[64,2,2560]{2,1,0:T(2,128)(2,1)S(1)}, u32[]{:S(2)}) copy-start(bf16[64,2,2560]{2,1,0:T(2,128)(2,1)S(1)} %all-to-all-done.3) | copy-start | bytes 1966084
  84.8 59.2 %all-to-all-start.1 = ((bf16[64,2,7680]{2,1,0:T(2,128)(2,1)}), bf16[64,2,7680]{2,1,0:T(2,128)(2,1)}, u32[]{:S(2)}, u32[]{:S(2)}) async-start(bf16[64,2,7680]{2,1,0:T(2,128)(2,1)} %reshape.296), calls=%async_computation.1 | async-start | bytes 3932160 | tf_op jit(solution)/shard_map/all_to_all | solution.py:81
  176.7 7.9 %copy-start.1 = (f32[64,64,64]{1,2,0:T(8,128)}, f32[64,64,64]{1,2,0:T(8,128)S(1)}, u32[]{:S(2)}) copy-start(f32[64,64,64]{1,2,0:T(8,128)S(1)} %get-tuple-element.7) | copy-start | bytes 3145732
  176.7 2.3 copy-start.4
  179.0 2.5 copy-start.3
  198.3 8.9 %copy-start.6 = (bf16[64,64,64]{1,2,0:T(8,128)(2,1)S(1)}, bf16[64,64,64]{1,2,0:T(8,128)(2,1)}, u32[]{:S(2)}) copy-start(bf16[64,64,64]{1,2,0:T(8,128)(2,1)} %get-tuple-element.9) | copy-start | bytes 1572868
  201.4 49.6 %all-to-all-start.2 = ((bf16[64,2,2560]{2,1,0:T(2,128)(2,1)}), bf16[64,2,2560]{2,1,0:T(2,128)(2,1)S(1)}, u32[]{:S(2)}, u32[]{:S(2)}) async-start(bf16[64,2,2560]{2,1,0:T(2,128)(2,1)} %reshape.298), calls=%async_computation.2 | async-start | bytes 1310720 | tf_op jit(solution)/shard_map/all_to_all | solution.py:89
  207.1 3.2 copy-start.2
  210.4 4.7 copy-start.5
  215.1 2.6 copy-start.10
  251.0 10.5 %copy-start.7 = (bf16[64,2,2560]{2,1,0:T(2,128)(2,1)}, bf16[64,2,2560]{2,1,0:T(2,128)(2,1)S(1)}, u32[]{:S(2)}) copy-start(bf16[64,2,2560]{2,1,0:T(2,128)(2,1)S(1)} %all-to-all-done.2) | copy-start | bytes 1966084
  251.0 297.3 %all-to-all-start.4 = ((bf16[64,2,7680]{2,1,0:T(2,128)(2,1)}), bf16[64,2,7680]{2,1,0:T(2,128)(2,1)}, u32[]{:S(2)}, u32[]{:S(2)}) async-start(bf16[64,2,7680]{2,1,0:T(2,128)(2,1)} %reshape.302), calls=%async_computation.4 | async-start | bytes 3932160 | tf_op jit(solution)/shard_map/all_to_all | solution.py:102
  261.4 239.8 %all-reduce.6.cloned.1.call-start = ((), (), s32[]{:S(2)}) async-start(), calls=%async_computation.5 | async-start | bytes 6553600
  273.0 3.2 copy-start.9
Sparse Core Ops, SparseCore 0:
  278.7 222.4 all-reduce.5
where the time goes:
time: 604 us; the launch traced here: 594 us
  waiting for transfers between devices  254 us (42%)
  local copies, waits for them, and re-layouts  120 us (20%)
  other arithmetic  82.3 us (14%)
  starting transfers between devices  51.6 us (9%)
  blocking collectives  45.5 us (8%)
  matrix products  24.1 us (4%)
  between operations  16.4 us (3%)
    unnamed x2, waiting for transfers between devices  220 us
    unnamed x34, local copies, waits for them, and re-layouts  50.2 us
    psum x1, blocking collectives, body(): d_weight = lax.psum(row_share, 'col') * scale  45.5 us
    all_to_all x1, waiting for transfers between devices, body(): lax.all_to_all(send_units, 'row', split_axis=0, concat_axis=0, tiled=True)  34.8 us
    all_to_all x2, other arithmetic, body(): lax.all_to_all(grad_slots.reshape(slot_total, -1), 'row', split_axis=0, c...  26.9 us
    all_to_all x2, other arithmetic, body(): lax.all_to_all(send_units, 'row', split_axis=0, concat_axis=0, tiled=True)  26.9 us
    all_to_all x1, starting transfers between devices, body(): lax.all_to_all(send_live, 'row', split_axis=0, concat_axis=0, tiled=True)  13.6 us
  transfers between devices with their start and end apart: 6, of which 2 were waited for; matrix products, arithmetic and copies ran while one was open for 17% of the time, Pallas kernels for 0%

commit v1 on v0

v1 whole, which is shorter than its diff:
```python
import jax
import jax.numpy as jnp
from jax import lax
from jax.sharding import PartitionSpec as P

HD = 80
H = 8
WIN = 64
HIGHEST = lax.Precision.HIGHEST


def attend(qkv_rows, live):
    token_count = qkv_rows.shape[0]
    window_count = token_count // WIN
    blocks = qkv_rows.reshape(window_count, WIN, H, 3, HD).astype(jnp.float32)
    query = blocks[:, :, :, 0, :]
    key = blocks[:, :, :, 1, :]
    value = blocks[:, :, :, 2, :]
    slots = jnp.arange(token_count, dtype=jnp.int32).reshape(window_count, WIN)
    alive = slots < live
    logits = jnp.einsum("wphc,wqhc->whpq", query, key, precision=HIGHEST) * HD ** (-0.5)
    logits = jnp.where(alive[:, None, None, :], logits, -1e30)
    peak = lax.optimization_barrier(jnp.max(logits, axis=-1, keepdims=True))
    weights = jnp.exp(logits - peak)
    total = lax.optimization_barrier(jnp.sum(weights, axis=-1, keepdims=True))
    probs = (weights / total).astype(jnp.bfloat16)
    attended = jnp.einsum(
        "whpq,wqhc->wphc", probs.astype(jnp.float32), value, precision=HIGHEST
    )
    attended = jnp.where(alive[:, :, None, None], attended, 0.0)
    return attended.astype(jnp.bfloat16).reshape(token_count, H * HD)


def body(qkv, cotangent, out_weight, live_patches):
    token_count = qkv.shape[1]
    live = live_patches[0, 0]
    grad_rows = cotangent[0]
    attended, pullback = jax.vjp(lambda rows: attend(rows, live), qkv[0])
    grad_attended = lax.dot_general(
        grad_rows, out_weight, (((1,), (1,)), ((), ())), preferred_element_type=jnp.float32
    ).astype(jnp.bfloat16)
    (d_qkv,) = pullback(grad_attended)
    output = jnp.dot(attended, out_weight, preferred_element_type=jnp.float32).astype(
        jnp.bfloat16
    )
    row_share = lax.psum_scatter(
        lax.dot_general(
            attended, grad_rows, (((0,), (0,)), ((), ())), preferred_element_type=jnp.float32
        ),
        "row",
        scatter_dimension=0,
        tiled=True,
    )
    scale = (lax.axis_size("col") * lax.axis_size("row") * token_count) ** (-0.5)
    d_weight = lax.psum(row_share, "col") * scale
    return (output[None], d_qkv[None], d_weight)


def solution(mesh):
    in_specs = (P("col", "row", None), P("col", "row", None), P(), P("col", "row"))
    out_specs = (P("col", "row", None), P("col", "row", None), P("row", None))
    return jax.shard_map(body, mesh=mesh, in_specs=in_specs, out_specs=out_specs, check_vma=False)
```

time: 604 us -> 292 us (0.48); the launches traced: 594 us -> 292 us
  local copies, waits for them, and re-layouts: 120 us -> 10.8 us
  other arithmetic: 82.3 us -> 1.17 us
  starting transfers between devices: 51.6 us -> 0.04 us
  waiting for transfers between devices: 254 us -> 211 us
  matrix products: 24.1 us -> 8.49 us
    all_to_all x7 -> x0, other arithmetic: 69.3 us -> none  [the longest x2 26.9 us: body(): lax.all_to_all(grad_slots.reshape(slot_total, -1), 'row', split_axis=0, c...]
    all_to_all x5 -> x0, starting transfers between devices: 51.5 us -> none  [the longest x1 13.6 us: body(): lax.all_to_all(send_live, 'row', split_axis=0, concat_axis=0, tiled=True)]
    unnamed x34 -> x22, local copies, waits for them, and re-layouts: 50.2 us -> 6.08 us
    all_to_all x5 -> x0, waiting for transfers between devices: 34.8 us -> none  [the longest x1 34.8 us: body(): lax.all_to_all(send_units, 'row', split_axis=0, concat_axis=0, tiled=True)]
    all_to_all x5 -> x0, local copies, waits for them, and re-layouts: 32.3 us -> none  [the longest x2 11.8 us: body(): lax.all_to_all(send_units, 'row', split_axis=0, concat_axis=0, tiled=True)]
    reshape x6 -> x1, local copies, waits for them, and re-layouts: 16.6 us -> 0.2 us  [attend(): return attended.astype(jnp.bfloat16).reshape(token_count, H * HD)]
    dot_general x9, matrix products: 24.1 us -> 8.49 us  [the longest x3 2.78 us: attend(): jnp.einsum('whpq,wqhc->wphc', probs.astype(jnp.float32), value, precision...]
    scatter x2 -> x0, local copies, waits for them, and re-layouts: 9.5 us -> none  [the longest x1 6.7 us: body(): d_units = jnp.zeros((unit_count, WIN, 3 * HD), jnp.bfloat16).at[target_ho...]
  transfers between devices with their start and end apart: 6 -> 1, of which waited for: 2 -> 1; matrix products, arithmetic and copies ran while one was open for 17% -> 3% of each run, Pallas kernels for 0% -> 0%
where the time goes in v1:
time: 292 us
  waiting for transfers between devices  211 us (72%)
  blocking collectives  45.2 us (15%)
  between operations  15.7 us (5%)
  local copies, waits for them, and re-layouts  10.8 us (4%)
  matrix products  8.49 us (3%)
    unnamed x2, waiting for transfers between devices  211 us
    psum x1, blocking collectives, body(): d_weight = lax.psum(row_share, 'col') * scale  45.2 us
    unnamed x22, local copies, waits for them, and re-layouts  6.08 us
  transfers between devices with their start and end apart: 1, of which 1 were waited for; matrix products, arithmetic and copies ran while one was open for 3% of the time, Pallas kernels for 0%

profile of v1, /device:TPU:2, one launch (start us, length us, event | category | flops | bytes accessed | tf_op | source)
XLA Modules:
  0.0 292.0 jit_solution(5829108580958924139)
XLA Ops:
  7.2 0.0 copy-start
  7.2 0.0 all-reduce.6.cloned.1.call-start
  8.0 3.0 %reshape.71 = bf16[2,64,8,3,80]{4,3,2,1,0:T(4,128)(2,1)S(1)} reshape(bf16[1,128,1920]{2,1,0:T(8,128)(2,1)} %param.4) | data formatting | bytes 983040 | tf_op jit(solution)/shard_map/jvp()/reshape;squeeze | solution.py:15
  11.0 1.1 fusion.31
  12.1 0.0 copy-start.2
  12.1 0.0 copy-start.4
  12.1 0.0 copy-start.8
  12.1 0.3 fusion.32
  12.4 0.1 fusion.8
  12.5 0.0 copy-start.1
  12.5 0.3 fusion.4
  12.8 0.0 copy-done.2
  12.9 0.2 copy-done.4
  13.1 0.1 copy-done.8
  13.2 0.2 copy.25
  13.4 0.2 reshape.66
  13.6 0.0 copy-done.1
  13.6 2.3 fusion.9
  16.0 0.0 all-reduce.6.cloned.1.call-update
  16.0 0.0 copy-done
  16.0 0.6 fusion.5
  16.7 0.2 reshape.68
  16.9 0.0 copy-start.6
  16.9 0.8 copy-done.6
  17.7 0.0 copy-start.5
  17.7 2.0 convert_reduce_fusion
  19.7 0.0 copy-start.3
  19.7 0.2 fusion.30
  19.9 0.0 copy-start.7
  20.0 0.0 copy-done.5
  20.0 0.5 convolution_bitcast_fusion.1
  20.5 0.2 copy-done.3
  20.7 0.7 convolution_bitcast_fusion
  21.5 0.0 copy-done.7
  21.5 0.5 convolution_bitcast_fusion.2
  22.0 0.2 add_convert_fusion
  22.2 0.7 copy.32
  22.9 1.8 reshape.69
  24.7 1.3 dynamic-slice
  26.6 1.2 fusion
  27.8 210.6 %all-reduce.6.cloned.1.call-done = f32[640,1280]{1,0:T(8,128)} async-done(((f32[640,1280]{1,0:T(8,128)}), f32[640,1280]{1,0:T(8,128)}) %all-reduce.6.cloned.1.call-update) | async-done | bytes 3276816
  238.4 0.9 constant_dynamic-slice_fusion
  239.3 45.2 %psum.7 = f32[10,1280]{1,0:T(8,128)S(1)} all-reduce(f32[10,1280]{1,0:T(8,128)S(1)} %constant_dynamic-slice_fusion), channel_id=1, replica_groups=mesh['row'=64,'col'=12] {'col'}, use_global_device_ids=true, to_apply=%region_6.7 | all-reduce | flops 12800 | bytes 102400 | tf_op jit(solution)/shard_map/psum | solution.py:55
  284.5 0.6 broadcast_multiply_fusion
  (5 shorter events, 0.0 us)
Async XLA Ops:
  7.2 8.8 %copy-start = (bf16[640,1280]{1,0:T(8,128)(2,1)S(1)}, bf16[640,1280]{1,0:T(8,128)(2,1)}, u32[]{:S(2)}) copy-start(bf16[640,1280]{1,0:T(8,128)(2,1)} %param.6) | copy-start | bytes 4915204
  7.2 231.2 %all-reduce.6.cloned.1.call-start = ((), (), s32[]{:S(2)}) async-start(), calls=%async_computation | async-start | bytes 6553600
  12.1 0.8 copy-start.2
  12.1 1.0 copy-start.4
  12.1 1.1 copy-start.8
  12.5 1.1 copy-start.1
  16.9 0.8 copy-start.6
  17.7 2.2 copy-start.5
  19.7 1.0 copy-start.3
  19.9 1.5 copy-start.7
Sparse Core Ops, SparseCore 0:
  16.1 222.2 all-reduce.5

commit v2 on v1

--- a/solution.py
+++ b/solution.py
@@ -31,11 +31,51 @@
     return attended.astype(jnp.bfloat16).reshape(token_count, H * HD)
 
 
+def bit_orders(steps):
+    low = list(range(1, steps))
+    split = min(2, steps - 1)
+    return [0] + low, [0] + low[split:] + low[:split]
+
+
+def reduce_rows(columns, grad_rows):
+    rank_total = lax.axis_size("row")
+    steps = rank_total.bit_length() - 1
+    rank = lax.axis_index("row")
+    odd = (rank & 1) == 1
+    orders = bit_orders(steps)
+    token_count, width = columns.shape
+    share = width // rank_total
+
+    shaped = columns.reshape((token_count,) + (2,) * steps + (share,))
+    halves = []
+    for parity, order in enumerate(orders):
+        half = lax.index_in_dim(shaped, parity, steps, keepdims=False)
+        axes = [1 + (steps - 1 - bit) for bit in order[1:]]
+        halves.append(half.transpose([0] + axes + [steps]))
+    arranged = jnp.stack(halves, axis=1).reshape(token_count, width)
+    current = lax.dot_general(
+        arranged, grad_rows, (((0,), (0,)), ((), ())), preferred_element_type=jnp.float32
+    )
+    current = current.reshape((2,) * steps + (share * grad_rows.shape[1],))
+    for step in range(steps):
+        even_bit, odd_bit = orders[0][step], orders[1][step]
+        bit = jnp.where(odd, odd_bit, even_bit)
+        mine = (rank >> bit) & 1
+        keep = lax.dynamic_index_in_dim(current, mine, 0, keepdims=False)
+        send = lax.dynamic_index_in_dim(current, 1 - mine, 0, keepdims=False)
+        pairs = [
+            (i, i ^ (1 << (odd_bit if i & 1 else even_bit))) for i in range(rank_total)
+        ]
+        current = keep + lax.ppermute(send, "row", pairs)
+    return current.reshape(share, grad_rows.shape[1])
+
+
 def body(qkv, cotangent, out_weight, live_patches):
     token_count = qkv.shape[1]
     live = live_patches[0, 0]
     grad_rows = cotangent[0]
     attended, pullback = jax.vjp(lambda rows: attend(rows, live), qkv[0])
+    row_share = reduce_rows(attended, grad_rows)
     grad_attended = lax.dot_general(
         grad_rows, out_weight, (((1,), (1,)), ((), ())), preferred_element_type=jnp.float32
     ).astype(jnp.bfloat16)
@@ -43,16 +83,8 @@
     output = jnp.dot(attended, out_weight, preferred_element_type=jnp.float32).astype(
         jnp.bfloat16
     )
-    row_share = lax.psum_scatter(
-        lax.dot_general(
-            attended, grad_rows, (((0,), (0,)), ((), ())), preferred_element_type=jnp.float32
-        ),
-        "row",
-        scatter_dimension=0,
-        tiled=True,
-    )
     scale = (lax.axis_size("col") * lax.axis_size("row") * token_count) ** (-0.5)
-    d_weight = lax.psum(row_share, "col") * scale
+    d_weight = lax.all_gather(row_share, "col", axis=0, tiled=False).sum(0) * scale
     return (output[None], d_qkv[None], d_weight)
 
 

time: 292 us -> 125 us (0.43)
  the two profiles are of different devices: /device:TPU:2 before, /device:TPU:56 now
where the time goes in v2:
time: 125 us
  blocking collectives  38.4 us (31%)
  starting transfers between devices  24.9 us (20%)
  local copies, waits for them, and re-layouts  20.4 us (16%)
  waiting for transfers between devices  17.8 us (14%)
  matrix products  11.6 us (9%)
  other arithmetic  9.8 us (8%)
  between operations  1.97 us (2%)
    all_gather x1, blocking collectives, body(): lax.all_gather(row_share, 'col', axis=0, tiled=False).sum(0) * scale  38.4 us
    ppermute x6, starting transfers between devices, reduce_rows(): current = keep + lax.ppermute(send, 'row', pairs)  24.9 us
    ppermute x6, waiting for transfers between devices, reduce_rows(): current = keep + lax.ppermute(send, 'row', pairs)  17.8 us
    add x6, other arithmetic, reduce_rows(): current = keep + lax.ppermute(send, 'row', pairs)  5.66 us
    reshape x1, local copies, waits for them, and re-layouts, reduce_rows(): current = current.reshape((2,) * steps + (share * grad_rows.shape[1],))  5.19 us
    dot_general x3, matrix products, attend(): jnp.einsum('whpq,wqhc->wphc', probs.astype(jnp.float32), value, precision...  4.26 us
    unnamed x44, local copies, waits for them, and re-layouts  3.38 us
    convert_element_type x3, local copies, waits for them, and re-layouts, attend(): return attended.astype(jnp.bfloat16).reshape(token_count, H * HD)  3.16 us
  transfers between devices with their start and end apart: 6, of which 5 were waited for; matrix products, arithmetic and copies ran while one was open for 15% of the time, Pallas kernels for 0%

profile of v2, /device:TPU:56, one launch (start us, length us, event | category | flops | bytes accessed | tf_op | source)
XLA Modules:
  0.0 124.8 jit_solution(14477577870048857683)
XLA Ops:
  0.6 0.0 copy-start
  1.4 0.0 copy-start.18
  1.4 3.0 %reshape.82 = bf16[2,64,8,3,80]{4,3,2,1,0:T(4,128)(2,1)S(1)} reshape(bf16[1,128,1920]{2,1,0:T(8,128)(2,1)} %param.4) | data formatting | bytes 983040 | tf_op jit(solution)/shard_map/jvp()/reshape;squeeze | solution.py:15
  4.4 1.1 fusion.31
  5.6 0.3 fusion.32
  5.9 0.1 fusion.8
  6.0 0.0 copy-done.18
  6.0 0.3 copy-done.8
  6.3 0.2 copy-done.10
  6.5 0.4 copy-done.2
  6.9 0.3 fusion.4
  7.2 0.0 copy-start.7
  7.2 0.3 copy.34
  7.5 0.2 reshape.77
  7.6 0.1 slice_bitcast_fusion.1
  7.8 0.1 copy.75
  7.8 0.2 pad_maximum_fusion
  8.1 0.1 copy.37
  8.1 0.1 reshape.78
  8.2 2.3 %fusion.9 = f32[640,1280]{1,0:T(8,128)} fusion(bf16[128,640]{0,1:T(8,128)(2,1)S(1)} %reshape.78, bf16[1,128,1280]{2,1,0:T(8,128)(2,1)S(1)} %copy-done.7), kind=kOutput, calls=%fused_computation.31 | convolution fusion | flops 209715200 | bytes 3768320 | tf_op jit(solution)/shard_map/dot_general | solution.py:56
  10.5 5.2 %reshape.79 = f32[2,2,2,2,2,2,12800]{6,5,4,3,2,1,0:T(2,128)} reshape(f32[640,1280]{1,0:T(8,128)} %fusion.9) | data formatting | bytes 6553600 | tf_op jit(solution)/shard_map/reshape | solution.py:59
  15.7 1.6 %dynamic-slice_bitcast_fusion = f32[2,2,2,2,2,12800]{5,4,3,2,1,0:T(2,128)S(1)} fusion(f32[2,2,2,2,2,2,12800]{6,5,4,3,2,1,0:T(2,128)} %reshape.79, s32[]{:T(128)S(6)} %select_n.81), kind=kLoop, calls=%fused_computation.3 | loop fusion | bytes 3276804 | tf_op jit(solution)/shard_map/jit(dynamic_index_in_dim)/squeeze | solution.py:65
  17.3 1.9 %collective-permute-start = (f32[2,2,2,2,2,12800]{5,4,3,2,1,0:T(2,128)S(1)}, f32[2,2,2,2,2,12800]{5,4,3,2,1,0:T(2,128)}, u32[]{:S(2)}, u32[]{:S(2)}) collective-permute-start(f32[2,2,2,2,2,12800]{5,4,3,2,1,0:T(2,128)S(1)} %dynamic-slice_bitcast_fusion), channel_id=1, source_target_pairs={{0,12},{12,0},{24,36},{36,24},{48,60},{60,48},{72,84},{84,72},{96,... | collective-permute-start | bytes 4915208 | tf_op jit(solution)/shard_map/ppermute | solution.py:69
  19.2 2.3 %fusion.5 = f32[128,640]{1,0:T(8,128)} fusion(bf16[640,1280]{1,0:T(8,128)(2,1)S(1)} %copy-done, bf16[1,128,1280]{2,1,0:T(8,128)(2,1)} %param.5), kind=kOutput, calls=%fused_computation.16 | convolution fusion | flops 209879040 | bytes 2293760 | tf_op jit(solution)/shard_map/dot_general | solution.py:79
  21.5 2.0 %reshape.80 = f32[2,64,8,80]{3,2,1,0:T(8,128)} reshape(f32[128,640]{1,0:T(8,128)} %fusion.5) | data formatting | bytes 655360 | tf_op jit(solution)/shard_map/transpose(jvp())/convert_element_type | solution.py:31
  23.6 0.0 collective-permute-done
  23.6 2.8 %bitcast_add_fusion = f32[2,2,2,2,2,12800]{5,4,3,2,1,0:T(2,128)S(1)} fusion(f32[2,2,2,2,2,12800]{5,4,3,2,1,0:T(2,128)} %collective-permute-done, f32[2,2,2,2,2,2,12800]{6,5,4,3,2,1,0:T(2,128)} %reshape.79, s32[]{:T(128)S(6)} %select_n.80), kind=kLoop, calls=%fused_computation.2 | loop fusion | flops 409600 | bytes 4915204 | tf_op jit(solution)/shard_map/add | solution.py:69
  26.3 0.0 copy-start.3
  26.4 0.0 copy-start.12
  26.4 0.0 copy-start.14
  26.4 1.0 dynamic-slice_bitcast_fusion.1
  27.3 3.4 %collective-permute-start.1 = (f32[2,2,2,2,12800]{4,3,2,1,0:T(2,128)}, f32[2,2,2,2,12800]{4,3,2,1,0:T(2,128)}, u32[]{:S(2)}, u32[]{:S(2)}) collective-permute-start(f32[2,2,2,2,12800]{4,3,2,1,0:T(2,128)} %dynamic-slice_bitcast_fusion.1), channel_id=1, source_target_pairs={{0,24},{12,108},{24,0},{36,132},{48,72},{60,156},{72,48},{84,180},... | collective-permute-start | bytes 2457608 | tf_op jit(solution)/shard_map/ppermute | solution.py:69
  30.8 2.3 %convert_reduce_fusion = (f32[2,8,64]{2,1,0:T(8,128)}, pred[2,8,64,64]{2,3,1,0:T(32,128)(4,1)}, f32[2,8,64]{2,1,0:T(8,128)}, f32[2,8,64,64]{2,3,1,0:T(8,128)}) fusion(f32[2,8,64,64]{2,3,1,0:T(8,128)S(1)} %copy-done.3, f32[2,8,64]{2,1,0:T(8,128)S(1)} %get-tuple-element.21, f32[2,8,64]{2,1,0:T(8,128)S(1)} %get-tuple-element.21, ...), kind=kOutput, calls=%fused_computation.23 | convolution fusion | flops 63584256 | bytes 1101952 | tf_op jit(solution)/shard_map/transpose(jvp(whpq,wqhc->wphc))/dot_general | solution.py:27
  33.1 0.9 copy.30
  34.0 1.2 reshape.75
  35.2 0.7 negate_bitcast_fusion.1
  35.9 2.2 %fusion.30 = (f32[2,8,64]{2,1,0:T(8,128)S(1)}, f32[2,8,64,64]{2,3,1,0:T(8,128)}) fusion(f32[2,8,64,64]{2,3,1,0:T(8,128)} %copy-done.2, f32[2,8,64]{2,1,0:T(8,128)S(1)} %get-tuple-element.21, f32[2,8,64]{2,1,0:T(8,128)S(1)} %bitcast.106, f32[2,8,64,64]{2,3,1,0:T(8,128)} %get-tuple-element.23, f32[2,8,64]{2,1,0:T(8,128)S(1)} %fusion.8), kind=kLoop, calls=%fused_computation.72 | loop fusion | flops 326656 | bytes 802816 | tf_op jit(solution)/shard_map/transpose(jvp())/reduce_sum | solution.py:24
  38.1 3.8 %collective-permute-done.1 = f32[2,2,2,2,12800]{4,3,2,1,0:T(2,128)} collective-permute-done((f32[2,2,2,2,12800]{4,3,2,1,0:T(2,128)}, f32[2,2,2,2,12800]{4,3,2,1,0:T(2,128)}, u32[]{:S(2)}, u32[]{:S(2)}) %collective-permute-start.1) | collective-permute-done | bytes 819232 | tf_op jit(solution)/shard_map/ppermute | solution.py:69
  41.9 1.6 %bitcast_add_fusion.1 = f32[2,2,2,2,12800]{4,3,2,1,0:T(2,128)S(1)} fusion(f32[2,2,2,2,12800]{4,3,2,1,0:T(2,128)} %collective-permute-done.1, f32[2,2,2,2,2,12800]{5,4,3,2,1,0:T(2,128)S(1)} %bitcast_add_fusion, s32[]{:T(128)S(6)} %select_n.83), kind=kLoop, calls=%fused_computation.17 | loop fusion | flops 204800 | bytes 2457604 | tf_op jit(solution)/shard_map/add | solution.py:69
  43.5 0.0 copy-start.17
  43.6 5.1 %collective-permute-start.2 = (f32[2,2,2,12800]{3,2,1,0:T(2,128)S(1)}, f32[2,2,2,12800]{3,2,1,0:T(2,128)S(1)}, u32[]{:S(2)}, u32[]{:S(2)}) collective-permute-start(f32[2,2,2,12800]{3,2,1,0:T(2,128)S(1)} %dynamic-slice_bitcast_fusion.2), channel_id=1, source_target_pairs={{0,48},{12,204},{24,72},{36,228},{48,0},{60,252},{72,24},{84,276},... | collective-permute-start | bytes 1228808 | tf_op jit(solution)/shard_map/ppermute | solution.py:69
  48.6 1.2 fusion
  49.8 5.2 %collective-permute-done.2 = f32[2,2,2,12800]{3,2,1,0:T(2,128)S(1)} collective-permute-done((f32[2,2,2,12800]{3,2,1,0:T(2,128)S(1)}, f32[2,2,2,12800]{3,2,1,0:T(2,128)S(1)}, u32[]{:S(2)}, u32[]{:S(2)}) %collective-permute-start.2) | collective-permute-done | bytes 409632 | tf_op jit(solution)/shard_map/ppermute | solution.py:69
  55.0 0.2 bitcast_add_fusion.2
  55.3 0.0 copy-start.5
  55.3 3.3 %collective-permute-start.3 = (f32[2,2,12800]{2,1,0:T(2,128)S(1)}, f32[2,2,12800]{2,1,0:T(2,128)}, u32[]{:S(2)}, u32[]{:S(2)}) collective-permute-start(f32[2,2,12800]{2,1,0:T(2,128)S(1)} %dynamic-slice_bitcast_fusion.3), channel_id=1, source_target_pairs={{0,96},{12,396},{24,120},{36,420},{48,144},{60,444},{72,168},{84,4... | collective-permute-start | bytes 614408 | tf_op jit(solution)/shard_map/ppermute | solution.py:69
  58.6 0.7 convolution_bitcast_fusion
  59.4 0.0 copy-start.6
  59.4 1.7 %convolution_bitcast_fusion.2 = f32[2,64,8,1,80]{4,1,2,0,3:T(8,128)S(1)} fusion(f32[2,64,8,80]{3,2,1,0:T(8,128)} %reshape.80, pred[2,64]{1,0:T(4,128)(4,1)S(1)} %copy-done.20, f32[2,8,64,64]{2,3,1,0:T(8,128)S(1)} %copy-done.4, f32[2,8,64]{2,1,0:T(8,128)S(1)} %fusion.8, f32[2,8,64]{2,1,0:T(8,128)S(1)} %get-tuple-element.21), kind=kOutput, calls=%fused_computation.7 | convolution fusion | flops 63193088 | bytes 925824 | tf_op jit(solution)/shard_map/transpose(jvp(whpq,wqhc->wphc))/dot_general | solution.py:27
  61.1 2.0 %collective-permute-done.3 = f32[2,2,12800]{2,1,0:T(2,128)} collective-permute-done((f32[2,2,12800]{2,1,0:T(2,128)S(1)}, f32[2,2,12800]{2,1,0:T(2,128)}, u32[]{:S(2)}, u32[]{:S(2)}) %collective-permute-start.3) | collective-permute-done | bytes 204832 | tf_op jit(solution)/shard_map/ppermute | solution.py:69
  63.1 1.0 bitcast_add_fusion.3
  64.1 4.2 %collective-permute-start.4 = (f32[2,12800]{1,0:T(2,128)S(1)}, f32[2,12800]{1,0:T(2,128)S(1)}, u32[]{:S(2)}, u32[]{:S(2)}) collective-permute-start(f32[2,12800]{1,0:T(2,128)S(1)} %dynamic-slice_bitcast_fusion.4), channel_id=1, source_target_pairs={{0,192},{12,36},{24,216},{36,12},{48,240},{60,84},{72,264},{84,60}... | collective-permute-start | bytes 307208 | tf_op jit(solution)/shard_map/ppermute | solution.py:69
  68.4 0.5 convolution_bitcast_fusion.1
  68.9 6.4 %collective-permute-done.4 = f32[2,12800]{1,0:T(2,128)S(1)} collective-permute-done((f32[2,12800]{1,0:T(2,128)S(1)}, f32[2,12800]{1,0:T(2,128)S(1)}, u32[]{:S(2)}, u32[]{:S(2)}) %collective-permute-start.4) | collective-permute-done | bytes 102432 | tf_op jit(solution)/shard_map/ppermute | solution.py:69
  75.3 0.1 bitcast_add_fusion.4
  75.3 0.3 dynamic-slice_reduce_fusion
  75.6 7.0 %collective-permute-start.5 = (f32[12800]{0:T(1024)S(1)}, f32[12800]{0:T(1024)S(1)}, u32[]{:S(2)}, u32[]{:S(2)}) collective-permute-start(f32[12800]{0:T(1024)S(1)} %get-tuple-element.9), channel_id=1, source_target_pairs={{0,384},{12,60},{24,408},{36,84},{48,432},{60,12},{72,456},{84,36}... | collective-permute-start | bytes 153608 | tf_op jit(solution)/shard_map/ppermute | solution.py:69
  82.7 0.2 add_convert_fusion
  82.9 0.7 copy.41
  83.5 1.7 %reshape.81 = bf16[1,128,1920]{2,1,0:T(8,128)(2,1)} reshape(bf16[2,64,8,3,80]{4,3,2,1,0:T(4,128)(2,1)S(1)} %copy.41) | data formatting | bytes 983040
  85.3 0.4 collective-permute-done.5
  85.7 38.4 %all_gather.3 = f32[12,10,1280]{2,1,0:T(8,128)S(1)} all-gather(f32[1,10,1280]{2,1,0:T(8,128)S(1)} %all_gather_reshape.3), channel_id=1, replica_groups=mesh['row'=64,'col'=12] {'col'}, dimensions={0}, use_global_device_ids=true | all-gather | bytes 665600 | tf_op jit(solution)/shard_map/all_gather | solution.py:87
  124.1 0.1 reduce_sum.63
  124.1 0.6 broadcast_multiply_fusion
  (38 shorter events, 0.2 us)
Async XLA Ops:
  0.6 18.6 %copy-start = (bf16[640,1280]{1,0:T(8,128)(2,1)S(1)}, bf16[640,1280]{1,0:T(8,128)(2,1)}, u32[]{:S(2)}) copy-start(bf16[640,1280]{1,0:T(8,128)(2,1)} %param.6) | copy-start | bytes 4915204
  1.4 4.6 %copy-start.18 = (pred[2,64]{1,0:T(4,128)(4,1)}, pred[2,64]{1,0:T(4,128)(4,1)S(1)}, u32[]{:S(2)}) copy-start(pred[2,64]{1,0:T(4,128)(4,1)S(1)} %add_compare_fusion) | copy-start | bytes 388
  5.5 0.8 copy-start.8
  5.5 1.0 copy-start.10
  5.5 5.0 %copy-start.13 = (bf16[2,64,8,1,80]{4,3,2,1,0:T(2,128)(2,1)}, bf16[2,64,8,1,80]{4,3,2,1,0:T(2,128)(2,1)S(1)}, u32[]{:S(2)}) copy-start(bf16[2,64,8,1,80]{4,3,2,1,0:T(2,128)(2,1)S(1)} %get-tuple-element.17) | copy-start | bytes 491524
  5.9 1.0 copy-start.2
  7.2 1.0 copy-start.7
  17.3 6.3 %collective-permute-start = (f32[2,2,2,2,2,12800]{5,4,3,2,1,0:T(2,128)S(1)}, f32[2,2,2,2,2,12800]{5,4,3,2,1,0:T(2,128)}, u32[]{:S(2)}, u32[]{:S(2)}) collective-permute-start(f32[2,2,2,2,2,12800]{5,4,3,2,1,0:T(2,128)S(1)} %dynamic-slice_bitcast_fusion), channel_id=1, source_target_pairs={{0,12},{12,0},{24,36},{36,24},{48,60},{60,48},{72,84},{84,72},{96,... | collective-permute-start | bytes 4915208 | tf_op jit(solution)/shard_map/ppermute | solution.py:69
  26.3 4.4 %copy-start.3 = (f32[2,8,64,64]{2,3,1,0:T(8,128)S(1)}, f32[2,8,64,64]{2,3,1,0:T(8,128)}, u32[]{:S(2)}) copy-start(f32[2,8,64,64]{2,3,1,0:T(8,128)} %copy-done.2) | copy-start | bytes 786436
  26.4 4.4 %copy-start.12 = (f32[2,64,8,80]{3,2,1,0:T(8,128)S(1)}, f32[2,64,8,80]{3,2,1,0:T(8,128)}, u32[]{:S(2)}) copy-start(f32[2,64,8,80]{3,2,1,0:T(8,128)} %reshape.80) | copy-start | bytes 983044
  26.4 4.4 %copy-start.14 = (bf16[2,64,8,1,80]{4,3,2,1,0:T(2,128)(2,1)S(1)}, bf16[2,64,8,1,80]{4,3,2,1,0:T(2,128)(2,1)}, u32[]{:S(2)}) copy-start(bf16[2,64,8,1,80]{4,3,2,1,0:T(2,128)(2,1)} %copy-done.13) | copy-start | bytes 491524
  26.4 4.4 %copy-start.19 = (pred[2,64]{1,0:T(4,128)(4,1)S(1)}, pred[2,64]{1,0:T(4,128)(4,1)}, u32[]{:S(2)}) copy-start(pred[2,64]{1,0:T(4,128)(4,1)} %copy-done.18) | copy-start | bytes 388
  27.3 14.5 %collective-permute-start.1 = (f32[2,2,2,2,12800]{4,3,2,1,0:T(2,128)}, f32[2,2,2,2,12800]{4,3,2,1,0:T(2,128)}, u32[]{:S(2)}, u32[]{:S(2)}) collective-permute-start(f32[2,2,2,2,12800]{4,3,2,1,0:T(2,128)} %dynamic-slice_bitcast_fusion.1), channel_id=1, source_target_pairs={{0,24},{12,108},{24,0},{36,132},{48,72},{60,156},{72,48},{84,180},... | collective-permute-start | bytes 2457608 | tf_op jit(solution)/shard_map/ppermute | solution.py:69
  43.5 6.3 %copy-start.17 = (f32[2,8,64]{2,1,0:T(8,128)S(1)}, f32[2,8,64]{2,1,0:T(8,128)}, u32[]{:S(2)}) copy-start(f32[2,8,64]{2,1,0:T(8,128)} %get-tuple-element.13) | copy-start | bytes 12292
  43.5 15.1 %copy-start.1 = (f32[2,8,64,64]{2,3,1,0:T(8,128)S(1)}, f32[2,8,64,64]{2,3,1,0:T(8,128)}, u32[]{:S(2)}) copy-start(f32[2,8,64,64]{2,3,1,0:T(8,128)} %get-tuple-element.12) | copy-start | bytes 786436
  43.5 15.1 %copy-start.11 = (bf16[2,64,8,1,80]{4,3,2,1,0:T(2,128)(2,1)S(1)}, bf16[2,64,8,1,80]{4,3,2,1,0:T(2,128)(2,1)}, u32[]{:S(2)}) copy-start(bf16[2,64,8,1,80]{4,3,2,1,0:T(2,128)(2,1)} %copy-done.10) | copy-start | bytes 491524
  43.5 15.1 %copy-start.15 = (pred[2,8,64,64]{2,3,1,0:T(32,128)(4,1)S(1)}, pred[2,8,64,64]{2,3,1,0:T(32,128)(4,1)}, u32[]{:S(2)}) copy-start(pred[2,8,64,64]{2,3,1,0:T(32,128)(4,1)} %get-tuple-element.14) | copy-start | bytes 196612
  43.5 15.1 %copy-start.20 = (pred[2,64]{1,0:T(4,128)(4,1)S(1)}, pred[2,64]{1,0:T(4,128)(4,1)}, u32[]{:S(2)}) copy-start(pred[2,64]{1,0:T(4,128)(4,1)} %copy-done.18) | copy-start | bytes 388
  43.6 11.5 %collective-permute-start.2 = (f32[2,2,2,12800]{3,2,1,0:T(2,128)S(1)}, f32[2,2,2,12800]{3,2,1,0:T(2,128)S(1)}, u32[]{:S(2)}, u32[]{:S(2)}) collective-permute-start(f32[2,2,2,12800]{3,2,1,0:T(2,128)S(1)} %dynamic-slice_bitcast_fusion.2), channel_id=1, source_target_pairs={{0,48},{12,204},{24,72},{36,228},{48,0},{60,252},{72,24},{84,276},... | collective-permute-start | bytes 1228808 | tf_op jit(solution)/shard_map/ppermute | solution.py:69
  49.8 9.6 %copy-start.4 = (f32[2,8,64,64]{2,3,1,0:T(8,128)S(1)}, f32[2,8,64,64]{2,3,1,0:T(8,128)}, u32[]{:S(2)}) copy-start(f32[2,8,64,64]{2,3,1,0:T(8,128)} %copy-done.2) | copy-start | bytes 786436
  55.3 3.3 %copy-start.5 = (f32[2,2,2,12800]{3,2,1,0:T(2,128)}, f32[2,2,2,12800]{3,2,1,0:T(2,128)S(1)}, u32[]{:S(2)}) copy-start(f32[2,2,2,12800]{3,2,1,0:T(2,128)S(1)} %bitcast_add_fusion.2) | copy-start | bytes 1228804
  55.3 7.8 %collective-permute-start.3 = (f32[2,2,12800]{2,1,0:T(2,128)S(1)}, f32[2,2,12800]{2,1,0:T(2,128)}, u32[]{:S(2)}, u32[]{:S(2)}) collective-permute-start(f32[2,2,12800]{2,1,0:T(2,128)S(1)} %dynamic-slice_bitcast_fusion.3), channel_id=1, source_target_pairs={{0,96},{12,396},{24,120},{36,420},{48,144},{60,444},{72,168},{84,4... | collective-permute-start | bytes 614408 | tf_op jit(solution)/shard_map/ppermute | solution.py:69
  59.4 3.7 %copy-start.6 = (f32[2,2,2,12800]{3,2,1,0:T(2,128)S(1)}, f32[2,2,2,12800]{3,2,1,0:T(2,128)}, u32[]{:S(2)}) copy-start(f32[2,2,2,12800]{3,2,1,0:T(2,128)} %copy-done.5) | copy-start | bytes 1228804
  59.4 9.0 %copy-start.9 = (bf16[2,64,8,1,80]{4,3,2,1,0:T(2,128)(2,1)S(1)}, bf16[2,64,8,1,80]{4,3,2,1,0:T(2,128)(2,1)}, u32[]{:S(2)}) copy-start(bf16[2,64,8,1,80]{4,3,2,1,0:T(2,128)(2,1)} %copy-done.8) | copy-start | bytes 491524
  59.4 9.0 %copy-start.16 = (pred[2,8,64,64]{2,3,1,0:T(32,128)(4,1)S(1)}, pred[2,8,64,64]{2,3,1,0:T(32,128)(4,1)}, u32[]{:S(2)}) copy-start(pred[2,8,64,64]{2,3,1,0:T(32,128)(4,1)} %get-tuple-element.14) | copy-start | bytes 196612
  64.1 11.2 %collective-permute-start.4 = (f32[2,12800]{1,0:T(2,128)S(1)}, f32[2,12800]{1,0:T(2,128)S(1)}, u32[]{:S(2)}, u32[]{:S(2)}) collective-permute-start(f32[2,12800]{1,0:T(2,128)S(1)} %dynamic-slice_bitcast_fusion.4), channel_id=1, source_target_pairs={{0,192},{12,36},{24,216},{36,12},{48,240},{60,84},{72,264},{84,60}... | collective-permute-start | bytes 307208 | tf_op jit(solution)/shard_map/ppermute | solution.py:69
  75.6 10.0 %collective-permute-start.5 = (f32[12800]{0:T(1024)S(1)}, f32[12800]{0:T(1024)S(1)}, u32[]{:S(2)}, u32[]{:S(2)}) collective-permute-start(f32[12800]{0:T(1024)S(1)} %get-tuple-element.9), channel_id=1, source_target_pairs={{0,384},{12,60},{24,408},{36,84},{48,432},{60,12},{72,456},{84,36}... | collective-permute-start | bytes 153608 | tf_op jit(solution)/shard_map/ppermute | solution.py:69

commit v3 on v2

--- a/solution.py
+++ b/solution.py
@@ -56,18 +56,43 @@
     current = lax.dot_general(
         arranged, grad_rows, (((0,), (0,)), ((), ())), preferred_element_type=jnp.float32
     )
-    current = current.reshape((2,) * steps + (share * grad_rows.shape[1],))
     for step in range(steps):
         even_bit, odd_bit = orders[0][step], orders[1][step]
         bit = jnp.where(odd, odd_bit, even_bit)
         mine = (rank >> bit) & 1
-        keep = lax.dynamic_index_in_dim(current, mine, 0, keepdims=False)
-        send = lax.dynamic_index_in_dim(current, 1 - mine, 0, keepdims=False)
+        half = current.shape[0] // 2
+        keep = lax.dynamic_slice_in_dim(current, mine * half, half, axis=0)
+        send = lax.dynamic_slice_in_dim(current, (1 - mine) * half, half, axis=0)
         pairs = [
             (i, i ^ (1 << (odd_bit if i & 1 else even_bit))) for i in range(rank_total)
         ]
         current = keep + lax.ppermute(send, "row", pairs)
-    return current.reshape(share, grad_rows.shape[1])
+    return current
+
+
+def sum_cols(share):
+    col_total = lax.axis_size("col")
+    col = lax.axis_index("col")
+    group = 1
+    while group * 2 <= col_total and col_total % (group * 2) == 0:
+        pairs = [(i, i ^ group) for i in range(col_total)]
+        share = share + lax.ppermute(share, "col", pairs)
+        group *= 2
+    groups = col_total // group
+    if groups == 1:
+        return share
+    parts = [share]
+    for shift in range(1, groups):
+        pairs = [(i, (i + shift * group) % col_total) for i in range(col_total)]
+        parts.append(lax.ppermute(share, "col", pairs))
+    mine = col // group
+    total = None
+    for target in range(groups):
+        value = parts[0]
+        for k in range(1, groups):
+            value = jnp.where((mine - k) % groups == target, parts[k], value)
+        total = value if total is None else total + value
+    return total
 
 
 def body(qkv, cotangent, out_weight, live_patches):
@@ -84,7 +109,7 @@
         jnp.bfloat16
     )
     scale = (lax.axis_size("col") * lax.axis_size("row") * token_count) ** (-0.5)
-    d_weight = lax.all_gather(row_share, "col", axis=0, tiled=False).sum(0) * scale
+    d_weight = sum_cols(row_share) * scale
     return (output[None], d_qkv[None], d_weight)
 
 

time: 125 us -> 125 us (level)
  the two profiles are of different devices: /device:TPU:56 before, /device:TPU:44 now
where the time goes in v3:
time: 125 us; the launch traced here: 124 us
  starting transfers between devices  45.9 us (37%)
  waiting for transfers between devices  39.9 us (32%)
  local copies, waits for them, and re-layouts  16.4 us (13%)
  matrix products  12.4 us (10%)
  other arithmetic  7.68 us (6%)
  between operations  2.05 us (2%)
    ppermute x6, waiting for transfers between devices, reduce_rows(): current = keep + lax.ppermute(send, 'row', pairs)  30 us
    ppermute x6, starting transfers between devices, reduce_rows(): current = keep + lax.ppermute(send, 'row', pairs)  19.5 us
    ppermute x2, starting transfers between devices, sum_cols(): parts.append(lax.ppermute(share, 'col', pairs))  16.4 us
    ppermute x2, starting transfers between devices, sum_cols(): share = share + lax.ppermute(share, 'col', pairs)  10.1 us
    ppermute x2, waiting for transfers between devices, sum_cols(): parts.append(lax.ppermute(share, 'col', pairs))  6.73 us
    dot_general x3, matrix products, attend(): jnp.einsum('whpq,wqhc->wphc', probs.astype(jnp.float32), value, precision...  5.33 us
    add x6, other arithmetic, reduce_rows(): current = keep + lax.ppermute(send, 'row', pairs)  5.32 us
    dynamic_slice x6, local copies, waits for them, and re-layouts, reduce_rows(): send = lax.dynamic_slice_in_dim(current, (1 - mine) * half, half, axis=0)  3.42 us
  transfers between devices with their start and end apart: 10, of which 9 were waited for; matrix products, arithmetic and copies ran while one was open for 14% of the time, Pallas kernels for 0%

profile of v3, /device:TPU:44, one launch (start us, length us, event | category | flops | bytes accessed | tf_op | source)
XLA Modules:
  0.0 124.3 jit_solution(3621529121714194038)
XLA Ops:
  0.6 0.0 copy-start
  1.4 3.0 %reshape.78 = bf16[2,64,8,3,80]{4,3,2,1,0:T(4,128)(2,1)S(1)} reshape(bf16[1,128,1920]{2,1,0:T(8,128)(2,1)} %param.4) | data formatting | bytes 983040 | tf_op jit(solution)/shard_map/jvp()/reshape;squeeze | solution.py:15
  4.4 1.1 fusion.31
  5.6 0.3 fusion.32
  5.9 0.0 copy-start.3
  5.9 0.0 copy-start.18
  5.9 0.1 fusion.8
  6.0 0.3 copy-done.8
  6.3 0.2 copy-done.10
  6.5 0.4 copy-done.3
  6.9 0.3 fusion.4
  7.2 0.0 copy-start.6
  7.2 0.3 copy.20
  7.5 0.2 reshape.74
  7.7 0.1 slice_bitcast_fusion.1
  7.8 0.1 copy.61
  7.9 0.2 pad_maximum_fusion
  8.1 0.1 copy.23
  8.2 0.1 reshape.75
  8.2 2.2 %fusion.9 = f32[640,1280]{1,0:T(8,128)} fusion(bf16[128,640]{0,1:T(8,128)(2,1)S(1)} %reshape.75, bf16[1,128,1280]{2,1,0:T(8,128)(2,1)S(1)} %copy-done.6), kind=kOutput, calls=%fused_computation.28 | convolution fusion | flops 209715200 | bytes 3768320 | tf_op jit(solution)/shard_map/dot_general | solution.py:56
  10.5 1.5 %constant_dynamic-slice_fusion.5 = f32[320,1280]{1,0:T(8,128)S(1)} fusion(f32[640,1280]{1,0:T(8,128)} %fusion.9, s32[]{:T(128)S(6)} %select_n.139), kind=kLoop, calls=%fused_computation.64 | loop fusion | bytes 3276804 | tf_op jit(solution)/shard_map/dynamic_slice | solution.py:65
  12.0 1.9 %collective-permute-start = (f32[320,1280]{1,0:T(8,128)S(1)}, f32[320,1280]{1,0:T(8,128)}, u32[]{:S(2)}, u32[]{:S(2)}) collective-permute-start(f32[320,1280]{1,0:T(8,128)S(1)} %constant_dynamic-slice_fusion.5), channel_id=1, source_target_pairs={{0,12},{12,0},{24,36},{36,24},{48,60},{60,48},{72,84},{84,72},{96,... | collective-permute-start | bytes 4915208 | tf_op jit(solution)/shard_map/ppermute | solution.py:69
  14.0 3.6 %collective-permute-done = f32[320,1280]{1,0:T(8,128)} collective-permute-done((f32[320,1280]{1,0:T(8,128)S(1)}, f32[320,1280]{1,0:T(8,128)}, u32[]{:S(2)}, u32[]{:S(2)}) %collective-permute-start) | collective-permute-done | bytes 1638432 | tf_op jit(solution)/shard_map/ppermute | solution.py:69
  17.6 2.1 %dynamic-slice_add_fusion = f32[320,1280]{1,0:T(8,128)S(1)} fusion(f32[320,1280]{1,0:T(8,128)} %collective-permute-done, f32[640,1280]{1,0:T(8,128)} %fusion.9, s32[]{:T(128)S(6)} %select_n.138), kind=kLoop, calls=%fused_computation.2 | loop fusion | flops 409600 | bytes 4915204 | tf_op jit(solution)/shard_map/add | solution.py:69
  19.7 0.0 copy-start.7
  19.7 1.0 constant_dynamic-slice_fusion.4
  20.6 3.1 %collective-permute-start.1 = (f32[160,1280]{1,0:T(8,128)}, f32[160,1280]{1,0:T(8,128)}, u32[]{:S(2)}, u32[]{:S(2)}) collective-permute-start(f32[160,1280]{1,0:T(8,128)} %constant_dynamic-slice_fusion.4), channel_id=1, source_target_pairs={{0,24},{12,108},{24,0},{36,132},{48,72},{60,156},{72,48},{84,180},... | collective-permute-start | bytes 2457608 | tf_op jit(solution)/shard_map/ppermute | solution.py:69
  23.7 1.4 %fusion.5 = f32[128,640]{1,0:T(8,128)} fusion(bf16[640,1280]{1,0:T(8,128)(2,1)S(1)} %copy-done, bf16[1,128,1280]{2,1,0:T(8,128)(2,1)S(1)} %copy-done.7), kind=kOutput, calls=%fused_computation.15 | convolution fusion | flops 209879040 | bytes 2293760 | tf_op jit(solution)/shard_map/dot_general | solution.py:104
  25.1 0.9 copy.16
  26.0 1.9 %reshape.72 = bf16[128,640]{1,0:T(8,128)(2,1)} reshape(bf16[2,64,8,80]{3,2,1,0:T(8,128)(2,1)} %copy.16) | data formatting | bytes 327680 | tf_op jit(solution)/shard_map/jvp()/reshape | solution.py:31
  27.9 2.0 %reshape.76 = f32[2,64,8,80]{3,2,1,0:T(8,128)} reshape(f32[128,640]{1,0:T(8,128)} %fusion.5) | data formatting | bytes 655360 | tf_op jit(solution)/shard_map/transpose(jvp())/convert_element_type | solution.py:31
  29.9 3.0 %convert_reduce_fusion = (f32[2,8,64]{2,1,0:T(8,128)S(1)}, pred[2,8,64,64]{2,3,1,0:T(32,128)(4,1)}, f32[2,8,64]{2,1,0:T(8,128)S(1)}, f32[2,8,64,64]{2,3,1,0:T(8,128)}) fusion(f32[2,8,64,64]{2,3,1,0:T(8,128)} %copy-done.3, f32[2,8,64]{2,1,0:T(8,128)S(1)} %get-tuple-element.16, f32[2,8,64]{2,1,0:T(8,128)S(1)} %get-tuple-element.16, ...), kind=kOutput, calls=%fused_computation.21 | convolution fusion | flops 63584256 | bytes 1101952 | tf_op jit(solution)/shard_map/transpose(jvp(whpq,wqhc->wphc))/dot_general | solution.py:27
  32.9 2.2 %collective-permute-done.1 = f32[160,1280]{1,0:T(8,128)} collective-permute-done((f32[160,1280]{1,0:T(8,128)}, f32[160,1280]{1,0:T(8,128)}, u32[]{:S(2)}, u32[]{:S(2)}) %collective-permute-start.1) | collective-permute-done | bytes 819232 | tf_op jit(solution)/shard_map/ppermute | solution.py:69
  35.2 1.2 dynamic-slice_add_fusion.1
  36.4 0.9 constant_dynamic-slice_fusion.3
  37.3 2.4 %collective-permute-start.2 = (f32[80,1280]{1,0:T(8,128)}, f32[80,1280]{1,0:T(8,128)}, u32[]{:S(2)}, u32[]{:S(2)}) collective-permute-start(f32[80,1280]{1,0:T(8,128)} %constant_dynamic-slice_fusion.3), channel_id=1, source_target_pairs={{0,48},{12,204},{24,72},{36,228},{48,0},{60,252},{72,24},{84,276},... | collective-permute-start | bytes 1228808 | tf_op jit(solution)/shard_map/ppermute | solution.py:69
  39.7 0.2 fusion.30
  39.9 0.0 copy-start.19
  40.0 9.0 %collective-permute-done.2 = f32[80,1280]{1,0:T(8,128)} collective-permute-done((f32[80,1280]{1,0:T(8,128)}, f32[80,1280]{1,0:T(8,128)}, u32[]{:S(2)}, u32[]{:S(2)}) %collective-permute-start.2) | collective-permute-done | bytes 409632 | tf_op jit(solution)/shard_map/ppermute | solution.py:69
  48.9 1.0 dynamic-slice_add_fusion.2
  50.0 3.3 %collective-permute-start.3 = (f32[40,1280]{1,0:T(8,128)S(1)}, f32[40,1280]{1,0:T(8,128)S(1)}, u32[]{:S(2)}, u32[]{:S(2)}) collective-permute-start(f32[40,1280]{1,0:T(8,128)S(1)} %constant_dynamic-slice_fusion.2), channel_id=1, source_target_pairs={{0,96},{12,396},{24,120},{36,420},{48,144},{60,444},{72,168},{84,4... | collective-permute-start | bytes 614408 | tf_op jit(solution)/shard_map/ppermute | solution.py:69
  53.3 8.1 %collective-permute-done.3 = f32[40,1280]{1,0:T(8,128)S(1)} collective-permute-done((f32[40,1280]{1,0:T(8,128)S(1)}, f32[40,1280]{1,0:T(8,128)S(1)}, u32[]{:S(2)}, u32[]{:S(2)}) %collective-permute-start.3) | collective-permute-done | bytes 204832 | tf_op jit(solution)/shard_map/ppermute | solution.py:69
  61.4 2.2 %collective-permute-start.4 = (f32[20,1280]{1,0:T(8,128)S(1)}, f32[20,1280]{1,0:T(8,128)S(1)}, u32[]{:S(2)}, u32[]{:S(2)}) collective-permute-start(f32[20,1280]{1,0:T(8,128)S(1)} %constant_dynamic-slice_fusion.1), channel_id=1, source_target_pairs={{0,192},{12,36},{24,216},{36,12},{48,240},{60,84},{72,264},{84,60}... | collective-permute-start | bytes 307208 | tf_op jit(solution)/shard_map/ppermute | solution.py:69
  63.7 2.0 %convolution_bitcast_fusion.2 = f32[2,64,8,1,80]{4,1,2,0,3:T(8,128)} fusion(f32[2,64,8,80]{3,2,1,0:T(8,128)S(1)} %copy-done.14, pred[2,64]{1,0:T(4,128)(4,1)} %copy-done.20, f32[2,8,64,64]{2,3,1,0:T(8,128)S(1)} %copy-done.5, f32[2,8,64]{2,1,0:T(8,128)S(1)} %fusion.8, f32[2,8,64]{2,1,0:T(8,128)S(1)} %copy-done.19), kind=kOutput, calls=%fused_computation.6 | convolution fusion | flops 63193088 | bytes 925824 | tf_op jit(solution)/shard_map/transpose(jvp(whpq,wqhc->wphc))/dot_general | solution.py:27
  65.7 3.6 %collective-permute-done.4 = f32[20,1280]{1,0:T(8,128)S(1)} collective-permute-done((f32[20,1280]{1,0:T(8,128)S(1)}, f32[20,1280]{1,0:T(8,128)S(1)}, u32[]{:S(2)}, u32[]{:S(2)}) %collective-permute-start.4) | collective-permute-done | bytes 102432 | tf_op jit(solution)/shard_map/ppermute | solution.py:69
  69.3 6.6 %collective-permute-start.5 = (f32[10,1280]{1,0:T(8,128)S(1)}, f32[10,1280]{1,0:T(8,128)}, u32[]{:S(2)}, u32[]{:S(2)}) collective-permute-start(f32[10,1280]{1,0:T(8,128)S(1)} %constant_dynamic-slice_fusion), channel_id=1, source_target_pairs={{0,384},{12,60},{24,408},{36,84},{48,432},{60,12},{72,456},{84,36}... | collective-permute-start | bytes 153608 | tf_op jit(solution)/shard_map/ppermute | solution.py:69
  75.9 0.0 copy-done.12
  75.9 1.2 fusion
  77.1 3.6 %collective-permute-done.5 = f32[10,1280]{1,0:T(8,128)} collective-permute-done((f32[10,1280]{1,0:T(8,128)S(1)}, f32[10,1280]{1,0:T(8,128)}, u32[]{:S(2)}, u32[]{:S(2)}) %collective-permute-start.5) | collective-permute-done | bytes 51232 | tf_op jit(solution)/shard_map/ppermute | solution.py:69
  80.7 0.9 dynamic-slice_add_fusion.5
  81.6 4.4 %collective-permute-start.6 = (f32[10,1280]{1,0:T(8,128)S(1)}, f32[10,1280]{1,0:T(8,128)S(1)}, u32[]{:S(2)}, u32[]{:S(2)}) collective-permute-start(f32[10,1280]{1,0:T(8,128)S(1)} %dynamic-slice_add_fusion.5), channel_id=1, source_target_pairs={{0,1},{1,0},{2,3},{3,2},{4,5},{5,4},{6,7},{7,6},{8,9},{9,8},{10,11... | collective-permute-start | bytes 153608 | tf_op jit(solution)/shard_map/ppermute | solution.py:79
  86.0 1.4 %convolution_bitcast_fusion = f32[2,64,8,1,80]{4,1,2,0,3:T(8,128)S(1)} fusion(f32[2,8,64,64]{2,3,1,0:T(8,128)S(1)} %get-tuple-element.7, pred[2,8,64,64]{2,3,1,0:T(32,128)(4,1)S(1)} %copy-done.17, f32[2,8,64]{2,1,0:T(8,128)S(1)} %bitcast_divide_fusion, pred[2,64]{1,0:T(4,128)(4,1)} %copy-done.20, bf16[2,64,8,1,80]{4,3,2,1,0:T(2,128)(2,1)S(1)} %copy-done.11), kind=kOutput, calls=%fused_computation.4 | convolution fusion | flops 63176704 | bytes 823424 | tf_op jit(solution)/shard_map/transpose(jvp(wphc,wqhc->whpq))/dot_general | solution.py:21
  87.4 1.4 %collective-permute-done.6 = f32[10,1280]{1,0:T(8,128)S(1)} collective-permute-done((f32[10,1280]{1,0:T(8,128)S(1)}, f32[10,1280]{1,0:T(8,128)S(1)}, u32[]{:S(2)}, u32[]{:S(2)}) %collective-permute-start.6) | collective-permute-done | bytes 51232 | tf_op jit(solution)/shard_map/ppermute | solution.py:79
  88.8 5.7 %collective-permute-start.7 = (f32[10,1280]{1,0:T(8,128)S(1)}, f32[10,1280]{1,0:T(8,128)S(1)}, u32[]{:S(2)}, u32[]{:S(2)}) collective-permute-start(f32[10,1280]{1,0:T(8,128)S(1)} %add.114), channel_id=1, source_target_pairs={{0,2},{1,3},{2,0},{3,1},{4,6},{5,7},{6,4},{7,5},{8,10},{9,11},{10,... | collective-permute-start | bytes 153608 | tf_op jit(solution)/shard_map/ppermute | solution.py:79
  94.5 0.5 convolution_bitcast_fusion.1
  95.1 1.8 %collective-permute-done.7 = f32[10,1280]{1,0:T(8,128)S(1)} collective-permute-done((f32[10,1280]{1,0:T(8,128)S(1)}, f32[10,1280]{1,0:T(8,128)S(1)}, u32[]{:S(2)}, u32[]{:S(2)}) %collective-permute-start.7) | collective-permute-done | bytes 51232 | tf_op jit(solution)/shard_map/ppermute | solution.py:79
  96.9 14.5 %collective-permute-start.8 = (f32[10,1280]{1,0:T(8,128)S(1)}, f32[10,1280]{1,0:T(8,128)}, u32[]{:S(2)}, u32[]{:S(2)}) collective-permute-start(f32[10,1280]{1,0:T(8,128)S(1)} %add.115), channel_id=1, source_target_pairs={{0,8},{1,9},{2,10},{3,11},{4,0},{5,1},{6,2},{7,3},{8,4},{9,5},{10,... | collective-permute-start | bytes 153608 | tf_op jit(solution)/shard_map/ppermute | solution.py:87
  111.4 1.9 %collective-permute-start.9 = (f32[10,1280]{1,0:T(8,128)S(1)}, f32[10,1280]{1,0:T(8,128)}, u32[]{:S(2)}, u32[]{:S(2)}) collective-permute-start(f32[10,1280]{1,0:T(8,128)S(1)} %add.115), channel_id=1, source_target_pairs={{0,4},{1,5},{2,6},{3,7},{4,8},{5,9},{6,10},{7,11},{8,0},{9,1},{10,... | collective-permute-start | bytes 153608 | tf_op jit(solution)/shard_map/ppermute | solution.py:87
  113.3 0.2 add_convert_fusion
  113.6 0.7 copy.27
  114.3 1.7 %reshape.77 = bf16[1,128,1920]{2,1,0:T(8,128)(2,1)} reshape(bf16[2,64,8,3,80]{4,3,2,1,0:T(4,128)(2,1)S(1)} %copy.27) | data formatting | bytes 983040
  116.0 0.0 collective-permute-done.8
  116.0 6.7 %collective-permute-done.9 = f32[10,1280]{1,0:T(8,128)} collective-permute-done((f32[10,1280]{1,0:T(8,128)S(1)}, f32[10,1280]{1,0:T(8,128)}, u32[]{:S(2)}, u32[]{:S(2)}) %collective-permute-start.9) | collective-permute-done | bytes 51232 | tf_op jit(solution)/shard_map/ppermute | solution.py:87
  122.7 1.6 %add_multiply_fusion.1 = f32[10,1280]{1,0:T(8,128)} fusion(f32[10,1280]{1,0:T(8,128)} %collective-permute-done.8, f32[10,1280]{1,0:T(8,128)} %collective-permute-done.9, f32[10,1280]{1,0:T(8,128)S(1)} %add.115, pred[]{:T(512)S(6)} %eq.44, pred[]{:T(512)S(6)} %eq.43, pred[]{:T(512)S(6)} %eq.42, pred[]{:T(512)S(6)} %eq.41, pred[]{:T(512)S(6)} %eq.40, pred[]{:T(512)S(6)} %eq.38), kind=kLoop, calls=%fused_computation.53 | loop fusion | flops 115200 | bytes 204806 | tf_op jit(solution)/shard_map/mul | solution.py:112
  (46 shorter events, 0.2 us)
Async XLA Ops:
  0.6 23.1 %copy-start = (bf16[640,1280]{1,0:T(8,128)(2,1)S(1)}, bf16[640,1280]{1,0:T(8,128)(2,1)}, u32[]{:S(2)}) copy-start(bf16[640,1280]{1,0:T(8,128)(2,1)} %param.6) | copy-start | bytes 4915204
  1.4 4.6 %copy-start.20 = (pred[2,64]{1,0:T(4,128)(4,1)}, pred[2,64]{1,0:T(4,128)(4,1)S(1)}, u32[]{:S(2)}) copy-start(pred[2,64]{1,0:T(4,128)(4,1)S(1)} %add_compare_fusion) | copy-start | bytes 388
  5.5 0.8 copy-start.8
  5.5 1.0 copy-start.10
  5.5 4.9 %copy-start.15 = (bf16[2,64,8,1,80]{4,3,2,1,0:T(2,128)(2,1)}, bf16[2,64,8,1,80]{4,3,2,1,0:T(2,128)(2,1)S(1)}, u32[]{:S(2)}) copy-start(bf16[2,64,8,1,80]{4,3,2,1,0:T(2,128)(2,1)S(1)} %get-tuple-element.12) | copy-start | bytes 491524
  5.9 1.0 copy-start.3
  5.9 33.8 %copy-start.18 = (f32[2,8,64]{2,1,0:T(8,128)}, f32[2,8,64]{2,1,0:T(8,128)S(1)}, u32[]{:S(2)}) copy-start(f32[2,8,64]{2,1,0:T(8,128)S(1)} %get-tuple-element.16) | copy-start | bytes 12292
  7.2 1.1 copy-start.6
  12.0 5.5 %collective-permute-start = (f32[320,1280]{1,0:T(8,128)S(1)}, f32[320,1280]{1,0:T(8,128)}, u32[]{:S(2)}, u32[]{:S(2)}) collective-permute-start(f32[320,1280]{1,0:T(8,128)S(1)} %constant_dynamic-slice_fusion.5), channel_id=1, source_target_pairs={{0,12},{12,0},{24,36},{36,24},{48,60},{60,48},{72,84},{84,72},{96,... | collective-permute-start | bytes 4915208 | tf_op jit(solution)/shard_map/ppermute | solution.py:69
  19.7 4.1 %copy-start.7 = (bf16[1,128,1280]{2,1,0:T(8,128)(2,1)S(1)}, bf16[1,128,1280]{2,1,0:T(8,128)(2,1)}, u32[]{:S(2)}) copy-start(bf16[1,128,1280]{2,1,0:T(8,128)(2,1)} %param.5) | copy-start | bytes 983044
  20.6 14.5 %collective-permute-start.1 = (f32[160,1280]{1,0:T(8,128)}, f32[160,1280]{1,0:T(8,128)}, u32[]{:S(2)}, u32[]{:S(2)}) collective-permute-start(f32[160,1280]{1,0:T(8,128)} %constant_dynamic-slice_fusion.4), channel_id=1, source_target_pairs={{0,24},{12,108},{24,0},{36,132},{48,72},{60,156},{72,48},{84,180},... | collective-permute-start | bytes 2457608 | tf_op jit(solution)/shard_map/ppermute | solution.py:69
  32.9 6.8 %copy-start.4 = (f32[2,8,64,64]{2,3,1,0:T(8,128)S(1)}, f32[2,8,64,64]{2,3,1,0:T(8,128)}, u32[]{:S(2)}) copy-start(f32[2,8,64,64]{2,3,1,0:T(8,128)} %copy-done.3) | copy-start | bytes 786436
  32.9 6.8 %copy-start.13 = (f32[2,8,64,64]{2,3,1,0:T(8,128)S(1)}, f32[2,8,64,64]{2,3,1,0:T(8,128)}, u32[]{:S(2)}) copy-start(f32[2,8,64,64]{2,3,1,0:T(8,128)} %get-tuple-element.18) | copy-start | bytes 786436
  36.4 3.3 %copy-start.1 = (f32[160,1280]{1,0:T(8,128)}, f32[160,1280]{1,0:T(8,128)S(1)}, u32[]{:S(2)}) copy-start(f32[160,1280]{1,0:T(8,128)S(1)} %dynamic-slice_add_fusion.1) | copy-start | bytes 2457604
  37.3 11.7 %collective-permute-start.2 = (f32[80,1280]{1,0:T(8,128)}, f32[80,1280]{1,0:T(8,128)}, u32[]{:S(2)}, u32[]{:S(2)}) collective-permute-start(f32[80,1280]{1,0:T(8,128)} %constant_dynamic-slice_fusion.3), channel_id=1, source_target_pairs={{0,48},{12,204},{24,72},{36,228},{48,0},{60,252},{72,24},{84,276},... | collective-permute-start | bytes 1228808 | tf_op jit(solution)/shard_map/ppermute | solution.py:69
  39.7 9.2 %copy-start.2 = (f32[160,1280]{1,0:T(8,128)S(1)}, f32[160,1280]{1,0:T(8,128)}, u32[]{:S(2)}) copy-start(f32[160,1280]{1,0:T(8,128)} %copy-done.1) | copy-start | bytes 2457604
  39.9 23.7 %copy-start.5 = (f32[2,8,64,64]{2,3,1,0:T(8,128)S(1)}, f32[2,8,64,64]{2,3,1,0:T(8,128)}, u32[]{:S(2)}) copy-start(f32[2,8,64,64]{2,3,1,0:T(8,128)} %copy-done.3) | copy-start | bytes 786436
  39.9 23.7 %copy-start.19 = (f32[2,8,64]{2,1,0:T(8,128)S(1)}, f32[2,8,64]{2,1,0:T(8,128)}, u32[]{:S(2)}) copy-start(f32[2,8,64]{2,1,0:T(8,128)} %copy-done.18) | copy-start | bytes 12292
  40.0 23.7 %copy-start.14 = (f32[2,64,8,80]{3,2,1,0:T(8,128)S(1)}, f32[2,64,8,80]{3,2,1,0:T(8,128)}, u32[]{:S(2)}) copy-start(f32[2,64,8,80]{3,2,1,0:T(8,128)} %reshape.76) | copy-start | bytes 983044
  50.0 11.4 %collective-permute-start.3 = (f32[40,1280]{1,0:T(8,128)S(1)}, f32[40,1280]{1,0:T(8,128)S(1)}, u32[]{:S(2)}, u32[]{:S(2)}) collective-permute-start(f32[40,1280]{1,0:T(8,128)S(1)} %constant_dynamic-slice_fusion.2), channel_id=1, source_target_pairs={{0,96},{12,396},{24,120},{36,420},{48,144},{60,444},{72,168},{84,4... | collective-permute-start | bytes 614408 | tf_op jit(solution)/shard_map/ppermute | solution.py:69
  61.4 14.5 %copy-start.12 = (bf16[128,640]{1,0:T(8,128)(2,1)S(1)}, bf16[128,640]{1,0:T(8,128)(2,1)}, u32[]{:S(2)}) copy-start(bf16[128,640]{1,0:T(8,128)(2,1)} %reshape.72) | copy-start | bytes 491524
  61.4 7.8 %collective-permute-start.4 = (f32[20,1280]{1,0:T(8,128)S(1)}, f32[20,1280]{1,0:T(8,128)S(1)}, u32[]{:S(2)}, u32[]{:S(2)}) collective-permute-start(f32[20,1280]{1,0:T(8,128)S(1)} %constant_dynamic-slice_fusion.1), channel_id=1, source_target_pairs={{0,192},{12,36},{24,216},{36,12},{48,240},{60,84},{72,264},{84,60}... | collective-permute-start | bytes 307208 | tf_op jit(solution)/shard_map/ppermute | solution.py:69
  65.7 20.3 %copy-start.11 = (bf16[2,64,8,1,80]{4,3,2,1,0:T(2,128)(2,1)S(1)}, bf16[2,64,8,1,80]{4,3,2,1,0:T(2,128)(2,1)}, u32[]{:S(2)}) copy-start(bf16[2,64,8,1,80]{4,3,2,1,0:T(2,128)(2,1)} %copy-done.10) | copy-start | bytes 491524
  65.7 20.3 %copy-start.17 = (pred[2,8,64,64]{2,3,1,0:T(32,128)(4,1)S(1)}, pred[2,8,64,64]{2,3,1,0:T(32,128)(4,1)}, u32[]{:S(2)}) copy-start(pred[2,8,64,64]{2,3,1,0:T(32,128)(4,1)} %get-tuple-element.9) | copy-start | bytes 196612
  69.3 25.2 %copy-start.9 = (bf16[2,64,8,1,80]{4,3,2,1,0:T(2,128)(2,1)S(1)}, bf16[2,64,8,1,80]{4,3,2,1,0:T(2,128)(2,1)}, u32[]{:S(2)}) copy-start(bf16[2,64,8,1,80]{4,3,2,1,0:T(2,128)(2,1)} %copy-done.8) | copy-start | bytes 491524
  69.3 11.4 %collective-permute-start.5 = (f32[10,1280]{1,0:T(8,128)S(1)}, f32[10,1280]{1,0:T(8,128)}, u32[]{:S(2)}, u32[]{:S(2)}) collective-permute-start(f32[10,1280]{1,0:T(8,128)S(1)} %constant_dynamic-slice_fusion), channel_id=1, source_target_pairs={{0,384},{12,60},{24,408},{36,84},{48,432},{60,12},{72,456},{84,36}... | collective-permute-start | bytes 153608 | tf_op jit(solution)/shard_map/ppermute | solution.py:69
  77.1 17.4 %copy-start.21 = (pred[2,64]{1,0:T(4,128)(4,1)S(1)}, pred[2,64]{1,0:T(4,128)(4,1)}, u32[]{:S(2)}) copy-start(pred[2,64]{1,0:T(4,128)(4,1)} %copy-done.20) | copy-start | bytes 388
  81.6 7.2 %collective-permute-start.6 = (f32[10,1280]{1,0:T(8,128)S(1)}, f32[10,1280]{1,0:T(8,128)S(1)}, u32[]{:S(2)}, u32[]{:S(2)}) collective-permute-start(f32[10,1280]{1,0:T(8,128)S(1)} %dynamic-slice_add_fusion.5), channel_id=1, source_target_pairs={{0,1},{1,0},{2,3},{3,2},{4,5},{5,4},{6,7},{7,6},{8,9},{9,8},{10,11... | collective-permute-start | bytes 153608 | tf_op jit(solution)/shard_map/ppermute | solution.py:79
  86.0 27.3 %copy-start.16 = (f32[2,64,8,1,80]{4,1,2,0,3:T(8,128)S(1)}, f32[2,64,8,1,80]{4,1,2,0,3:T(8,128)}, u32[]{:S(2)}) copy-start(f32[2,64,8,1,80]{4,1,2,0,3:T(8,128)} %convolution_bitcast_fusion.2) | copy-start | bytes 983044
  88.8 8.1 %collective-permute-start.7 = (f32[10,1280]{1,0:T(8,128)S(1)}, f32[10,1280]{1,0:T(8,128)S(1)}, u32[]{:S(2)}, u32[]{:S(2)}) collective-permute-start(f32[10,1280]{1,0:T(8,128)S(1)} %add.114), channel_id=1, source_target_pairs={{0,2},{1,3},{2,0},{3,1},{4,6},{5,7},{6,4},{7,5},{8,10},{9,11},{10,... | collective-permute-start | bytes 153608 | tf_op jit(solution)/shard_map/ppermute | solution.py:79
  96.9 19.1 %collective-permute-start.8 = (f32[10,1280]{1,0:T(8,128)S(1)}, f32[10,1280]{1,0:T(8,128)}, u32[]{:S(2)}, u32[]{:S(2)}) collective-permute-start(f32[10,1280]{1,0:T(8,128)S(1)} %add.115), channel_id=1, source_target_pairs={{0,8},{1,9},{2,10},{3,11},{4,0},{5,1},{6,2},{7,3},{8,4},{9,5},{10,... | collective-permute-start | bytes 153608 | tf_op jit(solution)/shard_map/ppermute | solution.py:87
  111.4 11.4 %collective-permute-start.9 = (f32[10,1280]{1,0:T(8,128)S(1)}, f32[10,1280]{1,0:T(8,128)}, u32[]{:S(2)}, u32[]{:S(2)}) collective-permute-start(f32[10,1280]{1,0:T(8,128)S(1)} %add.115), channel_id=1, source_target_pairs={{0,4},{1,5},{2,6},{3,7},{4,8},{5,9},{6,10},{7,11},{8,0},{9,1},{10,... | collective-permute-start | bytes 153608 | tf_op jit(solution)/shard_map/ppermute | solution.py:87

commit v4 on v3

--- a/solution.py
+++ b/solution.py
@@ -31,10 +31,19 @@
     return attended.astype(jnp.bfloat16).reshape(token_count, H * HD)
 
 
-def bit_orders(steps):
-    low = list(range(1, steps))
-    split = min(2, steps - 1)
-    return [0] + low, [0] + low[split:] + low[:split]
+def bit_steps(steps):
+    low = [tuple(range(1, min(3, steps)))] if steps > 1 else []
+    high = [tuple(range(3, min(5, steps)))] if steps > 3 else []
+    rest = [(bit,) for bit in range(5, steps)]
+    return [(0,)] + low + high + rest, [(0,)] + high + low + rest
+
+
+def spread(bits, delta):
+    out = 0
+    for k, bit in enumerate(bits):
+        if (delta >> (len(bits) - 1 - k)) & 1:
+            out |= 1 << bit
+    return out
 
 
 def reduce_rows(columns, grad_rows):
@@ -42,7 +51,8 @@
     steps = rank_total.bit_length() - 1
     rank = lax.axis_index("row")
     odd = (rank & 1) == 1
-    orders = bit_orders(steps)
+    even_steps, odd_steps = bit_steps(steps)
+    orders = [[bit for part in plan for bit in part] for plan in (even_steps, odd_steps)]
     token_count, width = columns.shape
     share = width // rank_total
 
@@ -56,28 +66,42 @@
     current = lax.dot_general(
         arranged, grad_rows, (((0,), (0,)), ((), ())), preferred_element_type=jnp.float32
     )
-    for step in range(steps):
-        even_bit, odd_bit = orders[0][step], orders[1][step]
-        bit = jnp.where(odd, odd_bit, even_bit)
-        mine = (rank >> bit) & 1
-        half = current.shape[0] // 2
-        keep = lax.dynamic_slice_in_dim(current, mine * half, half, axis=0)
-        send = lax.dynamic_slice_in_dim(current, (1 - mine) * half, half, axis=0)
-        pairs = [
-            (i, i ^ (1 << (odd_bit if i & 1 else even_bit))) for i in range(rank_total)
-        ]
-        current = keep + lax.ppermute(send, "row", pairs)
+    for even_bits, odd_bits in zip(even_steps, odd_steps):
+        count = 1 << len(even_bits)
+        mine = jnp.zeros((), jnp.int32)
+        for k in range(len(even_bits)):
+            bit = jnp.where(odd, odd_bits[k], even_bits[k])
+            mine = mine | (((rank >> bit) & 1) << (len(even_bits) - 1 - k))
+        part = current.shape[0] // count
+        total = lax.dynamic_slice_in_dim(current, mine * part, part, axis=0)
+        for delta in range(1, count):
+            send = lax.dynamic_slice_in_dim(current, (mine ^ delta) * part, part, axis=0)
+            pairs = [
+                (i, i ^ spread(odd_bits if i & 1 else even_bits, delta))
+                for i in range(rank_total)
+            ]
+            total = total + lax.ppermute(send, "row", pairs)
+        current = total
     return current
 
 
 def sum_cols(share):
     col_total = lax.axis_size("col")
     col = lax.axis_index("col")
-    group = 1
-    while group * 2 <= col_total and col_total % (group * 2) == 0:
-        pairs = [(i, i ^ group) for i in range(col_total)]
-        share = share + lax.ppermute(share, "col", pairs)
-        group *= 2
+    group = 4
+    while col_total % group:
+        group //= 2
+    got = {0: share}
+    for delta in range(1, group):
+        got[delta] = lax.ppermute(share, "col", [(i, i ^ delta) for i in range(col_total)])
+    own = col % group
+    total = None
+    for member in range(group):
+        value = got[0]
+        for delta in range(1, group):
+            value = jnp.where((own ^ delta) == member, got[delta], value)
+        total = value if total is None else total + value
+    share = total
     groups = col_total // group
     if groups == 1:
         return share

time: 125 us -> 120 us (0.960)
  the two profiles are of different devices: /device:TPU:44 before, /device:TPU:1 now
where the time goes in v4:
time: 120 us; the launch traced here: 119 us
  starting transfers between devices  57.8 us (48%)
  waiting for transfers between devices  24.8 us (21%)
  local copies, waits for them, and re-layouts  15.4 us (13%)
  matrix products  10.8 us (9%)
  other arithmetic  8.33 us (7%)
  between operations  1.97 us (2%)
    ppermute x8, starting transfers between devices, reduce_rows(): total = total + lax.ppermute(send, 'row', pairs)  34.3 us
    ppermute x8, waiting for transfers between devices, reduce_rows(): total = total + lax.ppermute(send, 'row', pairs)  15.6 us
    ppermute x2, starting transfers between devices, sum_cols(): parts.append(lax.ppermute(share, 'col', pairs))  14.2 us
    ppermute x3, starting transfers between devices, sum_cols(): lax.ppermute(share, 'col', [(i, i ^ delta) for i in range(col_total)])  9.26 us
    ppermute x2, waiting for transfers between devices, sum_cols(): parts.append(lax.ppermute(share, 'col', pairs))  6.97 us
    dot_general x3, matrix products, attend(): jnp.einsum('whpq,wqhc->wphc', probs.astype(jnp.float32), value, precision...  4.42 us
    add x4, other arithmetic, reduce_rows(): total = total + lax.ppermute(send, 'row', pairs)  3.79 us
    dynamic_slice x4, local copies, waits for them, and re-layouts, reduce_rows(): lax.dynamic_slice_in_dim(current, (mine ^ delta) * part, part, axis=0)  3.63 us
  transfers between devices with their start and end apart: 13, of which 6 were waited for; matrix products, arithmetic and copies ran while one was open for 12% of the time, Pallas kernels for 0%

profile of v4, /device:TPU:1, one launch (start us, length us, event | category | flops | bytes accessed | tf_op | source)
XLA Modules:
  0.0 119.0 jit_solution(10532724279775210483)
XLA Ops:
  0.6 0.0 copy-start
  1.4 0.0 copy-start.9
  1.4 3.0 %reshape.78 = bf16[2,64,8,3,80]{4,3,2,1,0:T(4,128)(2,1)S(1)} reshape(bf16[1,128,1920]{2,1,0:T(8,128)(2,1)} %param.4) | data formatting | bytes 983040 | tf_op jit(solution)/shard_map/jvp()/reshape;squeeze | solution.py:15
  4.4 1.1 fusion.31
  5.5 0.3 fusion.32
  5.9 0.1 fusion.8
  6.0 0.4 copy-done.2
  6.3 0.1 copy-done.8
  6.5 1.0 fusion.4
  7.5 1.3 %copy.20 = bf16[2,64,8,80]{1,0,2,3:T(2,128)(2,1)S(1)} copy(bf16[2,64,8,80]{3,1,2,0:T(8,128)(2,1)} %fusion.4) | data formatting | bytes 327680 | tf_op jit(solution)/shard_map/jvp()/convert_element_type | solution.py:31
  8.8 0.2 reshape.74
  8.9 0.1 slice_bitcast_fusion.1
  9.1 0.1 copy.61
  9.1 0.2 pad_maximum_fusion
  9.4 0.1 copy.23
  9.4 0.1 reshape.75
  9.5 2.3 %fusion.9 = f32[640,1280]{1,0:T(8,128)} fusion(bf16[128,640]{0,1:T(8,128)(2,1)S(1)} %reshape.75, bf16[1,128,1280]{2,1,0:T(8,128)(2,1)S(1)} %copy-done.1), kind=kOutput, calls=%fused_computation.27 | convolution fusion | flops 209715200 | bytes 3768320 | tf_op jit(solution)/shard_map/dot_general | solution.py:66
  11.8 2.8 %constant_dynamic-slice_fusion.7 = f32[320,1280]{1,0:T(8,128)} fusion(f32[640,1280]{1,0:T(8,128)} %fusion.9, s32[]{:T(128)S(6)} %select_n.215), kind=kLoop, calls=%fused_computation.65 | loop fusion | bytes 3276804 | tf_op jit(solution)/shard_map/dynamic_slice | solution.py:78
  14.6 12.4 %collective-permute-start = (f32[320,1280]{1,0:T(8,128)}, f32[320,1280]{1,0:T(8,128)}, u32[]{:S(2)}, u32[]{:S(2)}) collective-permute-start(f32[320,1280]{1,0:T(8,128)} %constant_dynamic-slice_fusion.7), channel_id=1, source_target_pairs={{0,12},{12,0},{24,36},{36,24},{48,60},{60,48},{72,84},{84,72},{96,... | collective-permute-start | bytes 4915208 | tf_op jit(solution)/shard_map/ppermute | solution.py:83
  27.0 0.9 copy.16
  27.9 1.9 %reshape.72 = bf16[128,640]{1,0:T(8,128)(2,1)} reshape(bf16[2,64,8,80]{3,2,1,0:T(8,128)(2,1)} %copy.16) | data formatting | bytes 327680 | tf_op jit(solution)/shard_map/jvp()/reshape | solution.py:31
  29.7 0.6 fusion.5
  30.4 0.2 reshape.76
  30.6 2.1 %convert_reduce_fusion = (f32[2,8,64]{2,1,0:T(8,128)S(1)}, pred[2,8,64,64]{2,3,1,0:T(32,128)(4,1)S(1)}, f32[2,8,64]{2,1,0:T(8,128)S(1)}, f32[2,8,64,64]{2,3,1,0:T(8,128)S(1)}) fusion(f32[2,8,64,64]{2,3,1,0:T(8,128)S(1)} %get-tuple-element.23, f32[2,8,64]{2,1,0:T(8,128)S(1)} %get-tuple-element.22, f32[2,8,64]{2,1,0:T(8,128)S(1)} %get-tuple-element.22, ...), kind=kOutput, calls=%fused_computation.20 | convolution fusion | flops 63584256 | bytes 1101952 | tf_op jit(solution)/shard_map/transpose(jvp(whpq,wqhc->wphc))/dot_general | solution.py:27
  32.8 0.2 fusion.30
  33.0 0.0 collective-permute-done
  33.0 2.1 %dynamic-slice_add_fusion = f32[320,1280]{1,0:T(8,128)S(1)} fusion(f32[320,1280]{1,0:T(8,128)} %collective-permute-done, f32[640,1280]{1,0:T(8,128)} %fusion.9, s32[]{:T(128)S(6)} %select_n.214), kind=kLoop, calls=%fused_computation.2 | loop fusion | flops 409600 | bytes 4915204 | tf_op jit(solution)/shard_map/add | solution.py:83
  35.2 0.0 copy-start.10
  35.2 0.1 constant_dynamic-slice_fusion.6
  35.3 2.1 %collective-permute-start.3 = (f32[80,1280]{1,0:T(8,128)S(1)}, f32[80,1280]{1,0:T(8,128)S(1)}, u32[]{:S(2)}, u32[]{:S(2)}) collective-permute-start(f32[80,1280]{1,0:T(8,128)S(1)} %get-tuple-element.11), channel_id=1, source_target_pairs={{0,72},{12,300},{24,48},{36,324},{48,24},{60,348},{72,0},{84,372},... | collective-permute-start | bytes 1228808 | tf_op jit(solution)/shard_map/ppermute | solution.py:83
  37.3 1.9 %collective-permute-start.2 = (f32[80,1280]{1,0:T(8,128)S(1)}, f32[80,1280]{1,0:T(8,128)S(1)}, u32[]{:S(2)}, u32[]{:S(2)}) collective-permute-start(f32[80,1280]{1,0:T(8,128)S(1)} %get-tuple-element.12), channel_id=1, source_target_pairs={{0,24},{12,108},{24,0},{36,132},{48,72},{60,156},{72,48},{84,180},... | collective-permute-start | bytes 1228808 | tf_op jit(solution)/shard_map/ppermute | solution.py:83
  39.3 5.4 %collective-permute-start.1 = (f32[80,1280]{1,0:T(8,128)S(1)}, f32[80,1280]{1,0:T(8,128)S(1)}, u32[]{:S(2)}, u32[]{:S(2)}) collective-permute-start(f32[80,1280]{1,0:T(8,128)S(1)} %get-tuple-element.10), channel_id=1, source_target_pairs={{0,48},{12,204},{24,72},{36,228},{48,0},{60,252},{72,24},{84,276},... | collective-permute-start | bytes 1228808 | tf_op jit(solution)/shard_map/ppermute | solution.py:83
  44.7 1.3 %convolution_bitcast_fusion.2 = f32[2,64,8,1,80]{4,1,2,0,3:T(8,128)} fusion(f32[2,64,8,80]{3,2,1,0:T(8,128)S(1)} %copy-done.7, pred[2,64]{1,0:T(4,128)(4,1)S(1)} %copy-done.10, f32[2,8,64,64]{2,3,1,0:T(8,128)S(1)} %get-tuple-element.23, f32[2,8,64]{2,1,0:T(8,128)S(1)} %fusion.8, f32[2,8,64]{2,1,0:T(8,128)S(1)} %get-tuple-element.22), kind=kOutput, calls=%fused_computation.6 | convolution fusion | flops 63193088 | bytes 925824 | tf_op jit(solution)/shard_map/transpose(jvp(whpq,wqhc->wphc))/dot_general | solution.py:27
  46.1 0.0 collective-permute-done.3
  46.1 8.6 %collective-permute-done.2 = f32[80,1280]{1,0:T(8,128)S(1)} collective-permute-done((f32[80,1280]{1,0:T(8,128)S(1)}, f32[80,1280]{1,0:T(8,128)S(1)}, u32[]{:S(2)}, u32[]{:S(2)}) %collective-permute-start.2) | collective-permute-done | bytes 409632 | tf_op jit(solution)/shard_map/ppermute | solution.py:83
  54.7 0.0 collective-permute-done.1
  54.7 0.1 add_add_fusion
  54.8 0.1 constant_dynamic-slice_fusion.3
  54.9 2.1 %collective-permute-start.6 = (f32[20,1280]{1,0:T(8,128)S(1)}, f32[20,1280]{1,0:T(8,128)S(1)}, u32[]{:S(2)}, u32[]{:S(2)}) collective-permute-start(f32[20,1280]{1,0:T(8,128)S(1)} %get-tuple-element.18), channel_id=1, source_target_pairs={{0,288},{12,84},{24,312},{36,60},{48,336},{60,36},{72,360},{84,12}... | collective-permute-start | bytes 307208 | tf_op jit(solution)/shard_map/ppermute | solution.py:83
  56.9 1.9 %collective-permute-start.5 = (f32[20,1280]{1,0:T(8,128)S(1)}, f32[20,1280]{1,0:T(8,128)S(1)}, u32[]{:S(2)}, u32[]{:S(2)}) collective-permute-start(f32[20,1280]{1,0:T(8,128)S(1)} %get-tuple-element.19), channel_id=1, source_target_pairs={{0,96},{12,36},{24,120},{36,12},{48,144},{60,84},{72,168},{84,60},... | collective-permute-start | bytes 307208 | tf_op jit(solution)/shard_map/ppermute | solution.py:83
  58.9 5.7 %collective-permute-start.4 = (f32[20,1280]{1,0:T(8,128)S(1)}, f32[20,1280]{1,0:T(8,128)S(1)}, u32[]{:S(2)}, u32[]{:S(2)}) collective-permute-start(f32[20,1280]{1,0:T(8,128)S(1)} %get-tuple-element.17), channel_id=1, source_target_pairs={{0,192},{12,60},{24,216},{36,84},{48,240},{60,12},{72,264},{84,36}... | collective-permute-start | bytes 307208 | tf_op jit(solution)/shard_map/ppermute | solution.py:83
  64.6 1.2 fusion
  65.8 0.0 collective-permute-done.6
  65.8 0.0 collective-permute-done.5
  65.8 1.1 collective-permute-done.4
  66.9 0.7 constant_dynamic-slice_fusion
  67.5 2.8 %collective-permute-start.7 = (f32[10,1280]{1,0:T(8,128)}, f32[10,1280]{1,0:T(8,128)}, u32[]{:S(2)}, u32[]{:S(2)}) collective-permute-start(f32[10,1280]{1,0:T(8,128)} %constant_dynamic-slice_fusion), channel_id=1, source_target_pairs={{0,384},{12,396},{24,408},{36,420},{48,432},{60,444},{72,456},{84,... | collective-permute-start | bytes 153608 | tf_op jit(solution)/shard_map/ppermute | solution.py:83
  70.4 0.7 convolution_bitcast_fusion
  71.1 5.9 %collective-permute-done.7 = f32[10,1280]{1,0:T(8,128)} collective-permute-done((f32[10,1280]{1,0:T(8,128)}, f32[10,1280]{1,0:T(8,128)}, u32[]{:S(2)}, u32[]{:S(2)}) %collective-permute-start.7) | collective-permute-done | bytes 51232 | tf_op jit(solution)/shard_map/ppermute | solution.py:83
  76.9 1.5 %dynamic-slice_add_fusion.1 = f32[10,1280]{1,0:T(8,128)} fusion(f32[10,1280]{1,0:T(8,128)} %collective-permute-done.7, f32[20,1280]{1,0:T(8,128)S(1)} %add_add_fusion.1, s32[]{:T(128)S(6)} %select_n.228), kind=kLoop, calls=%fused_computation.53 | loop fusion | flops 12800 | bytes 153604 | tf_op jit(solution)/shard_map/add | solution.py:83
  78.5 3.8 %collective-permute-start.8 = (f32[10,1280]{1,0:T(8,128)}, f32[10,1280]{1,0:T(8,128)S(1)}, u32[]{:S(2)}, u32[]{:S(2)}) collective-permute-start(f32[10,1280]{1,0:T(8,128)} %dynamic-slice_add_fusion.1), channel_id=1, source_target_pairs={{0,3},{1,2},{2,1},{3,0},{4,7},{5,6},{6,5},{7,4},{8,11},{9,10},{10,... | collective-permute-start | bytes 153608 | tf_op jit(solution)/shard_map/ppermute | solution.py:96
  82.3 1.9 %collective-permute-start.9 = (f32[10,1280]{1,0:T(8,128)}, f32[10,1280]{1,0:T(8,128)}, u32[]{:S(2)}, u32[]{:S(2)}) collective-permute-start(f32[10,1280]{1,0:T(8,128)} %dynamic-slice_add_fusion.1), channel_id=1, source_target_pairs={{0,2},{1,3},{2,0},{3,1},{4,6},{5,7},{6,4},{7,5},{8,10},{9,11},{10,... | collective-permute-start | bytes 153608 | tf_op jit(solution)/shard_map/ppermute | solution.py:96
  84.2 3.5 %collective-permute-start.10 = (f32[10,1280]{1,0:T(8,128)}, f32[10,1280]{1,0:T(8,128)}, u32[]{:S(2)}, u32[]{:S(2)}) collective-permute-start(f32[10,1280]{1,0:T(8,128)} %dynamic-slice_add_fusion.1), channel_id=1, source_target_pairs={{0,1},{1,0},{2,3},{3,2},{4,5},{5,4},{6,7},{7,6},{8,9},{9,8},{10,11... | collective-permute-start | bytes 153608 | tf_op jit(solution)/shard_map/ppermute | solution.py:96
  87.8 1.3 %convolution_bitcast_fusion.1 = f32[2,64,8,1,80]{4,1,2,0,3:T(8,128)} fusion(f32[2,8,64,64]{2,3,1,0:T(8,128)S(1)} %get-tuple-element.7, pred[2,8,64,64]{2,3,1,0:T(32,128)(4,1)S(1)} %get-tuple-element.9, f32[2,8,64]{2,1,0:T(8,128)S(1)} %bitcast_divide_fusion, pred[2,64]{1,0:T(4,128)(4,1)S(1)} %copy-done.10, bf16[2,64,8,1,80]{4,3,2,1,0:T(2,128)(2,1)S(1)} %get-tuple-element.14), kind=kOutput, calls=%fused_computation.5 | convolution fusion | flops 63176704 | bytes 823424 | tf_op jit(solution)/shard_map/transpose(jvp(wphc,wqhc->whpq))/dot_general | solution.py:21
  89.1 2.2 %collective-permute-done.10 = f32[10,1280]{1,0:T(8,128)} collective-permute-done((f32[10,1280]{1,0:T(8,128)}, f32[10,1280]{1,0:T(8,128)}, u32[]{:S(2)}, u32[]{:S(2)}) %collective-permute-start.10) | collective-permute-done | bytes 51232 | tf_op jit(solution)/shard_map/ppermute | solution.py:96
  91.3 1.0 select_add_fusion
  92.4 12.3 %collective-permute-start.11 = (f32[10,1280]{1,0:T(8,128)S(1)}, f32[10,1280]{1,0:T(8,128)}, u32[]{:S(2)}, u32[]{:S(2)}) collective-permute-start(f32[10,1280]{1,0:T(8,128)S(1)} %select_add_fusion), channel_id=1, source_target_pairs={{0,8},{1,9},{2,10},{3,11},{4,0},{5,1},{6,2},{7,3},{8,4},{9,5},{10,... | collective-permute-start | bytes 153608 | tf_op jit(solution)/shard_map/ppermute | solution.py:111
  104.7 1.9 %collective-permute-start.12 = (f32[10,1280]{1,0:T(8,128)S(1)}, f32[10,1280]{1,0:T(8,128)}, u32[]{:S(2)}, u32[]{:S(2)}) collective-permute-start(f32[10,1280]{1,0:T(8,128)S(1)} %select_add_fusion), channel_id=1, source_target_pairs={{0,4},{1,5},{2,6},{3,7},{4,8},{5,9},{6,10},{7,11},{8,0},{9,1},{10,... | collective-permute-start | bytes 153608 | tf_op jit(solution)/shard_map/ppermute | solution.py:111
  106.6 1.4 %add_convert_fusion = bf16[2,64,8,3,80]{4,1,2,0,3:T(8,128)(2,1)S(1)} fusion(f32[2,64,8,1,80]{4,1,2,0,3:T(8,128)S(1)} %convolution_bitcast_fusion, f32[2,64,8,1,80]{4,1,2,0,3:T(8,128)} %convolution_bitcast_fusion.1, f32[2,64,8,1,80]{4,1,2,0,3:T(8,128)} %convolution_bitcast_fusion.2), kind=kLoop, calls=%fused_computation.3 | loop fusion | flops 737280 | bytes 1474560 | tf_op jit(solution)/shard_map/transpose(jvp())/convert_element_type | solution.py:15
  108.1 0.7 copy.27
  108.7 1.7 %reshape.77 = bf16[1,128,1920]{2,1,0:T(8,128)(2,1)} reshape(bf16[2,64,8,3,80]{4,3,2,1,0:T(4,128)(2,1)S(1)} %copy.27) | data formatting | bytes 983040
  110.5 0.8 collective-permute-done.11
  111.3 6.2 %collective-permute-done.12 = f32[10,1280]{1,0:T(8,128)} collective-permute-done((f32[10,1280]{1,0:T(8,128)S(1)}, f32[10,1280]{1,0:T(8,128)}, u32[]{:S(2)}, u32[]{:S(2)}) %collective-permute-start.12) | collective-permute-done | bytes 51232 | tf_op jit(solution)/shard_map/ppermute | solution.py:111
  117.4 1.6 %add_multiply_fusion.1 = f32[10,1280]{1,0:T(8,128)} fusion(f32[10,1280]{1,0:T(8,128)} %collective-permute-done.11, f32[10,1280]{1,0:T(8,128)} %collective-permute-done.12, f32[10,1280]{1,0:T(8,128)S(1)} %select_add_fusion, pred[]{:T(512)S(6)} %eq.93, pred[]{:T(512)S(6)} %eq.92, pred[]{:T(512)S(6)} %eq.91, pred[]{:T(512)S(6)} %eq.90, pred[]{:T(512)S(6)} %eq.89, ...), kind=kLoop, calls=%fused_computation.51 | loop fusion | flops 115200 | bytes 204806 | tf_op jit(solution)/shard_map/mul | solution.py:136
  (25 shorter events, 0.1 us)
Async XLA Ops:
  0.6 29.1 %copy-start = (bf16[640,1280]{1,0:T(8,128)(2,1)S(1)}, bf16[640,1280]{1,0:T(8,128)(2,1)}, u32[]{:S(2)}) copy-start(bf16[640,1280]{1,0:T(8,128)(2,1)} %param.6) | copy-start | bytes 4915204
  1.4 4.5 %copy-start.9 = (pred[2,64]{1,0:T(4,128)(4,1)}, pred[2,64]{1,0:T(4,128)(4,1)S(1)}, u32[]{:S(2)}) copy-start(pred[2,64]{1,0:T(4,128)(4,1)S(1)} %add_compare_fusion) | copy-start | bytes 388
  5.5 0.8 copy-start.2
  5.5 1.0 copy-start.8
  7.5 2.0 %copy-start.1 = (bf16[1,128,1280]{2,1,0:T(8,128)(2,1)S(1)}, bf16[1,128,1280]{2,1,0:T(8,128)(2,1)}, u32[]{:S(2)}) copy-start(bf16[1,128,1280]{2,1,0:T(8,128)(2,1)} %param.5) | copy-start | bytes 983044
  11.8 15.2 %copy-start.4 = (bf16[2,64,8,80]{3,1,2,0:T(8,128)(2,1)S(1)}, bf16[2,64,8,80]{3,1,2,0:T(8,128)(2,1)}, u32[]{:S(2)}) copy-start(bf16[2,64,8,80]{3,1,2,0:T(8,128)(2,1)} %fusion.4) | copy-start | bytes 491524
  14.6 18.4 %collective-permute-start = (f32[320,1280]{1,0:T(8,128)}, f32[320,1280]{1,0:T(8,128)}, u32[]{:S(2)}, u32[]{:S(2)}) collective-permute-start(f32[320,1280]{1,0:T(8,128)} %constant_dynamic-slice_fusion.7), channel_id=1, source_target_pairs={{0,12},{12,0},{24,36},{36,24},{48,60},{60,48},{72,84},{84,72},{96,... | collective-permute-start | bytes 4915208 | tf_op jit(solution)/shard_map/ppermute | solution.py:83
  30.6 2.1 %copy-start.6 = (f32[2,64,8,80]{3,2,1,0:T(8,128)}, f32[2,64,8,80]{3,2,1,0:T(8,128)S(1)}, u32[]{:S(2)}) copy-start(f32[2,64,8,80]{3,2,1,0:T(8,128)S(1)} %reshape.76) | copy-start | bytes 983044
  35.1 9.6 %copy-start.7 = (f32[2,64,8,80]{3,2,1,0:T(8,128)S(1)}, f32[2,64,8,80]{3,2,1,0:T(8,128)}, u32[]{:S(2)}) copy-start(f32[2,64,8,80]{3,2,1,0:T(8,128)} %copy-done.6) | copy-start | bytes 983044
  35.2 9.6 %copy-start.10 = (pred[2,64]{1,0:T(4,128)(4,1)S(1)}, pred[2,64]{1,0:T(4,128)(4,1)}, u32[]{:S(2)}) copy-start(pred[2,64]{1,0:T(4,128)(4,1)} %copy-done.9) | copy-start | bytes 388
  35.3 10.8 %collective-permute-start.3 = (f32[80,1280]{1,0:T(8,128)S(1)}, f32[80,1280]{1,0:T(8,128)S(1)}, u32[]{:S(2)}, u32[]{:S(2)}) collective-permute-start(f32[80,1280]{1,0:T(8,128)S(1)} %get-tuple-element.11), channel_id=1, source_target_pairs={{0,72},{12,300},{24,48},{36,324},{48,24},{60,348},{72,0},{84,372},... | collective-permute-start | bytes 1228808 | tf_op jit(solution)/shard_map/ppermute | solution.py:83
  37.3 17.3 %collective-permute-start.2 = (f32[80,1280]{1,0:T(8,128)S(1)}, f32[80,1280]{1,0:T(8,128)S(1)}, u32[]{:S(2)}, u32[]{:S(2)}) collective-permute-start(f32[80,1280]{1,0:T(8,128)S(1)} %get-tuple-element.12), channel_id=1, source_target_pairs={{0,24},{12,108},{24,0},{36,132},{48,72},{60,156},{72,48},{84,180},... | collective-permute-start | bytes 1228808 | tf_op jit(solution)/shard_map/ppermute | solution.py:83
  39.3 15.4 %collective-permute-start.1 = (f32[80,1280]{1,0:T(8,128)S(1)}, f32[80,1280]{1,0:T(8,128)S(1)}, u32[]{:S(2)}, u32[]{:S(2)}) collective-permute-start(f32[80,1280]{1,0:T(8,128)S(1)} %get-tuple-element.10), channel_id=1, source_target_pairs={{0,48},{12,204},{24,72},{36,228},{48,0},{60,252},{72,24},{84,276},... | collective-permute-start | bytes 1228808 | tf_op jit(solution)/shard_map/ppermute | solution.py:83
  46.1 18.5 %copy-start.5 = (bf16[128,640]{1,0:T(8,128)(2,1)S(1)}, bf16[128,640]{1,0:T(8,128)(2,1)}, u32[]{:S(2)}) copy-start(bf16[128,640]{1,0:T(8,128)(2,1)} %reshape.72) | copy-start | bytes 491524
  54.9 15.5 %copy-start.3 = (bf16[2,64,8,1,80]{4,3,2,1,0:T(2,128)(2,1)S(1)}, bf16[2,64,8,1,80]{4,3,2,1,0:T(2,128)(2,1)}, u32[]{:S(2)}) copy-start(bf16[2,64,8,1,80]{4,3,2,1,0:T(2,128)(2,1)} %copy-done.2) | copy-start | bytes 491524
  54.9 10.9 %collective-permute-start.6 = (f32[20,1280]{1,0:T(8,128)S(1)}, f32[20,1280]{1,0:T(8,128)S(1)}, u32[]{:S(2)}, u32[]{:S(2)}) collective-permute-start(f32[20,1280]{1,0:T(8,128)S(1)} %get-tuple-element.18), channel_id=1, source_target_pairs={{0,288},{12,84},{24,312},{36,60},{48,336},{60,36},{72,360},{84,12}... | collective-permute-start | bytes 307208 | tf_op jit(solution)/shard_map/ppermute | solution.py:83
  56.9 8.9 %collective-permute-start.5 = (f32[20,1280]{1,0:T(8,128)S(1)}, f32[20,1280]{1,0:T(8,128)S(1)}, u32[]{:S(2)}, u32[]{:S(2)}) collective-permute-start(f32[20,1280]{1,0:T(8,128)S(1)} %get-tuple-element.19), channel_id=1, source_target_pairs={{0,96},{12,36},{24,120},{36,12},{48,144},{60,84},{72,168},{84,60},... | collective-permute-start | bytes 307208 | tf_op jit(solution)/shard_map/ppermute | solution.py:83
  58.9 8.0 %collective-permute-start.4 = (f32[20,1280]{1,0:T(8,128)S(1)}, f32[20,1280]{1,0:T(8,128)S(1)}, u32[]{:S(2)}, u32[]{:S(2)}) collective-permute-start(f32[20,1280]{1,0:T(8,128)S(1)} %get-tuple-element.17), channel_id=1, source_target_pairs={{0,192},{12,60},{24,216},{36,84},{48,240},{60,12},{72,264},{84,36}... | collective-permute-start | bytes 307208 | tf_op jit(solution)/shard_map/ppermute | solution.py:83
  67.5 9.4 %collective-permute-start.7 = (f32[10,1280]{1,0:T(8,128)}, f32[10,1280]{1,0:T(8,128)}, u32[]{:S(2)}, u32[]{:S(2)}) collective-permute-start(f32[10,1280]{1,0:T(8,128)} %constant_dynamic-slice_fusion), channel_id=1, source_target_pairs={{0,384},{12,396},{24,408},{36,420},{48,432},{60,444},{72,456},{84,... | collective-permute-start | bytes 153608 | tf_op jit(solution)/shard_map/ppermute | solution.py:83
  78.5 10.6 %collective-permute-start.8 = (f32[10,1280]{1,0:T(8,128)}, f32[10,1280]{1,0:T(8,128)S(1)}, u32[]{:S(2)}, u32[]{:S(2)}) collective-permute-start(f32[10,1280]{1,0:T(8,128)} %dynamic-slice_add_fusion.1), channel_id=1, source_target_pairs={{0,3},{1,2},{2,1},{3,0},{4,7},{5,6},{6,5},{7,4},{8,11},{9,10},{10,... | collective-permute-start | bytes 153608 | tf_op jit(solution)/shard_map/ppermute | solution.py:96
  82.3 6.8 %collective-permute-start.9 = (f32[10,1280]{1,0:T(8,128)}, f32[10,1280]{1,0:T(8,128)}, u32[]{:S(2)}, u32[]{:S(2)}) collective-permute-start(f32[10,1280]{1,0:T(8,128)} %dynamic-slice_add_fusion.1), channel_id=1, source_target_pairs={{0,2},{1,3},{2,0},{3,1},{4,6},{5,7},{6,4},{7,5},{8,10},{9,11},{10,... | collective-permute-start | bytes 153608 | tf_op jit(solution)/shard_map/ppermute | solution.py:96
  84.2 7.1 %collective-permute-start.10 = (f32[10,1280]{1,0:T(8,128)}, f32[10,1280]{1,0:T(8,128)}, u32[]{:S(2)}, u32[]{:S(2)}) collective-permute-start(f32[10,1280]{1,0:T(8,128)} %dynamic-slice_add_fusion.1), channel_id=1, source_target_pairs={{0,1},{1,0},{2,3},{3,2},{4,5},{5,4},{6,7},{7,6},{8,9},{9,8},{10,11... | collective-permute-start | bytes 153608 | tf_op jit(solution)/shard_map/ppermute | solution.py:96
  92.4 18.9 %collective-permute-start.11 = (f32[10,1280]{1,0:T(8,128)S(1)}, f32[10,1280]{1,0:T(8,128)}, u32[]{:S(2)}, u32[]{:S(2)}) collective-permute-start(f32[10,1280]{1,0:T(8,128)S(1)} %select_add_fusion), channel_id=1, source_target_pairs={{0,8},{1,9},{2,10},{3,11},{4,0},{5,1},{6,2},{7,3},{8,4},{9,5},{10,... | collective-permute-start | bytes 153608 | tf_op jit(solution)/shard_map/ppermute | solution.py:111
  104.7 12.8 %collective-permute-start.12 = (f32[10,1280]{1,0:T(8,128)S(1)}, f32[10,1280]{1,0:T(8,128)}, u32[]{:S(2)}, u32[]{:S(2)}) collective-permute-start(f32[10,1280]{1,0:T(8,128)S(1)} %select_add_fusion), channel_id=1, source_target_pairs={{0,4},{1,5},{2,6},{3,7},{4,8},{5,9},{6,10},{7,11},{8,0},{9,1},{10,... | collective-permute-start | bytes 153608 | tf_op jit(solution)/shard_map/ppermute | solution.py:111

commit v5 on v4

--- a/solution.py
+++ b/solution.py
@@ -63,10 +63,18 @@
         axes = [1 + (steps - 1 - bit) for bit in order[1:]]
         halves.append(half.transpose([0] + axes + [steps]))
     arranged = jnp.stack(halves, axis=1).reshape(token_count, width)
-    current = lax.dot_general(
-        arranged, grad_rows, (((0,), (0,)), ((), ())), preferred_element_type=jnp.float32
-    )
-    for even_bits, odd_bits in zip(even_steps, odd_steps):
+
+    def product(index, count):
+        part = width // count
+        picked = lax.dynamic_slice_in_dim(arranged, index * part, part, axis=1)
+        return lax.dot_general(
+            picked, grad_rows, (((0,), (0,)), ((), ())), preferred_element_type=jnp.float32
+        )
+
+    half = (rank & 1).astype(jnp.int32)
+    pairs = [(i, i ^ 1) for i in range(rank_total)]
+    current = product(half, 2) + lax.ppermute(product(1 - half, 2), "row", pairs)
+    for even_bits, odd_bits in zip(even_steps[1:], odd_steps[1:]):
         count = 1 << len(even_bits)
         mine = jnp.zeros((), jnp.int32)
         for k in range(len(even_bits)):

time: 120 us -> 118 us (0.983)
  matrix products: 10.8 us -> 14 us
  local copies, waits for them, and re-layouts: 15.4 us -> 12.4 us
  other arithmetic: 8.33 us -> 6.74 us
    ppermute x0 -> x1, starting transfers between devices: none -> 12.4 us  [reduce_rows(): lax.ppermute(product(1 - half, 2), 'row', pairs)]
    ppermute x8 -> x7, starting transfers between devices: 34.3 us -> 21.9 us  [reduce_rows(): total = total + lax.ppermute(send, 'row', pairs)]
    dynamic_slice x4 -> x3, local copies, waits for them, and re-layouts: 3.63 us -> 0.82 us  [reduce_rows(): lax.dynamic_slice_in_dim(current, (mine ^ delta) * part, part, axis=0)]
    add x4 -> x3, other arithmetic: 3.79 us -> 1.65 us  [reduce_rows(): total = total + lax.ppermute(send, 'row', pairs)]
    dot_general x1 -> x2, matrix products: 2.25 us -> 4.25 us  [product(): lax.dot_general(picked, grad_rows, (((0,), (0,)), ((), ())), preferred_el...]
    dot_general x3, matrix products: 4.42 us -> 5.64 us  [attend(): jnp.einsum('whpq,wqhc->wphc', probs.astype(jnp.float32), value, precision...]
    unnamed x24 -> x32, local copies, waits for them, and re-layouts: 2.97 us -> 3.02 us
    ppermute x8 -> x7, waiting for transfers between devices: 15.6 us -> 15.5 us  [reduce_rows(): total = total + lax.ppermute(send, 'row', pairs)]
  transfers between devices with their start and end apart: 13 -> 13, of which waited for: 6 -> 7; matrix products, arithmetic and copies ran while one was open for 12% -> 13% of each run, Pallas kernels for 0% -> 0%
where the time goes in v5:
time: 118 us
  starting transfers between devices  57.8 us (49%)
  waiting for transfers between devices  24.7 us (21%)
  matrix products  14 us (12%)
  local copies, waits for them, and re-layouts  12.4 us (11%)
  other arithmetic  6.74 us (6%)
  between operations  1.97 us (2%)
    ppermute x7, starting transfers between devices, reduce_rows(): total = total + lax.ppermute(send, 'row', pairs)  21.9 us
    ppermute x7, waiting for transfers between devices, reduce_rows(): total = total + lax.ppermute(send, 'row', pairs)  15.5 us
    ppermute x2, starting transfers between devices, sum_cols(): parts.append(lax.ppermute(share, 'col', pairs))  14.2 us
    ppermute x1, starting transfers between devices, reduce_rows(): lax.ppermute(product(1 - half, 2), 'row', pairs)  12.4 us
    ppermute x3, starting transfers between devices, sum_cols(): lax.ppermute(share, 'col', [(i, i ^ delta) for i in range(col_total)])  9.26 us
    ppermute x2, waiting for transfers between devices, sum_cols(): parts.append(lax.ppermute(share, 'col', pairs))  6.97 us
    dot_general x3, matrix products, attend(): jnp.einsum('whpq,wqhc->wphc', probs.astype(jnp.float32), value, precision...  5.64 us
    dot_general x2, matrix products, product(): lax.dot_general(picked, grad_rows, (((0,), (0,)), ((), ())), preferred_el...  4.25 us
  transfers between devices with their start and end apart: 13, of which 7 were waited for; matrix products, arithmetic and copies ran while one was open for 13% of the time, Pallas kernels for 0%

profile of v5, /device:TPU:1, one launch (start us, length us, event | category | flops | bytes accessed | tf_op | source)
XLA Modules:
  0.0 117.6 jit_solution(15736589605691362146)
XLA Ops:
  0.6 0.0 copy-start
  1.4 3.0 %reshape.78 = bf16[2,64,8,3,80]{4,3,2,1,0:T(4,128)(2,1)S(1)} reshape(bf16[1,128,1920]{2,1,0:T(8,128)(2,1)} %param.4) | data formatting | bytes 983040 | tf_op jit(solution)/shard_map/jvp()/reshape;squeeze | solution.py:15
  4.4 1.1 fusion.36
  5.5 0.3 fusion.37
  5.9 0.1 fusion.8
  6.0 0.4 copy-done.2
  6.3 0.2 copy-done.7
  6.5 1.0 fusion.4
  7.5 1.3 %copy.20 = bf16[2,64,8,80]{1,0,2,3:T(2,128)(2,1)S(1)} copy(bf16[2,64,8,80]{3,1,2,0:T(8,128)(2,1)} %fusion.4) | data formatting | bytes 327680 | tf_op jit(solution)/shard_map/jvp()/convert_element_type | solution.py:31
  8.8 0.2 reshape.74
  9.0 0.1 slice_bitcast_fusion.1
  9.1 0.1 copy.61
  9.2 0.0 copy-start.4
  9.2 0.2 pad_maximum_fusion
  9.4 0.1 copy.23
  9.5 0.7 reshape.75
  10.2 2.4 %fusion.9 = f32[320,1280]{1,0:T(8,128)} fusion(bf16[1,128,1280]{2,1,0:T(8,128)(2,1)S(1)} %copy-done.1, bf16[128,640]{0,1:T(8,128)(2,1)} %reshape.75, s32[]{:T(128)S(6)} %select_n.214), kind=kOutput, calls=%fused_computation.27 | convolution fusion | flops 104857600 | bytes 2048004 | tf_op jit(solution)/shard_map/dot_general | solution.py:70
  12.6 12.4 %collective-permute-start = (f32[320,1280]{1,0:T(8,128)}, f32[320,1280]{1,0:T(8,128)}, u32[]{:S(2)}, u32[]{:S(2)}) collective-permute-start(f32[320,1280]{1,0:T(8,128)} %fusion.9), channel_id=1, source_target_pairs={{0,12},{12,0},{24,36},{36,24},{48,60},{60,48},{72,84},{84,72},{96,... | collective-permute-start | bytes 4915208 | tf_op jit(solution)/shard_map/ppermute | solution.py:76
  25.0 0.2 copy.16
  25.3 0.9 reshape.72
  26.1 0.6 fusion.5
  26.8 1.0 reshape.76
  27.8 3.3 %convert_reduce_fusion = (f32[2,8,64]{2,1,0:T(8,128)}, pred[2,8,64,64]{2,3,1,0:T(32,128)(4,1)}, f32[2,8,64]{2,1,0:T(8,128)S(1)}, f32[2,8,64,64]{2,3,1,0:T(8,128)S(1)}) fusion(f32[2,8,64,64]{2,3,1,0:T(8,128)S(1)} %get-tuple-element.23, f32[2,8,64]{2,1,0:T(8,128)S(1)} %get-tuple-element.22, f32[2,8,64]{2,1,0:T(8,128)S(1)} %get-tuple-element.22, ...), kind=kOutput, calls=%fused_computation.20 | convolution fusion | flops 63584256 | bytes 1101952 | tf_op jit(solution)/shard_map/transpose(jvp(whpq,wqhc->wphc))/dot_general | solution.py:27
  31.1 0.2 fusion.35
  31.3 0.6 negate_bitcast_fusion
  31.9 0.0 collective-permute-done
  31.9 1.8 %convolution_add_fusion = f32[320,1280]{1,0:T(8,128)S(1)} fusion(f32[320,1280]{1,0:T(8,128)} %collective-permute-done, bf16[1,128,1280]{2,1,0:T(8,128)(2,1)S(1)} %copy-done.1, bf16[128,640]{0,1:T(8,128)(2,1)} %reshape.75, s32[]{:T(128)S(6)} %select_n.213), kind=kOutput, calls=%fused_computation | convolution fusion | flops 105267200 | bytes 3686404 | tf_op jit(solution)/shard_map/dot_general | solution.py:70
  33.8 0.1 constant_dynamic-slice_fusion.6
  33.9 0.0 copy-start.10
  33.9 2.1 %collective-permute-start.3 = (f32[80,1280]{1,0:T(8,128)S(1)}, f32[80,1280]{1,0:T(8,128)S(1)}, u32[]{:S(2)}, u32[]{:S(2)}) collective-permute-start(f32[80,1280]{1,0:T(8,128)S(1)} %get-tuple-element.11), channel_id=1, source_target_pairs={{0,72},{12,300},{24,48},{36,324},{48,24},{60,348},{72,0},{84,372},... | collective-permute-start | bytes 1228808 | tf_op jit(solution)/shard_map/ppermute | solution.py:91
  36.0 1.9 %collective-permute-start.2 = (f32[80,1280]{1,0:T(8,128)S(1)}, f32[80,1280]{1,0:T(8,128)S(1)}, u32[]{:S(2)}, u32[]{:S(2)}) collective-permute-start(f32[80,1280]{1,0:T(8,128)S(1)} %get-tuple-element.12), channel_id=1, source_target_pairs={{0,24},{12,108},{24,0},{36,132},{48,72},{60,156},{72,48},{84,180},... | collective-permute-start | bytes 1228808 | tf_op jit(solution)/shard_map/ppermute | solution.py:91
  37.9 5.4 %collective-permute-start.1 = (f32[80,1280]{1,0:T(8,128)S(1)}, f32[80,1280]{1,0:T(8,128)S(1)}, u32[]{:S(2)}, u32[]{:S(2)}) collective-permute-start(f32[80,1280]{1,0:T(8,128)S(1)} %get-tuple-element.10), channel_id=1, source_target_pairs={{0,48},{12,204},{24,72},{36,228},{48,0},{60,252},{72,24},{84,276},... | collective-permute-start | bytes 1228808 | tf_op jit(solution)/shard_map/ppermute | solution.py:91
  43.4 1.3 %convolution_bitcast_fusion.2 = f32[2,64,8,1,80]{4,1,2,0,3:T(8,128)} fusion(f32[2,64,8,80]{3,2,1,0:T(8,128)S(1)} %copy-done.6, pred[2,64]{1,0:T(4,128)(4,1)S(1)} %copy-done.13, f32[2,8,64,64]{2,3,1,0:T(8,128)S(1)} %get-tuple-element.23, f32[2,8,64]{2,1,0:T(8,128)S(1)} %fusion.8, f32[2,8,64]{2,1,0:T(8,128)S(1)} %get-tuple-element.22), kind=kOutput, calls=%fused_computation.6 | convolution fusion | flops 63193088 | bytes 925824 | tf_op jit(solution)/shard_map/transpose(jvp(whpq,wqhc->wphc))/dot_general | solution.py:27
  44.7 8.6 %collective-permute-done.2 = f32[80,1280]{1,0:T(8,128)S(1)} collective-permute-done((f32[80,1280]{1,0:T(8,128)S(1)}, f32[80,1280]{1,0:T(8,128)S(1)}, u32[]{:S(2)}, u32[]{:S(2)}) %collective-permute-start.2) | collective-permute-done | bytes 409632 | tf_op jit(solution)/shard_map/ppermute | solution.py:91
  53.3 0.0 collective-permute-done.1
  53.3 0.1 add_add_fusion
  53.4 0.1 constant_dynamic-slice_fusion.3
  53.5 2.1 %collective-permute-start.6 = (f32[20,1280]{1,0:T(8,128)S(1)}, f32[20,1280]{1,0:T(8,128)S(1)}, u32[]{:S(2)}, u32[]{:S(2)}) collective-permute-start(f32[20,1280]{1,0:T(8,128)S(1)} %get-tuple-element.18), channel_id=1, source_target_pairs={{0,288},{12,84},{24,312},{36,60},{48,336},{60,36},{72,360},{84,12}... | collective-permute-start | bytes 307208 | tf_op jit(solution)/shard_map/ppermute | solution.py:91
  55.5 1.9 %collective-permute-start.5 = (f32[20,1280]{1,0:T(8,128)S(1)}, f32[20,1280]{1,0:T(8,128)S(1)}, u32[]{:S(2)}, u32[]{:S(2)}) collective-permute-start(f32[20,1280]{1,0:T(8,128)S(1)} %get-tuple-element.19), channel_id=1, source_target_pairs={{0,96},{12,36},{24,120},{36,12},{48,144},{60,84},{72,168},{84,60},... | collective-permute-start | bytes 307208 | tf_op jit(solution)/shard_map/ppermute | solution.py:91
  57.5 5.7 %collective-permute-start.4 = (f32[20,1280]{1,0:T(8,128)S(1)}, f32[20,1280]{1,0:T(8,128)S(1)}, u32[]{:S(2)}, u32[]{:S(2)}) collective-permute-start(f32[20,1280]{1,0:T(8,128)S(1)} %get-tuple-element.17), channel_id=1, source_target_pairs={{0,192},{12,60},{24,216},{36,84},{48,240},{60,12},{72,264},{84,36}... | collective-permute-start | bytes 307208 | tf_op jit(solution)/shard_map/ppermute | solution.py:91
  63.2 1.2 fusion
  64.4 0.0 collective-permute-done.6
  64.4 0.0 collective-permute-done.5
  64.4 1.1 collective-permute-done.4
  65.5 0.7 constant_dynamic-slice_fusion
  66.2 2.8 %collective-permute-start.7 = (f32[10,1280]{1,0:T(8,128)}, f32[10,1280]{1,0:T(8,128)}, u32[]{:S(2)}, u32[]{:S(2)}) collective-permute-start(f32[10,1280]{1,0:T(8,128)} %constant_dynamic-slice_fusion), channel_id=1, source_target_pairs={{0,384},{12,396},{24,408},{36,420},{48,432},{60,444},{72,456},{84,... | collective-permute-start | bytes 153608 | tf_op jit(solution)/shard_map/ppermute | solution.py:91
  69.0 0.7 convolution_bitcast_fusion
  69.7 5.9 %collective-permute-done.7 = f32[10,1280]{1,0:T(8,128)} collective-permute-done((f32[10,1280]{1,0:T(8,128)}, f32[10,1280]{1,0:T(8,128)}, u32[]{:S(2)}, u32[]{:S(2)}) %collective-permute-start.7) | collective-permute-done | bytes 51232 | tf_op jit(solution)/shard_map/ppermute | solution.py:91
  75.6 1.5 %dynamic-slice_add_fusion = f32[10,1280]{1,0:T(8,128)} fusion(f32[10,1280]{1,0:T(8,128)} %collective-permute-done.7, f32[20,1280]{1,0:T(8,128)S(1)} %add_add_fusion.1, s32[]{:T(128)S(6)} %select_n.227), kind=kLoop, calls=%fused_computation.54 | loop fusion | flops 12800 | bytes 153604 | tf_op jit(solution)/shard_map/add | solution.py:91
  77.1 3.8 %collective-permute-start.8 = (f32[10,1280]{1,0:T(8,128)}, f32[10,1280]{1,0:T(8,128)S(1)}, u32[]{:S(2)}, u32[]{:S(2)}) collective-permute-start(f32[10,1280]{1,0:T(8,128)} %dynamic-slice_add_fusion), channel_id=1, source_target_pairs={{0,3},{1,2},{2,1},{3,0},{4,7},{5,6},{6,5},{7,4},{8,11},{9,10},{10,... | collective-permute-start | bytes 153608 | tf_op jit(solution)/shard_map/ppermute | solution.py:104
  80.9 1.9 %collective-permute-start.9 = (f32[10,1280]{1,0:T(8,128)}, f32[10,1280]{1,0:T(8,128)S(1)}, u32[]{:S(2)}, u32[]{:S(2)}) collective-permute-start(f32[10,1280]{1,0:T(8,128)} %dynamic-slice_add_fusion), channel_id=1, source_target_pairs={{0,2},{1,3},{2,0},{3,1},{4,6},{5,7},{6,4},{7,5},{8,10},{9,11},{10,... | collective-permute-start | bytes 153608 | tf_op jit(solution)/shard_map/ppermute | solution.py:104
  82.9 3.5 %collective-permute-start.10 = (f32[10,1280]{1,0:T(8,128)}, f32[10,1280]{1,0:T(8,128)}, u32[]{:S(2)}, u32[]{:S(2)}) collective-permute-start(f32[10,1280]{1,0:T(8,128)} %dynamic-slice_add_fusion), channel_id=1, source_target_pairs={{0,1},{1,0},{2,3},{3,2},{4,5},{5,4},{6,7},{7,6},{8,9},{9,8},{10,11... | collective-permute-start | bytes 153608 | tf_op jit(solution)/shard_map/ppermute | solution.py:104
  86.4 1.3 %convolution_bitcast_fusion.1 = f32[2,64,8,1,80]{4,1,2,0,3:T(8,128)} fusion(f32[2,8,64,64]{2,3,1,0:T(8,128)S(1)} %get-tuple-element.7, pred[2,8,64,64]{2,3,1,0:T(32,128)(4,1)S(1)} %copy-done.8, f32[2,8,64]{2,1,0:T(8,128)S(1)} %bitcast_divide_fusion, pred[2,64]{1,0:T(4,128)(4,1)S(1)} %copy-done.14, bf16[2,64,8,1,80]{4,3,2,1,0:T(2,128)(2,1)S(1)} %get-tuple-element.14), kind=kOutput, calls=%fused_computation.5 | convolution fusion | flops 63176704 | bytes 823424 | tf_op jit(solution)/shard_map/transpose(jvp(wphc,wqhc->whpq))/dot_general | solution.py:21
  87.7 0.6 collective-permute-done.9
  88.3 1.7 %collective-permute-done.10 = f32[10,1280]{1,0:T(8,128)} collective-permute-done((f32[10,1280]{1,0:T(8,128)}, f32[10,1280]{1,0:T(8,128)}, u32[]{:S(2)}, u32[]{:S(2)}) %collective-permute-start.10) | collective-permute-done | bytes 51232 | tf_op jit(solution)/shard_map/ppermute | solution.py:104
  90.0 1.0 select_add_fusion
  90.9 12.3 %collective-permute-start.11 = (f32[10,1280]{1,0:T(8,128)S(1)}, f32[10,1280]{1,0:T(8,128)}, u32[]{:S(2)}, u32[]{:S(2)}) collective-permute-start(f32[10,1280]{1,0:T(8,128)S(1)} %select_add_fusion), channel_id=1, source_target_pairs={{0,8},{1,9},{2,10},{3,11},{4,0},{5,1},{6,2},{7,3},{8,4},{9,5},{10,... | collective-permute-start | bytes 153608 | tf_op jit(solution)/shard_map/ppermute | solution.py:119
  103.3 1.9 %collective-permute-start.12 = (f32[10,1280]{1,0:T(8,128)S(1)}, f32[10,1280]{1,0:T(8,128)}, u32[]{:S(2)}, u32[]{:S(2)}) collective-permute-start(f32[10,1280]{1,0:T(8,128)S(1)} %select_add_fusion), channel_id=1, source_target_pairs={{0,4},{1,5},{2,6},{3,7},{4,8},{5,9},{6,10},{7,11},{8,0},{9,1},{10,... | collective-permute-start | bytes 153608 | tf_op jit(solution)/shard_map/ppermute | solution.py:119
  105.2 1.4 %add_convert_fusion = bf16[2,64,8,3,80]{4,1,2,0,3:T(8,128)(2,1)S(1)} fusion(f32[2,64,8,1,80]{4,1,2,0,3:T(8,128)S(1)} %convolution_bitcast_fusion, f32[2,64,8,1,80]{4,1,2,0,3:T(8,128)} %convolution_bitcast_fusion.1, f32[2,64,8,1,80]{4,1,2,0,3:T(8,128)} %convolution_bitcast_fusion.2), kind=kLoop, calls=%fused_computation.3 | loop fusion | flops 737280 | bytes 1474560 | tf_op jit(solution)/shard_map/transpose(jvp())/convert_element_type | solution.py:15
  106.6 0.7 copy.27
  107.3 1.7 %reshape.77 = bf16[1,128,1920]{2,1,0:T(8,128)(2,1)} reshape(bf16[2,64,8,3,80]{4,3,2,1,0:T(4,128)(2,1)S(1)} %copy.27) | data formatting | bytes 983040
  109.1 0.8 collective-permute-done.11
  109.8 6.2 %collective-permute-done.12 = f32[10,1280]{1,0:T(8,128)} collective-permute-done((f32[10,1280]{1,0:T(8,128)S(1)}, f32[10,1280]{1,0:T(8,128)}, u32[]{:S(2)}, u32[]{:S(2)}) %collective-permute-start.12) | collective-permute-done | bytes 51232 | tf_op jit(solution)/shard_map/ppermute | solution.py:119
  116.0 1.6 %add_multiply_fusion.1 = f32[10,1280]{1,0:T(8,128)} fusion(f32[10,1280]{1,0:T(8,128)} %collective-permute-done.11, f32[10,1280]{1,0:T(8,128)} %collective-permute-done.12, f32[10,1280]{1,0:T(8,128)S(1)} %select_add_fusion, pred[]{:T(512)S(6)} %eq.93, pred[]{:T(512)S(6)} %eq.92, pred[]{:T(512)S(6)} %eq.91, pred[]{:T(512)S(6)} %eq.90, pred[]{:T(512)S(6)} %eq.89, ...), kind=kLoop, calls=%fused_computation.52 | loop fusion | flops 115200 | bytes 204806 | tf_op jit(solution)/shard_map/mul | solution.py:144
  (32 shorter events, 0.1 us)
Async XLA Ops:
  0.6 25.5 %copy-start = (bf16[640,1280]{1,0:T(8,128)(2,1)S(1)}, bf16[640,1280]{1,0:T(8,128)(2,1)}, u32[]{:S(2)}) copy-start(bf16[640,1280]{1,0:T(8,128)(2,1)} %param.6) | copy-start | bytes 4915204
  1.4 4.5 %copy-start.11 = (pred[2,64]{1,0:T(4,128)(4,1)}, pred[2,64]{1,0:T(4,128)(4,1)S(1)}, u32[]{:S(2)}) copy-start(pred[2,64]{1,0:T(4,128)(4,1)S(1)} %add_compare_fusion) | copy-start | bytes 388
  5.5 0.8 copy-start.2
  5.5 1.0 copy-start.7
  7.5 2.7 %copy-start.1 = (bf16[1,128,1280]{2,1,0:T(8,128)(2,1)S(1)}, bf16[1,128,1280]{2,1,0:T(8,128)(2,1)}, u32[]{:S(2)}) copy-start(bf16[1,128,1280]{2,1,0:T(8,128)(2,1)} %param.5) | copy-start | bytes 983044
  9.2 15.8 %copy-start.4 = (bf16[2,64,8,80]{3,1,2,0:T(8,128)(2,1)S(1)}, bf16[2,64,8,80]{3,1,2,0:T(8,128)(2,1)}, u32[]{:S(2)}) copy-start(bf16[2,64,8,80]{3,1,2,0:T(8,128)(2,1)} %fusion.4) | copy-start | bytes 491524
  12.6 19.3 %collective-permute-start = (f32[320,1280]{1,0:T(8,128)}, f32[320,1280]{1,0:T(8,128)}, u32[]{:S(2)}, u32[]{:S(2)}) collective-permute-start(f32[320,1280]{1,0:T(8,128)} %fusion.9), channel_id=1, source_target_pairs={{0,12},{12,0},{24,36},{36,24},{48,60},{60,48},{72,84},{84,72},{96,... | collective-permute-start | bytes 4915208 | tf_op jit(solution)/shard_map/ppermute | solution.py:76
  26.1 1.7 %copy-start.12 = (pred[2,64]{1,0:T(4,128)(4,1)S(1)}, pred[2,64]{1,0:T(4,128)(4,1)}, u32[]{:S(2)}) copy-start(pred[2,64]{1,0:T(4,128)(4,1)} %copy-done.11) | copy-start | bytes 388
  33.8 9.6 %copy-start.6 = (f32[2,64,8,80]{3,2,1,0:T(8,128)S(1)}, f32[2,64,8,80]{3,2,1,0:T(8,128)}, u32[]{:S(2)}) copy-start(f32[2,64,8,80]{3,2,1,0:T(8,128)} %reshape.76) | copy-start | bytes 983044
  33.8 9.6 %copy-start.13 = (pred[2,64]{1,0:T(4,128)(4,1)S(1)}, pred[2,64]{1,0:T(4,128)(4,1)}, u32[]{:S(2)}) copy-start(pred[2,64]{1,0:T(4,128)(4,1)} %copy-done.11) | copy-start | bytes 388
  33.9 10.8 %copy-start.9 = (f32[2,8,64,1]{2,1,0,3:T(8,128)S(1)}, f32[2,8,64,1]{2,1,0,3:T(8,128)}, u32[]{:S(2)}) copy-start(f32[2,8,64,1]{2,1,0,3:T(8,128)} %negate_bitcast_fusion) | copy-start | bytes 12292
  33.9 10.8 %copy-start.10 = (f32[2,8,64]{2,1,0:T(8,128)S(1)}, f32[2,8,64]{2,1,0:T(8,128)}, u32[]{:S(2)}) copy-start(f32[2,8,64]{2,1,0:T(8,128)} %get-tuple-element.8) | copy-start | bytes 12292
  33.9 10.8 %collective-permute-start.3 = (f32[80,1280]{1,0:T(8,128)S(1)}, f32[80,1280]{1,0:T(8,128)S(1)}, u32[]{:S(2)}, u32[]{:S(2)}) collective-permute-start(f32[80,1280]{1,0:T(8,128)S(1)} %get-tuple-element.11), channel_id=1, source_target_pairs={{0,72},{12,300},{24,48},{36,324},{48,24},{60,348},{72,0},{84,372},... | collective-permute-start | bytes 1228808 | tf_op jit(solution)/shard_map/ppermute | solution.py:91
  36.0 17.3 %collective-permute-start.2 = (f32[80,1280]{1,0:T(8,128)S(1)}, f32[80,1280]{1,0:T(8,128)S(1)}, u32[]{:S(2)}, u32[]{:S(2)}) collective-permute-start(f32[80,1280]{1,0:T(8,128)S(1)} %get-tuple-element.12), channel_id=1, source_target_pairs={{0,24},{12,108},{24,0},{36,132},{48,72},{60,156},{72,48},{84,180},... | collective-permute-start | bytes 1228808 | tf_op jit(solution)/shard_map/ppermute | solution.py:91
  37.9 15.4 %collective-permute-start.1 = (f32[80,1280]{1,0:T(8,128)S(1)}, f32[80,1280]{1,0:T(8,128)S(1)}, u32[]{:S(2)}, u32[]{:S(2)}) collective-permute-start(f32[80,1280]{1,0:T(8,128)S(1)} %get-tuple-element.10), channel_id=1, source_target_pairs={{0,48},{12,204},{24,72},{36,228},{48,0},{60,252},{72,24},{84,276},... | collective-permute-start | bytes 1228808 | tf_op jit(solution)/shard_map/ppermute | solution.py:91
  44.7 18.5 %copy-start.5 = (bf16[128,640]{1,0:T(8,128)(2,1)S(1)}, bf16[128,640]{1,0:T(8,128)(2,1)}, u32[]{:S(2)}) copy-start(bf16[128,640]{1,0:T(8,128)(2,1)} %reshape.72) | copy-start | bytes 491524
  53.5 15.5 %copy-start.3 = (bf16[2,64,8,1,80]{4,3,2,1,0:T(2,128)(2,1)S(1)}, bf16[2,64,8,1,80]{4,3,2,1,0:T(2,128)(2,1)}, u32[]{:S(2)}) copy-start(bf16[2,64,8,1,80]{4,3,2,1,0:T(2,128)(2,1)} %copy-done.2) | copy-start | bytes 491524
  53.5 15.5 %copy-start.8 = (pred[2,8,64,64]{2,3,1,0:T(32,128)(4,1)S(1)}, pred[2,8,64,64]{2,3,1,0:T(32,128)(4,1)}, u32[]{:S(2)}) copy-start(pred[2,8,64,64]{2,3,1,0:T(32,128)(4,1)} %get-tuple-element.9) | copy-start | bytes 196612
  53.5 10.9 %collective-permute-start.6 = (f32[20,1280]{1,0:T(8,128)S(1)}, f32[20,1280]{1,0:T(8,128)S(1)}, u32[]{:S(2)}, u32[]{:S(2)}) collective-permute-start(f32[20,1280]{1,0:T(8,128)S(1)} %get-tuple-element.18), channel_id=1, source_target_pairs={{0,288},{12,84},{24,312},{36,60},{48,336},{60,36},{72,360},{84,12}... | collective-permute-start | bytes 307208 | tf_op jit(solution)/shard_map/ppermute | solution.py:91
  55.5 8.9 %collective-permute-start.5 = (f32[20,1280]{1,0:T(8,128)S(1)}, f32[20,1280]{1,0:T(8,128)S(1)}, u32[]{:S(2)}, u32[]{:S(2)}) collective-permute-start(f32[20,1280]{1,0:T(8,128)S(1)} %get-tuple-element.19), channel_id=1, source_target_pairs={{0,96},{12,36},{24,120},{36,12},{48,144},{60,84},{72,168},{84,60},... | collective-permute-start | bytes 307208 | tf_op jit(solution)/shard_map/ppermute | solution.py:91
  57.5 8.0 %collective-permute-start.4 = (f32[20,1280]{1,0:T(8,128)S(1)}, f32[20,1280]{1,0:T(8,128)S(1)}, u32[]{:S(2)}, u32[]{:S(2)}) collective-permute-start(f32[20,1280]{1,0:T(8,128)S(1)} %get-tuple-element.17), channel_id=1, source_target_pairs={{0,192},{12,60},{24,216},{36,84},{48,240},{60,12},{72,264},{84,36}... | collective-permute-start | bytes 307208 | tf_op jit(solution)/shard_map/ppermute | solution.py:91
  64.4 22.0 %copy-start.14 = (pred[2,64]{1,0:T(4,128)(4,1)S(1)}, pred[2,64]{1,0:T(4,128)(4,1)}, u32[]{:S(2)}) copy-start(pred[2,64]{1,0:T(4,128)(4,1)} %copy-done.11) | copy-start | bytes 388
  66.2 9.4 %collective-permute-start.7 = (f32[10,1280]{1,0:T(8,128)}, f32[10,1280]{1,0:T(8,128)}, u32[]{:S(2)}, u32[]{:S(2)}) collective-permute-start(f32[10,1280]{1,0:T(8,128)} %constant_dynamic-slice_fusion), channel_id=1, source_target_pairs={{0,384},{12,396},{24,408},{36,420},{48,432},{60,444},{72,456},{84,... | collective-permute-start | bytes 153608 | tf_op jit(solution)/shard_map/ppermute | solution.py:91
  77.1 10.6 %collective-permute-start.8 = (f32[10,1280]{1,0:T(8,128)}, f32[10,1280]{1,0:T(8,128)S(1)}, u32[]{:S(2)}, u32[]{:S(2)}) collective-permute-start(f32[10,1280]{1,0:T(8,128)} %dynamic-slice_add_fusion), channel_id=1, source_target_pairs={{0,3},{1,2},{2,1},{3,0},{4,7},{5,6},{6,5},{7,4},{8,11},{9,10},{10,... | collective-permute-start | bytes 153608 | tf_op jit(solution)/shard_map/ppermute | solution.py:104
  80.9 7.4 %collective-permute-start.9 = (f32[10,1280]{1,0:T(8,128)}, f32[10,1280]{1,0:T(8,128)S(1)}, u32[]{:S(2)}, u32[]{:S(2)}) collective-permute-start(f32[10,1280]{1,0:T(8,128)} %dynamic-slice_add_fusion), channel_id=1, source_target_pairs={{0,2},{1,3},{2,0},{3,1},{4,6},{5,7},{6,4},{7,5},{8,10},{9,11},{10,... | collective-permute-start | bytes 153608 | tf_op jit(solution)/shard_map/ppermute | solution.py:104
  82.9 7.1 %collective-permute-start.10 = (f32[10,1280]{1,0:T(8,128)}, f32[10,1280]{1,0:T(8,128)}, u32[]{:S(2)}, u32[]{:S(2)}) collective-permute-start(f32[10,1280]{1,0:T(8,128)} %dynamic-slice_add_fusion), channel_id=1, source_target_pairs={{0,1},{1,0},{2,3},{3,2},{4,5},{5,4},{6,7},{7,6},{8,9},{9,8},{10,11... | collective-permute-start | bytes 153608 | tf_op jit(solution)/shard_map/ppermute | solution.py:104
  90.9 18.9 %collective-permute-start.11 = (f32[10,1280]{1,0:T(8,128)S(1)}, f32[10,1280]{1,0:T(8,128)}, u32[]{:S(2)}, u32[]{:S(2)}) collective-permute-start(f32[10,1280]{1,0:T(8,128)S(1)} %select_add_fusion), channel_id=1, source_target_pairs={{0,8},{1,9},{2,10},{3,11},{4,0},{5,1},{6,2},{7,3},{8,4},{9,5},{10,... | collective-permute-start | bytes 153608 | tf_op jit(solution)/shard_map/ppermute | solution.py:119
  103.3 12.8 %collective-permute-start.12 = (f32[10,1280]{1,0:T(8,128)S(1)}, f32[10,1280]{1,0:T(8,128)}, u32[]{:S(2)}, u32[]{:S(2)}) collective-permute-start(f32[10,1280]{1,0:T(8,128)S(1)} %select_add_fusion), channel_id=1, source_target_pairs={{0,4},{1,5},{2,6},{3,7},{4,8},{5,9},{6,10},{7,11},{8,0},{9,1},{10,... | collective-permute-start | bytes 153608 | tf_op jit(solution)/shard_map/ppermute | solution.py:119

commit v6 on v5

--- a/solution.py
+++ b/solution.py
@@ -33,8 +33,8 @@
 
 def bit_steps(steps):
     low = [tuple(range(1, min(3, steps)))] if steps > 1 else []
-    high = [tuple(range(3, min(5, steps)))] if steps > 3 else []
-    rest = [(bit,) for bit in range(5, steps)]
+    high = [tuple(range(4, min(6, steps)))] if steps > 4 else []
+    rest = [(bit,) for bit in range(3, steps) if bit not in sum(high, ())]
     return [(0,)] + low + high + rest, [(0,)] + high + low + rest
 
 

time: 118 us -> 121 us (1.025)
  starting transfers between devices: 57.8 us -> 59.1 us
    ppermute x7, starting transfers between devices: 21.9 us -> 23.1 us  [reduce_rows(): total = total + lax.ppermute(send, 'row', pairs)]
where the time goes in v6:
time: 121 us; the launch traced here: 120 us
  starting transfers between devices  59.1 us (49%)
  waiting for transfers between devices  25.7 us (21%)
  matrix products  14 us (12%)
  local copies, waits for them, and re-layouts  12.4 us (10%)
  other arithmetic  6.74 us (6%)
  between operations  1.97 us (2%)
    ppermute x7, starting transfers between devices, reduce_rows(): total = total + lax.ppermute(send, 'row', pairs)  23.1 us
    ppermute x7, waiting for transfers between devices, reduce_rows(): total = total + lax.ppermute(send, 'row', pairs)  15.7 us
    ppermute x2, starting transfers between devices, sum_cols(): parts.append(lax.ppermute(share, 'col', pairs))  14.3 us
    ppermute x1, starting transfers between devices, reduce_rows(): lax.ppermute(product(1 - half, 2), 'row', pairs)  12.4 us
    ppermute x3, starting transfers between devices, sum_cols(): lax.ppermute(share, 'col', [(i, i ^ delta) for i in range(col_total)])  9.26 us
    ppermute x2, waiting for transfers between devices, sum_cols(): parts.append(lax.ppermute(share, 'col', pairs))  6.7 us
    dot_general x3, matrix products, attend(): jnp.einsum('whpq,wqhc->wphc', probs.astype(jnp.float32), value, precision...  5.64 us
    dot_general x2, matrix products, product(): lax.dot_general(picked, grad_rows, (((0,), (0,)), ((), ())), preferred_el...  4.26 us
  transfers between devices with their start and end apart: 13, of which 7 were waited for; matrix products, arithmetic and copies ran while one was open for 13% of the time, Pallas kernels for 0%

profile of v6, /device:TPU:1, one launch (start us, length us, event | category | flops | bytes accessed | tf_op | source)
XLA Modules:
  0.0 120.0 jit_solution(15685098957150773755)
XLA Ops:
  0.6 0.0 copy-start
  1.4 3.0 %reshape.78 = bf16[2,64,8,3,80]{4,3,2,1,0:T(4,128)(2,1)S(1)} reshape(bf16[1,128,1920]{2,1,0:T(8,128)(2,1)} %param.4) | data formatting | bytes 983040 | tf_op jit(solution)/shard_map/jvp()/reshape;squeeze | solution.py:15
  4.4 1.1 fusion.36
  5.5 0.3 fusion.37
  5.9 0.1 fusion.8
  6.0 0.4 copy-done.2
  6.3 0.2 copy-done.7
  6.5 1.0 fusion.4
  7.5 1.3 %copy.20 = bf16[2,64,8,80]{1,0,2,3:T(2,128)(2,1)S(1)} copy(bf16[2,64,8,80]{3,1,2,0:T(8,128)(2,1)} %fusion.4) | data formatting | bytes 327680 | tf_op jit(solution)/shard_map/jvp()/convert_element_type | solution.py:31
  8.8 0.2 reshape.74
  9.0 0.1 slice_bitcast_fusion.1
  9.1 0.1 copy.61
  9.2 0.0 copy-start.4
  9.2 0.2 pad_maximum_fusion
  9.4 0.1 copy.23
  9.5 0.7 reshape.75
  10.2 2.4 %fusion.9 = f32[320,1280]{1,0:T(8,128)} fusion(bf16[1,128,1280]{2,1,0:T(8,128)(2,1)S(1)} %copy-done.1, bf16[128,640]{0,1:T(8,128)(2,1)} %reshape.75, s32[]{:T(128)S(6)} %select_n.214), kind=kOutput, calls=%fused_computation.27 | convolution fusion | flops 104857600 | bytes 2048004 | tf_op jit(solution)/shard_map/dot_general | solution.py:70
  12.6 12.4 %collective-permute-start = (f32[320,1280]{1,0:T(8,128)}, f32[320,1280]{1,0:T(8,128)}, u32[]{:S(2)}, u32[]{:S(2)}) collective-permute-start(f32[320,1280]{1,0:T(8,128)} %fusion.9), channel_id=1, source_target_pairs={{0,12},{12,0},{24,36},{36,24},{48,60},{60,48},{72,84},{84,72},{96,... | collective-permute-start | bytes 4915208 | tf_op jit(solution)/shard_map/ppermute | solution.py:76
  25.0 0.2 copy.16
  25.3 0.9 reshape.72
  26.1 0.6 fusion.5
  26.8 1.0 reshape.76
  27.8 3.3 %convert_reduce_fusion = (f32[2,8,64]{2,1,0:T(8,128)}, pred[2,8,64,64]{2,3,1,0:T(32,128)(4,1)}, f32[2,8,64]{2,1,0:T(8,128)S(1)}, f32[2,8,64,64]{2,3,1,0:T(8,128)S(1)}) fusion(f32[2,8,64,64]{2,3,1,0:T(8,128)S(1)} %get-tuple-element.23, f32[2,8,64]{2,1,0:T(8,128)S(1)} %get-tuple-element.22, f32[2,8,64]{2,1,0:T(8,128)S(1)} %get-tuple-element.22, ...), kind=kOutput, calls=%fused_computation.20 | convolution fusion | flops 63584256 | bytes 1101952 | tf_op jit(solution)/shard_map/transpose(jvp(whpq,wqhc->wphc))/dot_general | solution.py:27
  31.1 0.2 fusion.35
  31.3 0.6 negate_bitcast_fusion
  31.9 0.0 collective-permute-done
  31.9 1.8 %convolution_add_fusion = f32[320,1280]{1,0:T(8,128)S(1)} fusion(f32[320,1280]{1,0:T(8,128)} %collective-permute-done, bf16[1,128,1280]{2,1,0:T(8,128)(2,1)S(1)} %copy-done.1, bf16[128,640]{0,1:T(8,128)(2,1)} %reshape.75, s32[]{:T(128)S(6)} %select_n.213), kind=kOutput, calls=%fused_computation | convolution fusion | flops 105267200 | bytes 3686404 | tf_op jit(solution)/shard_map/dot_general | solution.py:70
  33.8 0.1 constant_dynamic-slice_fusion.6
  33.9 0.0 copy-start.10
  33.9 2.1 %collective-permute-start.3 = (f32[80,1280]{1,0:T(8,128)S(1)}, f32[80,1280]{1,0:T(8,128)S(1)}, u32[]{:S(2)}, u32[]{:S(2)}) collective-permute-start(f32[80,1280]{1,0:T(8,128)S(1)} %get-tuple-element.11), channel_id=1, source_target_pairs={{0,72},{12,588},{24,48},{36,612},{48,24},{60,636},{72,0},{84,660},... | collective-permute-start | bytes 1228808 | tf_op jit(solution)/shard_map/ppermute | solution.py:91
  36.0 1.9 %collective-permute-start.2 = (f32[80,1280]{1,0:T(8,128)S(1)}, f32[80,1280]{1,0:T(8,128)S(1)}, u32[]{:S(2)}, u32[]{:S(2)}) collective-permute-start(f32[80,1280]{1,0:T(8,128)S(1)} %get-tuple-element.12), channel_id=1, source_target_pairs={{0,24},{12,204},{24,0},{36,228},{48,72},{60,252},{72,48},{84,276},... | collective-permute-start | bytes 1228808 | tf_op jit(solution)/shard_map/ppermute | solution.py:91
  37.9 7.5 %collective-permute-start.1 = (f32[80,1280]{1,0:T(8,128)S(1)}, f32[80,1280]{1,0:T(8,128)S(1)}, u32[]{:S(2)}, u32[]{:S(2)}) collective-permute-start(f32[80,1280]{1,0:T(8,128)S(1)} %get-tuple-element.10), channel_id=1, source_target_pairs={{0,48},{12,396},{24,72},{36,420},{48,0},{60,444},{72,24},{84,468},... | collective-permute-start | bytes 1228808 | tf_op jit(solution)/shard_map/ppermute | solution.py:91
  45.5 1.3 %convolution_bitcast_fusion.2 = f32[2,64,8,1,80]{4,1,2,0,3:T(8,128)} fusion(f32[2,64,8,80]{3,2,1,0:T(8,128)S(1)} %copy-done.6, pred[2,64]{1,0:T(4,128)(4,1)S(1)} %copy-done.13, f32[2,8,64,64]{2,3,1,0:T(8,128)S(1)} %get-tuple-element.23, f32[2,8,64]{2,1,0:T(8,128)S(1)} %fusion.8, f32[2,8,64]{2,1,0:T(8,128)S(1)} %get-tuple-element.22), kind=kOutput, calls=%fused_computation.6 | convolution fusion | flops 63193088 | bytes 925824 | tf_op jit(solution)/shard_map/transpose(jvp(whpq,wqhc->wphc))/dot_general | solution.py:27
  46.8 0.0 collective-permute-done.3
  46.8 9.2 %collective-permute-done.2 = f32[80,1280]{1,0:T(8,128)S(1)} collective-permute-done((f32[80,1280]{1,0:T(8,128)S(1)}, f32[80,1280]{1,0:T(8,128)S(1)}, u32[]{:S(2)}, u32[]{:S(2)}) %collective-permute-start.2) | collective-permute-done | bytes 409632 | tf_op jit(solution)/shard_map/ppermute | solution.py:91
  56.0 2.6 %collective-permute-done.1 = f32[80,1280]{1,0:T(8,128)S(1)} collective-permute-done((f32[80,1280]{1,0:T(8,128)S(1)}, f32[80,1280]{1,0:T(8,128)S(1)}, u32[]{:S(2)}, u32[]{:S(2)}) %collective-permute-start.1) | collective-permute-done | bytes 409632 | tf_op jit(solution)/shard_map/ppermute | solution.py:91
  58.6 0.1 add_add_fusion
  58.7 0.1 constant_dynamic-slice_fusion.3
  58.8 2.1 %collective-permute-start.6 = (f32[20,1280]{1,0:T(8,128)S(1)}, f32[20,1280]{1,0:T(8,128)S(1)}, u32[]{:S(2)}, u32[]{:S(2)}) collective-permute-start(f32[20,1280]{1,0:T(8,128)S(1)} %get-tuple-element.18), channel_id=1, source_target_pairs={{0,576},{12,84},{24,600},{36,60},{48,624},{60,36},{72,648},{84,12}... | collective-permute-start | bytes 307208 | tf_op jit(solution)/shard_map/ppermute | solution.py:91
  60.8 1.9 %collective-permute-start.5 = (f32[20,1280]{1,0:T(8,128)S(1)}, f32[20,1280]{1,0:T(8,128)S(1)}, u32[]{:S(2)}, u32[]{:S(2)}) collective-permute-start(f32[20,1280]{1,0:T(8,128)S(1)} %get-tuple-element.19), channel_id=1, source_target_pairs={{0,192},{12,36},{24,216},{36,12},{48,240},{60,84},{72,264},{84,60}... | collective-permute-start | bytes 307208 | tf_op jit(solution)/shard_map/ppermute | solution.py:91
  62.8 5.7 %collective-permute-start.4 = (f32[20,1280]{1,0:T(8,128)S(1)}, f32[20,1280]{1,0:T(8,128)S(1)}, u32[]{:S(2)}, u32[]{:S(2)}) collective-permute-start(f32[20,1280]{1,0:T(8,128)S(1)} %get-tuple-element.17), channel_id=1, source_target_pairs={{0,384},{12,60},{24,408},{36,84},{48,432},{60,12},{72,456},{84,36}... | collective-permute-start | bytes 307208 | tf_op jit(solution)/shard_map/ppermute | solution.py:91
  68.5 1.2 fusion
  69.7 0.0 collective-permute-done.6
  69.7 0.0 collective-permute-done.5
  69.7 1.1 collective-permute-done.4
  70.8 0.7 constant_dynamic-slice_fusion
  71.5 1.9 %collective-permute-start.7 = (f32[10,1280]{1,0:T(8,128)}, f32[10,1280]{1,0:T(8,128)}, u32[]{:S(2)}, u32[]{:S(2)}) collective-permute-start(f32[10,1280]{1,0:T(8,128)} %constant_dynamic-slice_fusion), channel_id=1, source_target_pairs={{0,96},{12,108},{24,120},{36,132},{48,144},{60,156},{72,168},{84,1... | collective-permute-start | bytes 153608 | tf_op jit(solution)/shard_map/ppermute | solution.py:91
  73.4 0.7 convolution_bitcast_fusion
  74.1 2.8 %collective-permute-done.7 = f32[10,1280]{1,0:T(8,128)} collective-permute-done((f32[10,1280]{1,0:T(8,128)}, f32[10,1280]{1,0:T(8,128)}, u32[]{:S(2)}, u32[]{:S(2)}) %collective-permute-start.7) | collective-permute-done | bytes 51232 | tf_op jit(solution)/shard_map/ppermute | solution.py:91
  77.0 1.5 %dynamic-slice_add_fusion = f32[10,1280]{1,0:T(8,128)} fusion(f32[10,1280]{1,0:T(8,128)} %collective-permute-done.7, f32[20,1280]{1,0:T(8,128)S(1)} %add_add_fusion.1, s32[]{:T(128)S(6)} %select_n.227), kind=kLoop, calls=%fused_computation.54 | loop fusion | flops 12800 | bytes 153604 | tf_op jit(solution)/shard_map/add | solution.py:91
  78.5 4.7 %collective-permute-start.8 = (f32[10,1280]{1,0:T(8,128)}, f32[10,1280]{1,0:T(8,128)S(1)}, u32[]{:S(2)}, u32[]{:S(2)}) collective-permute-start(f32[10,1280]{1,0:T(8,128)} %dynamic-slice_add_fusion), channel_id=1, source_target_pairs={{0,3},{1,2},{2,1},{3,0},{4,7},{5,6},{6,5},{7,4},{8,11},{9,10},{10,... | collective-permute-start | bytes 153608 | tf_op jit(solution)/shard_map/ppermute | solution.py:104
  83.2 1.9 %collective-permute-start.9 = (f32[10,1280]{1,0:T(8,128)}, f32[10,1280]{1,0:T(8,128)S(1)}, u32[]{:S(2)}, u32[]{:S(2)}) collective-permute-start(f32[10,1280]{1,0:T(8,128)} %dynamic-slice_add_fusion), channel_id=1, source_target_pairs={{0,2},{1,3},{2,0},{3,1},{4,6},{5,7},{6,4},{7,5},{8,10},{9,11},{10,... | collective-permute-start | bytes 153608 | tf_op jit(solution)/shard_map/ppermute | solution.py:104
  85.1 2.7 %collective-permute-start.10 = (f32[10,1280]{1,0:T(8,128)}, f32[10,1280]{1,0:T(8,128)}, u32[]{:S(2)}, u32[]{:S(2)}) collective-permute-start(f32[10,1280]{1,0:T(8,128)} %dynamic-slice_add_fusion), channel_id=1, source_target_pairs={{0,1},{1,0},{2,3},{3,2},{4,5},{5,4},{6,7},{7,6},{8,9},{9,8},{10,11... | collective-permute-start | bytes 153608 | tf_op jit(solution)/shard_map/ppermute | solution.py:104
  87.8 1.3 %convolution_bitcast_fusion.1 = f32[2,64,8,1,80]{4,1,2,0,3:T(8,128)} fusion(f32[2,8,64,64]{2,3,1,0:T(8,128)S(1)} %get-tuple-element.7, pred[2,8,64,64]{2,3,1,0:T(32,128)(4,1)S(1)} %copy-done.8, f32[2,8,64]{2,1,0:T(8,128)S(1)} %bitcast_divide_fusion, pred[2,64]{1,0:T(4,128)(4,1)S(1)} %copy-done.14, bf16[2,64,8,1,80]{4,3,2,1,0:T(2,128)(2,1)S(1)} %get-tuple-element.14), kind=kOutput, calls=%fused_computation.5 | convolution fusion | flops 63176704 | bytes 823424 | tf_op jit(solution)/shard_map/transpose(jvp(wphc,wqhc->whpq))/dot_general | solution.py:21
  89.1 1.1 collective-permute-done.9
  90.2 2.3 %collective-permute-done.10 = f32[10,1280]{1,0:T(8,128)} collective-permute-done((f32[10,1280]{1,0:T(8,128)}, f32[10,1280]{1,0:T(8,128)}, u32[]{:S(2)}, u32[]{:S(2)}) %collective-permute-start.10) | collective-permute-done | bytes 51232 | tf_op jit(solution)/shard_map/ppermute | solution.py:104
  92.5 1.0 select_add_fusion
  93.4 12.4 %collective-permute-start.11 = (f32[10,1280]{1,0:T(8,128)S(1)}, f32[10,1280]{1,0:T(8,128)}, u32[]{:S(2)}, u32[]{:S(2)}) collective-permute-start(f32[10,1280]{1,0:T(8,128)S(1)} %select_add_fusion), channel_id=1, source_target_pairs={{0,8},{1,9},{2,10},{3,11},{4,0},{5,1},{6,2},{7,3},{8,4},{9,5},{10,... | collective-permute-start | bytes 153608 | tf_op jit(solution)/shard_map/ppermute | solution.py:119
  105.9 1.9 %collective-permute-start.12 = (f32[10,1280]{1,0:T(8,128)S(1)}, f32[10,1280]{1,0:T(8,128)}, u32[]{:S(2)}, u32[]{:S(2)}) collective-permute-start(f32[10,1280]{1,0:T(8,128)S(1)} %select_add_fusion), channel_id=1, source_target_pairs={{0,4},{1,5},{2,6},{3,7},{4,8},{5,9},{6,10},{7,11},{8,0},{9,1},{10,... | collective-permute-start | bytes 153608 | tf_op jit(solution)/shard_map/ppermute | solution.py:119
  107.8 1.4 %add_convert_fusion = bf16[2,64,8,3,80]{4,1,2,0,3:T(8,128)(2,1)S(1)} fusion(f32[2,64,8,1,80]{4,1,2,0,3:T(8,128)S(1)} %convolution_bitcast_fusion, f32[2,64,8,1,80]{4,1,2,0,3:T(8,128)} %convolution_bitcast_fusion.1, f32[2,64,8,1,80]{4,1,2,0,3:T(8,128)} %convolution_bitcast_fusion.2), kind=kLoop, calls=%fused_computation.3 | loop fusion | flops 737280 | bytes 1474560 | tf_op jit(solution)/shard_map/transpose(jvp())/convert_element_type | solution.py:15
  109.3 0.7 copy.27
  109.9 1.7 %reshape.77 = bf16[1,128,1920]{2,1,0:T(8,128)(2,1)} reshape(bf16[2,64,8,3,80]{4,3,2,1,0:T(4,128)(2,1)S(1)} %copy.27) | data formatting | bytes 983040
  111.7 6.7 %collective-permute-done.12 = f32[10,1280]{1,0:T(8,128)} collective-permute-done((f32[10,1280]{1,0:T(8,128)S(1)}, f32[10,1280]{1,0:T(8,128)}, u32[]{:S(2)}, u32[]{:S(2)}) %collective-permute-start.12) | collective-permute-done | bytes 51232 | tf_op jit(solution)/shard_map/ppermute | solution.py:119
  118.4 1.6 %add_multiply_fusion.1 = f32[10,1280]{1,0:T(8,128)} fusion(f32[10,1280]{1,0:T(8,128)} %collective-permute-done.11, f32[10,1280]{1,0:T(8,128)} %collective-permute-done.12, f32[10,1280]{1,0:T(8,128)S(1)} %select_add_fusion, pred[]{:T(512)S(6)} %eq.93, pred[]{:T(512)S(6)} %eq.92, pred[]{:T(512)S(6)} %eq.91, pred[]{:T(512)S(6)} %eq.90, pred[]{:T(512)S(6)} %eq.89, ...), kind=kLoop, calls=%fused_computation.52 | loop fusion | flops 115200 | bytes 204806 | tf_op jit(solution)/shard_map/mul | solution.py:144
  (32 shorter events, 0.1 us)
Async XLA Ops:
  0.6 25.5 %copy-start = (bf16[640,1280]{1,0:T(8,128)(2,1)S(1)}, bf16[640,1280]{1,0:T(8,128)(2,1)}, u32[]{:S(2)}) copy-start(bf16[640,1280]{1,0:T(8,128)(2,1)} %param.6) | copy-start | bytes 4915204
  1.4 4.5 %copy-start.11 = (pred[2,64]{1,0:T(4,128)(4,1)}, pred[2,64]{1,0:T(4,128)(4,1)S(1)}, u32[]{:S(2)}) copy-start(pred[2,64]{1,0:T(4,128)(4,1)S(1)} %add_compare_fusion) | copy-start | bytes 388
  5.5 0.8 copy-start.2
  5.5 1.0 copy-start.7
  7.5 2.7 %copy-start.1 = (bf16[1,128,1280]{2,1,0:T(8,128)(2,1)S(1)}, bf16[1,128,1280]{2,1,0:T(8,128)(2,1)}, u32[]{:S(2)}) copy-start(bf16[1,128,1280]{2,1,0:T(8,128)(2,1)} %param.5) | copy-start | bytes 983044
  9.2 15.9 %copy-start.4 = (bf16[2,64,8,80]{3,1,2,0:T(8,128)(2,1)S(1)}, bf16[2,64,8,80]{3,1,2,0:T(8,128)(2,1)}, u32[]{:S(2)}) copy-start(bf16[2,64,8,80]{3,1,2,0:T(8,128)(2,1)} %fusion.4) | copy-start | bytes 491524
  12.6 19.3 %collective-permute-start = (f32[320,1280]{1,0:T(8,128)}, f32[320,1280]{1,0:T(8,128)}, u32[]{:S(2)}, u32[]{:S(2)}) collective-permute-start(f32[320,1280]{1,0:T(8,128)} %fusion.9), channel_id=1, source_target_pairs={{0,12},{12,0},{24,36},{36,24},{48,60},{60,48},{72,84},{84,72},{96,... | collective-permute-start | bytes 4915208 | tf_op jit(solution)/shard_map/ppermute | solution.py:76
  26.1 1.7 %copy-start.12 = (pred[2,64]{1,0:T(4,128)(4,1)S(1)}, pred[2,64]{1,0:T(4,128)(4,1)}, u32[]{:S(2)}) copy-start(pred[2,64]{1,0:T(4,128)(4,1)} %copy-done.11) | copy-start | bytes 388
  33.8 11.7 %copy-start.6 = (f32[2,64,8,80]{3,2,1,0:T(8,128)S(1)}, f32[2,64,8,80]{3,2,1,0:T(8,128)}, u32[]{:S(2)}) copy-start(f32[2,64,8,80]{3,2,1,0:T(8,128)} %reshape.76) | copy-start | bytes 983044
  33.8 11.7 %copy-start.13 = (pred[2,64]{1,0:T(4,128)(4,1)S(1)}, pred[2,64]{1,0:T(4,128)(4,1)}, u32[]{:S(2)}) copy-start(pred[2,64]{1,0:T(4,128)(4,1)} %copy-done.11) | copy-start | bytes 388
  33.9 12.9 %copy-start.9 = (f32[2,8,64,1]{2,1,0,3:T(8,128)S(1)}, f32[2,8,64,1]{2,1,0,3:T(8,128)}, u32[]{:S(2)}) copy-start(f32[2,8,64,1]{2,1,0,3:T(8,128)} %negate_bitcast_fusion) | copy-start | bytes 12292
  33.9 12.9 %copy-start.10 = (f32[2,8,64]{2,1,0:T(8,128)S(1)}, f32[2,8,64]{2,1,0:T(8,128)}, u32[]{:S(2)}) copy-start(f32[2,8,64]{2,1,0:T(8,128)} %get-tuple-element.8) | copy-start | bytes 12292
  33.9 12.9 %collective-permute-start.3 = (f32[80,1280]{1,0:T(8,128)S(1)}, f32[80,1280]{1,0:T(8,128)S(1)}, u32[]{:S(2)}, u32[]{:S(2)}) collective-permute-start(f32[80,1280]{1,0:T(8,128)S(1)} %get-tuple-element.11), channel_id=1, source_target_pairs={{0,72},{12,588},{24,48},{36,612},{48,24},{60,636},{72,0},{84,660},... | collective-permute-start | bytes 1228808 | tf_op jit(solution)/shard_map/ppermute | solution.py:91
  36.0 20.1 %collective-permute-start.2 = (f32[80,1280]{1,0:T(8,128)S(1)}, f32[80,1280]{1,0:T(8,128)S(1)}, u32[]{:S(2)}, u32[]{:S(2)}) collective-permute-start(f32[80,1280]{1,0:T(8,128)S(1)} %get-tuple-element.12), channel_id=1, source_target_pairs={{0,24},{12,204},{24,0},{36,228},{48,72},{60,252},{72,48},{84,276},... | collective-permute-start | bytes 1228808 | tf_op jit(solution)/shard_map/ppermute | solution.py:91
  37.9 20.7 %collective-permute-start.1 = (f32[80,1280]{1,0:T(8,128)S(1)}, f32[80,1280]{1,0:T(8,128)S(1)}, u32[]{:S(2)}, u32[]{:S(2)}) collective-permute-start(f32[80,1280]{1,0:T(8,128)S(1)} %get-tuple-element.10), channel_id=1, source_target_pairs={{0,48},{12,396},{24,72},{36,420},{48,0},{60,444},{72,24},{84,468},... | collective-permute-start | bytes 1228808 | tf_op jit(solution)/shard_map/ppermute | solution.py:91
  46.8 21.7 %copy-start.5 = (bf16[128,640]{1,0:T(8,128)(2,1)S(1)}, bf16[128,640]{1,0:T(8,128)(2,1)}, u32[]{:S(2)}) copy-start(bf16[128,640]{1,0:T(8,128)(2,1)} %reshape.72) | copy-start | bytes 491524
  58.8 14.6 %copy-start.3 = (bf16[2,64,8,1,80]{4,3,2,1,0:T(2,128)(2,1)S(1)}, bf16[2,64,8,1,80]{4,3,2,1,0:T(2,128)(2,1)}, u32[]{:S(2)}) copy-start(bf16[2,64,8,1,80]{4,3,2,1,0:T(2,128)(2,1)} %copy-done.2) | copy-start | bytes 491524
  58.8 14.6 %copy-start.8 = (pred[2,8,64,64]{2,3,1,0:T(32,128)(4,1)S(1)}, pred[2,8,64,64]{2,3,1,0:T(32,128)(4,1)}, u32[]{:S(2)}) copy-start(pred[2,8,64,64]{2,3,1,0:T(32,128)(4,1)} %get-tuple-element.9) | copy-start | bytes 196612
  58.8 10.9 %collective-permute-start.6 = (f32[20,1280]{1,0:T(8,128)S(1)}, f32[20,1280]{1,0:T(8,128)S(1)}, u32[]{:S(2)}, u32[]{:S(2)}) collective-permute-start(f32[20,1280]{1,0:T(8,128)S(1)} %get-tuple-element.18), channel_id=1, source_target_pairs={{0,576},{12,84},{24,600},{36,60},{48,624},{60,36},{72,648},{84,12}... | collective-permute-start | bytes 307208 | tf_op jit(solution)/shard_map/ppermute | solution.py:91
  60.8 8.9 %collective-permute-start.5 = (f32[20,1280]{1,0:T(8,128)S(1)}, f32[20,1280]{1,0:T(8,128)S(1)}, u32[]{:S(2)}, u32[]{:S(2)}) collective-permute-start(f32[20,1280]{1,0:T(8,128)S(1)} %get-tuple-element.19), channel_id=1, source_target_pairs={{0,192},{12,36},{24,216},{36,12},{48,240},{60,84},{72,264},{84,60}... | collective-permute-start | bytes 307208 | tf_op jit(solution)/shard_map/ppermute | solution.py:91
  62.8 8.0 %collective-permute-start.4 = (f32[20,1280]{1,0:T(8,128)S(1)}, f32[20,1280]{1,0:T(8,128)S(1)}, u32[]{:S(2)}, u32[]{:S(2)}) collective-permute-start(f32[20,1280]{1,0:T(8,128)S(1)} %get-tuple-element.17), channel_id=1, source_target_pairs={{0,384},{12,60},{24,408},{36,84},{48,432},{60,12},{72,456},{84,36}... | collective-permute-start | bytes 307208 | tf_op jit(solution)/shard_map/ppermute | solution.py:91
  69.7 18.1 %copy-start.14 = (pred[2,64]{1,0:T(4,128)(4,1)S(1)}, pred[2,64]{1,0:T(4,128)(4,1)}, u32[]{:S(2)}) copy-start(pred[2,64]{1,0:T(4,128)(4,1)} %copy-done.11) | copy-start | bytes 388
  71.5 5.5 %collective-permute-start.7 = (f32[10,1280]{1,0:T(8,128)}, f32[10,1280]{1,0:T(8,128)}, u32[]{:S(2)}, u32[]{:S(2)}) collective-permute-start(f32[10,1280]{1,0:T(8,128)} %constant_dynamic-slice_fusion), channel_id=1, source_target_pairs={{0,96},{12,108},{24,120},{36,132},{48,144},{60,156},{72,168},{84,1... | collective-permute-start | bytes 153608 | tf_op jit(solution)/shard_map/ppermute | solution.py:91
  78.5 10.6 %collective-permute-start.8 = (f32[10,1280]{1,0:T(8,128)}, f32[10,1280]{1,0:T(8,128)S(1)}, u32[]{:S(2)}, u32[]{:S(2)}) collective-permute-start(f32[10,1280]{1,0:T(8,128)} %dynamic-slice_add_fusion), channel_id=1, source_target_pairs={{0,3},{1,2},{2,1},{3,0},{4,7},{5,6},{6,5},{7,4},{8,11},{9,10},{10,... | collective-permute-start | bytes 153608 | tf_op jit(solution)/shard_map/ppermute | solution.py:104
  83.2 7.0 %collective-permute-start.9 = (f32[10,1280]{1,0:T(8,128)}, f32[10,1280]{1,0:T(8,128)S(1)}, u32[]{:S(2)}, u32[]{:S(2)}) collective-permute-start(f32[10,1280]{1,0:T(8,128)} %dynamic-slice_add_fusion), channel_id=1, source_target_pairs={{0,2},{1,3},{2,0},{3,1},{4,6},{5,7},{6,4},{7,5},{8,10},{9,11},{10,... | collective-permute-start | bytes 153608 | tf_op jit(solution)/shard_map/ppermute | solution.py:104
  85.1 7.4 %collective-permute-start.10 = (f32[10,1280]{1,0:T(8,128)}, f32[10,1280]{1,0:T(8,128)}, u32[]{:S(2)}, u32[]{:S(2)}) collective-permute-start(f32[10,1280]{1,0:T(8,128)} %dynamic-slice_add_fusion), channel_id=1, source_target_pairs={{0,1},{1,0},{2,3},{3,2},{4,5},{5,4},{6,7},{7,6},{8,9},{9,8},{10,11... | collective-permute-start | bytes 153608 | tf_op jit(solution)/shard_map/ppermute | solution.py:104
  93.4 18.2 %collective-permute-start.11 = (f32[10,1280]{1,0:T(8,128)S(1)}, f32[10,1280]{1,0:T(8,128)}, u32[]{:S(2)}, u32[]{:S(2)}) collective-permute-start(f32[10,1280]{1,0:T(8,128)S(1)} %select_add_fusion), channel_id=1, source_target_pairs={{0,8},{1,9},{2,10},{3,11},{4,0},{5,1},{6,2},{7,3},{8,4},{9,5},{10,... | collective-permute-start | bytes 153608 | tf_op jit(solution)/shard_map/ppermute | solution.py:119
  105.9 12.5 %collective-permute-start.12 = (f32[10,1280]{1,0:T(8,128)S(1)}, f32[10,1280]{1,0:T(8,128)}, u32[]{:S(2)}, u32[]{:S(2)}) collective-permute-start(f32[10,1280]{1,0:T(8,128)S(1)} %select_add_fusion), channel_id=1, source_target_pairs={{0,4},{1,5},{2,6},{3,7},{4,8},{5,9},{6,10},{7,11},{8,0},{9,1},{10,... | collective-permute-start | bytes 153608 | tf_op jit(solution)/shard_map/ppermute | solution.py:119

commit v7 on v5

--- a/solution.py
+++ b/solution.py
@@ -82,7 +82,7 @@
             mine = mine | (((rank >> bit) & 1) << (len(even_bits) - 1 - k))
         part = current.shape[0] // count
         total = lax.dynamic_slice_in_dim(current, mine * part, part, axis=0)
-        for delta in range(1, count):
+        for delta in range(count - 1, 0, -1):
             send = lax.dynamic_slice_in_dim(current, (mine ^ delta) * part, part, axis=0)
             pairs = [
                 (i, i ^ spread(odd_bits if i & 1 else even_bits, delta))

time: 118 us -> 116 us (0.983)
  the two profiles are of different devices: /device:TPU:1 before, /device:TPU:41 now
where the time goes in v7:
time: 116 us; the launch traced here: 115 us
  starting transfers between devices  50.6 us (44%)
  waiting for transfers between devices  29.8 us (26%)
  matrix products  14 us (12%)
  local copies, waits for them, and re-layouts  12.4 us (11%)
  other arithmetic  6.75 us (6%)
  between operations  1.96 us (2%)
    ppermute x7, starting transfers between devices, reduce_rows(): total = total + lax.ppermute(send, 'row', pairs)  22.6 us
    ppermute x7, waiting for transfers between devices, reduce_rows(): total = total + lax.ppermute(send, 'row', pairs)  22.3 us
    ppermute x2, starting transfers between devices, sum_cols(): parts.append(lax.ppermute(share, 'col', pairs))  13.7 us
    ppermute x3, starting transfers between devices, sum_cols(): lax.ppermute(share, 'col', [(i, i ^ delta) for i in range(col_total)])  11.7 us
    dot_general x3, matrix products, attend(): jnp.einsum('whpq,wqhc->wphc', probs.astype(jnp.float32), value, precision...  5.64 us
    ppermute x2, waiting for transfers between devices, sum_cols(): parts.append(lax.ppermute(share, 'col', pairs))  5.57 us
    dot_general x2, matrix products, product(): lax.dot_general(picked, grad_rows, (((0,), (0,)), ((), ())), preferred_el...  4.25 us
    unnamed x32, local copies, waits for them, and re-layouts  3.02 us
  transfers between devices with their start and end apart: 13, of which 9 were waited for; matrix products, arithmetic and copies ran while one was open for 13% of the time, Pallas kernels for 0%

profile of v7, /device:TPU:41, one launch (start us, length us, event | category | flops | bytes accessed | tf_op | source)
XLA Modules:
  0.0 115.5 jit_solution(17534602515568804362)
XLA Ops:
  0.6 0.0 copy-start
  1.4 3.0 %reshape.78 = bf16[2,64,8,3,80]{4,3,2,1,0:T(4,128)(2,1)S(1)} reshape(bf16[1,128,1920]{2,1,0:T(8,128)(2,1)} %param.4) | data formatting | bytes 983040 | tf_op jit(solution)/shard_map/jvp()/reshape;squeeze | solution.py:15
  4.4 1.1 fusion.36
  5.5 0.3 fusion.37
  5.8 0.1 fusion.8
  6.0 0.4 copy-done.2
  6.3 0.2 copy-done.7
  6.5 1.0 fusion.4
  7.5 1.3 %copy.20 = bf16[2,64,8,80]{1,0,2,3:T(2,128)(2,1)S(1)} copy(bf16[2,64,8,80]{3,1,2,0:T(8,128)(2,1)} %fusion.4) | data formatting | bytes 327680 | tf_op jit(solution)/shard_map/jvp()/convert_element_type | solution.py:31
  8.8 0.2 reshape.74
  9.0 0.1 slice_bitcast_fusion.1
  9.1 0.1 copy.61
  9.2 0.0 copy-start.4
  9.2 0.2 pad_maximum_fusion
  9.4 0.1 copy.23
  9.5 0.7 reshape.75
  10.2 2.4 %fusion.9 = f32[320,1280]{1,0:T(8,128)} fusion(bf16[1,128,1280]{2,1,0:T(8,128)(2,1)S(1)} %copy-done.1, bf16[128,640]{0,1:T(8,128)(2,1)} %reshape.75, s32[]{:T(128)S(6)} %select_n.214), kind=kOutput, calls=%fused_computation.27 | convolution fusion | flops 104857600 | bytes 2048004 | tf_op jit(solution)/shard_map/dot_general | solution.py:70
  12.6 2.6 %collective-permute-start = (f32[320,1280]{1,0:T(8,128)}, f32[320,1280]{1,0:T(8,128)}, u32[]{:S(2)}, u32[]{:S(2)}) collective-permute-start(f32[320,1280]{1,0:T(8,128)} %fusion.9), channel_id=1, source_target_pairs={{0,12},{12,0},{24,36},{36,24},{48,60},{60,48},{72,84},{84,72},{96,... | collective-permute-start | bytes 4915208 | tf_op jit(solution)/shard_map/ppermute | solution.py:76
  15.2 0.2 copy.16
  15.5 0.9 reshape.72
  16.3 0.6 fusion.5
  17.0 1.0 reshape.76
  18.0 3.3 %convert_reduce_fusion = (f32[2,8,64]{2,1,0:T(8,128)}, pred[2,8,64,64]{2,3,1,0:T(32,128)(4,1)}, f32[2,8,64]{2,1,0:T(8,128)S(1)}, f32[2,8,64,64]{2,3,1,0:T(8,128)S(1)}) fusion(f32[2,8,64,64]{2,3,1,0:T(8,128)S(1)} %get-tuple-element.23, f32[2,8,64]{2,1,0:T(8,128)S(1)} %get-tuple-element.22, f32[2,8,64]{2,1,0:T(8,128)S(1)} %get-tuple-element.22, ...), kind=kOutput, calls=%fused_computation.20 | convolution fusion | flops 63584256 | bytes 1101952 | tf_op jit(solution)/shard_map/transpose(jvp(whpq,wqhc->wphc))/dot_general | solution.py:27
  21.3 0.2 fusion.35
  21.5 0.6 negate_bitcast_fusion
  22.1 0.0 collective-permute-done
  22.1 1.8 %convolution_add_fusion = f32[320,1280]{1,0:T(8,128)S(1)} fusion(f32[320,1280]{1,0:T(8,128)} %collective-permute-done, bf16[1,128,1280]{2,1,0:T(8,128)(2,1)S(1)} %copy-done.1, bf16[128,640]{0,1:T(8,128)(2,1)} %reshape.75, s32[]{:T(128)S(6)} %select_n.213), kind=kOutput, calls=%fused_computation | convolution fusion | flops 105267200 | bytes 3686404 | tf_op jit(solution)/shard_map/dot_general | solution.py:70
  24.0 0.1 constant_dynamic-slice_fusion.6
  24.1 0.0 copy-start.10
  24.1 2.5 %collective-permute-start.3 = (f32[80,1280]{1,0:T(8,128)S(1)}, f32[80,1280]{1,0:T(8,128)S(1)}, u32[]{:S(2)}, u32[]{:S(2)}) collective-permute-start(f32[80,1280]{1,0:T(8,128)S(1)} %get-tuple-element.11), channel_id=1, source_target_pairs={{0,48},{12,204},{24,72},{36,228},{48,0},{60,252},{72,24},{84,276},... | collective-permute-start | bytes 1228808 | tf_op jit(solution)/shard_map/ppermute | solution.py:91
  26.7 3.0 %collective-permute-start.2 = (f32[80,1280]{1,0:T(8,128)S(1)}, f32[80,1280]{1,0:T(8,128)S(1)}, u32[]{:S(2)}, u32[]{:S(2)}) collective-permute-start(f32[80,1280]{1,0:T(8,128)S(1)} %get-tuple-element.12), channel_id=1, source_target_pairs={{0,24},{12,108},{24,0},{36,132},{48,72},{60,156},{72,48},{84,180},... | collective-permute-start | bytes 1228808 | tf_op jit(solution)/shard_map/ppermute | solution.py:91
  29.7 3.0 %collective-permute-start.1 = (f32[80,1280]{1,0:T(8,128)S(1)}, f32[80,1280]{1,0:T(8,128)S(1)}, u32[]{:S(2)}, u32[]{:S(2)}) collective-permute-start(f32[80,1280]{1,0:T(8,128)S(1)} %get-tuple-element.10), channel_id=1, source_target_pairs={{0,72},{12,300},{24,48},{36,324},{48,24},{60,348},{72,0},{84,372},... | collective-permute-start | bytes 1228808 | tf_op jit(solution)/shard_map/ppermute | solution.py:91
  32.7 1.3 %convolution_bitcast_fusion.2 = f32[2,64,8,1,80]{4,1,2,0,3:T(8,128)} fusion(f32[2,64,8,80]{3,2,1,0:T(8,128)S(1)} %copy-done.6, pred[2,64]{1,0:T(4,128)(4,1)S(1)} %copy-done.13, f32[2,8,64,64]{2,3,1,0:T(8,128)S(1)} %get-tuple-element.23, f32[2,8,64]{2,1,0:T(8,128)S(1)} %fusion.8, f32[2,8,64]{2,1,0:T(8,128)S(1)} %get-tuple-element.22), kind=kOutput, calls=%fused_computation.6 | convolution fusion | flops 63193088 | bytes 925824 | tf_op jit(solution)/shard_map/transpose(jvp(whpq,wqhc->wphc))/dot_general | solution.py:27
  34.0 2.0 %collective-permute-done.3 = f32[80,1280]{1,0:T(8,128)S(1)} collective-permute-done((f32[80,1280]{1,0:T(8,128)S(1)}, f32[80,1280]{1,0:T(8,128)S(1)}, u32[]{:S(2)}, u32[]{:S(2)}) %collective-permute-start.3) | collective-permute-done | bytes 409632 | tf_op jit(solution)/shard_map/ppermute | solution.py:91
  36.0 7.1 %collective-permute-done.2 = f32[80,1280]{1,0:T(8,128)S(1)} collective-permute-done((f32[80,1280]{1,0:T(8,128)S(1)}, f32[80,1280]{1,0:T(8,128)S(1)}, u32[]{:S(2)}, u32[]{:S(2)}) %collective-permute-start.2) | collective-permute-done | bytes 409632 | tf_op jit(solution)/shard_map/ppermute | solution.py:91
  43.1 3.8 %collective-permute-done.1 = f32[80,1280]{1,0:T(8,128)S(1)} collective-permute-done((f32[80,1280]{1,0:T(8,128)S(1)}, f32[80,1280]{1,0:T(8,128)S(1)}, u32[]{:S(2)}, u32[]{:S(2)}) %collective-permute-start.1) | collective-permute-done | bytes 409632 | tf_op jit(solution)/shard_map/ppermute | solution.py:91
  46.9 0.1 add_add_fusion
  47.0 0.1 constant_dynamic-slice_fusion.3
  47.1 7.0 %collective-permute-start.6 = (f32[20,1280]{1,0:T(8,128)S(1)}, f32[20,1280]{1,0:T(8,128)S(1)}, u32[]{:S(2)}, u32[]{:S(2)}) collective-permute-start(f32[20,1280]{1,0:T(8,128)S(1)} %get-tuple-element.18), channel_id=1, source_target_pairs={{0,192},{12,60},{24,216},{36,84},{48,240},{60,12},{72,264},{84,36}... | collective-permute-start | bytes 307208 | tf_op jit(solution)/shard_map/ppermute | solution.py:91
  54.1 2.2 %collective-permute-start.5 = (f32[20,1280]{1,0:T(8,128)S(1)}, f32[20,1280]{1,0:T(8,128)S(1)}, u32[]{:S(2)}, u32[]{:S(2)}) collective-permute-start(f32[20,1280]{1,0:T(8,128)S(1)} %get-tuple-element.19), channel_id=1, source_target_pairs={{0,96},{12,36},{24,120},{36,12},{48,144},{60,84},{72,168},{84,60},... | collective-permute-start | bytes 307208 | tf_op jit(solution)/shard_map/ppermute | solution.py:91
  56.3 1.9 %collective-permute-start.4 = (f32[20,1280]{1,0:T(8,128)S(1)}, f32[20,1280]{1,0:T(8,128)S(1)}, u32[]{:S(2)}, u32[]{:S(2)}) collective-permute-start(f32[20,1280]{1,0:T(8,128)S(1)} %get-tuple-element.17), channel_id=1, source_target_pairs={{0,288},{12,84},{24,312},{36,60},{48,336},{60,36},{72,360},{84,12}... | collective-permute-start | bytes 307208 | tf_op jit(solution)/shard_map/ppermute | solution.py:91
  58.2 1.2 %fusion = bf16[1,128,1280]{2,1,0:T(8,128)(2,1)} fusion(bf16[128,640]{1,0:T(8,128)(2,1)S(1)} %copy-done.5, bf16[640,1280]{1,0:T(8,128)(2,1)S(1)} %copy-done), kind=kOutput, calls=%fused_computation.2 | convolution fusion | flops 209879040 | bytes 2129920 | tf_op jit(solution)/shard_map/dot_general | solution.py:140
  59.4 0.3 collective-permute-done.5
  59.7 3.4 %collective-permute-done.4 = f32[20,1280]{1,0:T(8,128)S(1)} collective-permute-done((f32[20,1280]{1,0:T(8,128)S(1)}, f32[20,1280]{1,0:T(8,128)S(1)}, u32[]{:S(2)}, u32[]{:S(2)}) %collective-permute-start.4) | collective-permute-done | bytes 102432 | tf_op jit(solution)/shard_map/ppermute | solution.py:91
  63.1 0.7 constant_dynamic-slice_fusion
  63.8 3.0 %collective-permute-start.7 = (f32[10,1280]{1,0:T(8,128)}, f32[10,1280]{1,0:T(8,128)}, u32[]{:S(2)}, u32[]{:S(2)}) collective-permute-start(f32[10,1280]{1,0:T(8,128)} %constant_dynamic-slice_fusion), channel_id=1, source_target_pairs={{0,384},{12,396},{24,408},{36,420},{48,432},{60,444},{72,456},{84,... | collective-permute-start | bytes 153608 | tf_op jit(solution)/shard_map/ppermute | solution.py:91
  66.8 0.7 convolution_bitcast_fusion
  67.6 5.6 %collective-permute-done.7 = f32[10,1280]{1,0:T(8,128)} collective-permute-done((f32[10,1280]{1,0:T(8,128)}, f32[10,1280]{1,0:T(8,128)}, u32[]{:S(2)}, u32[]{:S(2)}) %collective-permute-start.7) | collective-permute-done | bytes 51232 | tf_op jit(solution)/shard_map/ppermute | solution.py:91
  73.2 1.5 %dynamic-slice_add_fusion = f32[10,1280]{1,0:T(8,128)} fusion(f32[10,1280]{1,0:T(8,128)} %collective-permute-done.7, f32[20,1280]{1,0:T(8,128)S(1)} %add_add_fusion.1, s32[]{:T(128)S(6)} %select_n.227), kind=kLoop, calls=%fused_computation.54 | loop fusion | flops 12800 | bytes 153604 | tf_op jit(solution)/shard_map/add | solution.py:91
  74.7 7.6 %collective-permute-start.8 = (f32[10,1280]{1,0:T(8,128)}, f32[10,1280]{1,0:T(8,128)S(1)}, u32[]{:S(2)}, u32[]{:S(2)}) collective-permute-start(f32[10,1280]{1,0:T(8,128)} %dynamic-slice_add_fusion), channel_id=1, source_target_pairs={{0,3},{1,2},{2,1},{3,0},{4,7},{5,6},{6,5},{7,4},{8,11},{9,10},{10,... | collective-permute-start | bytes 153608 | tf_op jit(solution)/shard_map/ppermute | solution.py:104
  82.3 1.9 %collective-permute-start.9 = (f32[10,1280]{1,0:T(8,128)}, f32[10,1280]{1,0:T(8,128)S(1)}, u32[]{:S(2)}, u32[]{:S(2)}) collective-permute-start(f32[10,1280]{1,0:T(8,128)} %dynamic-slice_add_fusion), channel_id=1, source_target_pairs={{0,2},{1,3},{2,0},{3,1},{4,6},{5,7},{6,4},{7,5},{8,10},{9,11},{10,... | collective-permute-start | bytes 153608 | tf_op jit(solution)/shard_map/ppermute | solution.py:104
  84.3 2.2 %collective-permute-start.10 = (f32[10,1280]{1,0:T(8,128)}, f32[10,1280]{1,0:T(8,128)}, u32[]{:S(2)}, u32[]{:S(2)}) collective-permute-start(f32[10,1280]{1,0:T(8,128)} %dynamic-slice_add_fusion), channel_id=1, source_target_pairs={{0,1},{1,0},{2,3},{3,2},{4,5},{5,4},{6,7},{7,6},{8,9},{9,8},{10,11... | collective-permute-start | bytes 153608 | tf_op jit(solution)/shard_map/ppermute | solution.py:104
  86.5 1.3 %convolution_bitcast_fusion.1 = f32[2,64,8,1,80]{4,1,2,0,3:T(8,128)} fusion(f32[2,8,64,64]{2,3,1,0:T(8,128)S(1)} %get-tuple-element.7, pred[2,8,64,64]{2,3,1,0:T(32,128)(4,1)S(1)} %copy-done.8, f32[2,8,64]{2,1,0:T(8,128)S(1)} %bitcast_divide_fusion, pred[2,64]{1,0:T(4,128)(4,1)S(1)} %copy-done.14, bf16[2,64,8,1,80]{4,3,2,1,0:T(2,128)(2,1)S(1)} %get-tuple-element.14), kind=kOutput, calls=%fused_computation.5 | convolution fusion | flops 63176704 | bytes 823424 | tf_op jit(solution)/shard_map/transpose(jvp(wphc,wqhc->whpq))/dot_general | solution.py:21
  87.8 0.0 collective-permute-done.8
  87.8 0.8 collective-permute-done.9
  88.6 1.1 collective-permute-done.10
  89.8 1.0 select_add_fusion
  90.7 11.8 %collective-permute-start.11 = (f32[10,1280]{1,0:T(8,128)S(1)}, f32[10,1280]{1,0:T(8,128)}, u32[]{:S(2)}, u32[]{:S(2)}) collective-permute-start(f32[10,1280]{1,0:T(8,128)S(1)} %select_add_fusion), channel_id=1, source_target_pairs={{0,8},{1,9},{2,10},{3,11},{4,0},{5,1},{6,2},{7,3},{8,4},{9,5},{10,... | collective-permute-start | bytes 153608 | tf_op jit(solution)/shard_map/ppermute | solution.py:119
  102.5 1.9 %collective-permute-start.12 = (f32[10,1280]{1,0:T(8,128)S(1)}, f32[10,1280]{1,0:T(8,128)}, u32[]{:S(2)}, u32[]{:S(2)}) collective-permute-start(f32[10,1280]{1,0:T(8,128)S(1)} %select_add_fusion), channel_id=1, source_target_pairs={{0,4},{1,5},{2,6},{3,7},{4,8},{5,9},{6,10},{7,11},{8,0},{9,1},{10,... | collective-permute-start | bytes 153608 | tf_op jit(solution)/shard_map/ppermute | solution.py:119
  104.5 1.4 %add_convert_fusion = bf16[2,64,8,3,80]{4,1,2,0,3:T(8,128)(2,1)S(1)} fusion(f32[2,64,8,1,80]{4,1,2,0,3:T(8,128)S(1)} %convolution_bitcast_fusion, f32[2,64,8,1,80]{4,1,2,0,3:T(8,128)} %convolution_bitcast_fusion.1, f32[2,64,8,1,80]{4,1,2,0,3:T(8,128)} %convolution_bitcast_fusion.2), kind=kLoop, calls=%fused_computation.3 | loop fusion | flops 737280 | bytes 1474560 | tf_op jit(solution)/shard_map/transpose(jvp())/convert_element_type | solution.py:15
  105.9 0.7 copy.27
  106.6 1.7 %reshape.77 = bf16[1,128,1920]{2,1,0:T(8,128)(2,1)} reshape(bf16[2,64,8,3,80]{4,3,2,1,0:T(4,128)(2,1)S(1)} %copy.27) | data formatting | bytes 983040
  108.3 5.6 %collective-permute-done.12 = f32[10,1280]{1,0:T(8,128)} collective-permute-done((f32[10,1280]{1,0:T(8,128)S(1)}, f32[10,1280]{1,0:T(8,128)}, u32[]{:S(2)}, u32[]{:S(2)}) %collective-permute-start.12) | collective-permute-done | bytes 51232 | tf_op jit(solution)/shard_map/ppermute | solution.py:119
  113.9 1.6 %add_multiply_fusion.1 = f32[10,1280]{1,0:T(8,128)} fusion(f32[10,1280]{1,0:T(8,128)} %collective-permute-done.11, f32[10,1280]{1,0:T(8,128)} %collective-permute-done.12, f32[10,1280]{1,0:T(8,128)S(1)} %select_add_fusion, pred[]{:T(512)S(6)} %eq.93, pred[]{:T(512)S(6)} %eq.92, pred[]{:T(512)S(6)} %eq.91, pred[]{:T(512)S(6)} %eq.90, pred[]{:T(512)S(6)} %eq.89, ...), kind=kLoop, calls=%fused_computation.52 | loop fusion | flops 115200 | bytes 204806 | tf_op jit(solution)/shard_map/mul | solution.py:144
  (32 shorter events, 0.1 us)
Async XLA Ops:
  0.6 15.7 %copy-start = (bf16[640,1280]{1,0:T(8,128)(2,1)S(1)}, bf16[640,1280]{1,0:T(8,128)(2,1)}, u32[]{:S(2)}) copy-start(bf16[640,1280]{1,0:T(8,128)(2,1)} %param.6) | copy-start | bytes 4915204
  1.4 4.5 %copy-start.11 = (pred[2,64]{1,0:T(4,128)(4,1)}, pred[2,64]{1,0:T(4,128)(4,1)S(1)}, u32[]{:S(2)}) copy-start(pred[2,64]{1,0:T(4,128)(4,1)S(1)} %add_compare_fusion) | copy-start | bytes 388
  5.5 0.8 copy-start.2
  5.5 1.0 copy-start.7
  7.5 2.7 %copy-start.1 = (bf16[1,128,1280]{2,1,0:T(8,128)(2,1)S(1)}, bf16[1,128,1280]{2,1,0:T(8,128)(2,1)}, u32[]{:S(2)}) copy-start(bf16[1,128,1280]{2,1,0:T(8,128)(2,1)} %param.5) | copy-start | bytes 983044
  9.2 6.0 %copy-start.4 = (bf16[2,64,8,80]{3,1,2,0:T(8,128)(2,1)S(1)}, bf16[2,64,8,80]{3,1,2,0:T(8,128)(2,1)}, u32[]{:S(2)}) copy-start(bf16[2,64,8,80]{3,1,2,0:T(8,128)(2,1)} %fusion.4) | copy-start | bytes 491524
  12.6 9.5 %collective-permute-start = (f32[320,1280]{1,0:T(8,128)}, f32[320,1280]{1,0:T(8,128)}, u32[]{:S(2)}, u32[]{:S(2)}) collective-permute-start(f32[320,1280]{1,0:T(8,128)} %fusion.9), channel_id=1, source_target_pairs={{0,12},{12,0},{24,36},{36,24},{48,60},{60,48},{72,84},{84,72},{96,... | collective-permute-start | bytes 4915208 | tf_op jit(solution)/shard_map/ppermute | solution.py:76
  16.3 1.7 %copy-start.12 = (pred[2,64]{1,0:T(4,128)(4,1)S(1)}, pred[2,64]{1,0:T(4,128)(4,1)}, u32[]{:S(2)}) copy-start(pred[2,64]{1,0:T(4,128)(4,1)} %copy-done.11) | copy-start | bytes 388
  24.0 8.7 %copy-start.6 = (f32[2,64,8,80]{3,2,1,0:T(8,128)S(1)}, f32[2,64,8,80]{3,2,1,0:T(8,128)}, u32[]{:S(2)}) copy-start(f32[2,64,8,80]{3,2,1,0:T(8,128)} %reshape.76) | copy-start | bytes 983044
  24.0 8.7 %copy-start.13 = (pred[2,64]{1,0:T(4,128)(4,1)S(1)}, pred[2,64]{1,0:T(4,128)(4,1)}, u32[]{:S(2)}) copy-start(pred[2,64]{1,0:T(4,128)(4,1)} %copy-done.11) | copy-start | bytes 388
  24.1 9.9 %copy-start.9 = (f32[2,8,64,1]{2,1,0,3:T(8,128)S(1)}, f32[2,8,64,1]{2,1,0,3:T(8,128)}, u32[]{:S(2)}) copy-start(f32[2,8,64,1]{2,1,0,3:T(8,128)} %negate_bitcast_fusion) | copy-start | bytes 12292
  24.1 9.9 %copy-start.10 = (f32[2,8,64]{2,1,0:T(8,128)S(1)}, f32[2,8,64]{2,1,0:T(8,128)}, u32[]{:S(2)}) copy-start(f32[2,8,64]{2,1,0:T(8,128)} %get-tuple-element.8) | copy-start | bytes 12292
  24.1 11.9 %collective-permute-start.3 = (f32[80,1280]{1,0:T(8,128)S(1)}, f32[80,1280]{1,0:T(8,128)S(1)}, u32[]{:S(2)}, u32[]{:S(2)}) collective-permute-start(f32[80,1280]{1,0:T(8,128)S(1)} %get-tuple-element.11), channel_id=1, source_target_pairs={{0,48},{12,204},{24,72},{36,228},{48,0},{60,252},{72,24},{84,276},... | collective-permute-start | bytes 1228808 | tf_op jit(solution)/shard_map/ppermute | solution.py:91
  26.7 16.4 %collective-permute-start.2 = (f32[80,1280]{1,0:T(8,128)S(1)}, f32[80,1280]{1,0:T(8,128)S(1)}, u32[]{:S(2)}, u32[]{:S(2)}) collective-permute-start(f32[80,1280]{1,0:T(8,128)S(1)} %get-tuple-element.12), channel_id=1, source_target_pairs={{0,24},{12,108},{24,0},{36,132},{48,72},{60,156},{72,48},{84,180},... | collective-permute-start | bytes 1228808 | tf_op jit(solution)/shard_map/ppermute | solution.py:91
  29.7 17.3 %collective-permute-start.1 = (f32[80,1280]{1,0:T(8,128)S(1)}, f32[80,1280]{1,0:T(8,128)S(1)}, u32[]{:S(2)}, u32[]{:S(2)}) collective-permute-start(f32[80,1280]{1,0:T(8,128)S(1)} %get-tuple-element.10), channel_id=1, source_target_pairs={{0,72},{12,300},{24,48},{36,324},{48,24},{60,348},{72,0},{84,372},... | collective-permute-start | bytes 1228808 | tf_op jit(solution)/shard_map/ppermute | solution.py:91
  34.0 24.2 %copy-start.5 = (bf16[128,640]{1,0:T(8,128)(2,1)S(1)}, bf16[128,640]{1,0:T(8,128)(2,1)}, u32[]{:S(2)}) copy-start(bf16[128,640]{1,0:T(8,128)(2,1)} %reshape.72) | copy-start | bytes 491524
  47.1 19.7 %copy-start.3 = (bf16[2,64,8,1,80]{4,3,2,1,0:T(2,128)(2,1)S(1)}, bf16[2,64,8,1,80]{4,3,2,1,0:T(2,128)(2,1)}, u32[]{:S(2)}) copy-start(bf16[2,64,8,1,80]{4,3,2,1,0:T(2,128)(2,1)} %copy-done.2) | copy-start | bytes 491524
  47.1 19.7 %copy-start.8 = (pred[2,8,64,64]{2,3,1,0:T(32,128)(4,1)S(1)}, pred[2,8,64,64]{2,3,1,0:T(32,128)(4,1)}, u32[]{:S(2)}) copy-start(pred[2,8,64,64]{2,3,1,0:T(32,128)(4,1)} %get-tuple-element.9) | copy-start | bytes 196612
  47.1 12.3 %collective-permute-start.6 = (f32[20,1280]{1,0:T(8,128)S(1)}, f32[20,1280]{1,0:T(8,128)S(1)}, u32[]{:S(2)}, u32[]{:S(2)}) collective-permute-start(f32[20,1280]{1,0:T(8,128)S(1)} %get-tuple-element.18), channel_id=1, source_target_pairs={{0,192},{12,60},{24,216},{36,84},{48,240},{60,12},{72,264},{84,36}... | collective-permute-start | bytes 307208 | tf_op jit(solution)/shard_map/ppermute | solution.py:91
  54.1 5.6 %collective-permute-start.5 = (f32[20,1280]{1,0:T(8,128)S(1)}, f32[20,1280]{1,0:T(8,128)S(1)}, u32[]{:S(2)}, u32[]{:S(2)}) collective-permute-start(f32[20,1280]{1,0:T(8,128)S(1)} %get-tuple-element.19), channel_id=1, source_target_pairs={{0,96},{12,36},{24,120},{36,12},{48,144},{60,84},{72,168},{84,60},... | collective-permute-start | bytes 307208 | tf_op jit(solution)/shard_map/ppermute | solution.py:91
  56.3 6.8 %collective-permute-start.4 = (f32[20,1280]{1,0:T(8,128)S(1)}, f32[20,1280]{1,0:T(8,128)S(1)}, u32[]{:S(2)}, u32[]{:S(2)}) collective-permute-start(f32[20,1280]{1,0:T(8,128)S(1)} %get-tuple-element.17), channel_id=1, source_target_pairs={{0,288},{12,84},{24,312},{36,60},{48,336},{60,36},{72,360},{84,12}... | collective-permute-start | bytes 307208 | tf_op jit(solution)/shard_map/ppermute | solution.py:91
  59.4 27.1 %copy-start.14 = (pred[2,64]{1,0:T(4,128)(4,1)S(1)}, pred[2,64]{1,0:T(4,128)(4,1)}, u32[]{:S(2)}) copy-start(pred[2,64]{1,0:T(4,128)(4,1)} %copy-done.11) | copy-start | bytes 388
  63.8 9.4 %collective-permute-start.7 = (f32[10,1280]{1,0:T(8,128)}, f32[10,1280]{1,0:T(8,128)}, u32[]{:S(2)}, u32[]{:S(2)}) collective-permute-start(f32[10,1280]{1,0:T(8,128)} %constant_dynamic-slice_fusion), channel_id=1, source_target_pairs={{0,384},{12,396},{24,408},{36,420},{48,432},{60,444},{72,456},{84,... | collective-permute-start | bytes 153608 | tf_op jit(solution)/shard_map/ppermute | solution.py:91
  74.7 13.1 %collective-permute-start.8 = (f32[10,1280]{1,0:T(8,128)}, f32[10,1280]{1,0:T(8,128)S(1)}, u32[]{:S(2)}, u32[]{:S(2)}) collective-permute-start(f32[10,1280]{1,0:T(8,128)} %dynamic-slice_add_fusion), channel_id=1, source_target_pairs={{0,3},{1,2},{2,1},{3,0},{4,7},{5,6},{6,5},{7,4},{8,11},{9,10},{10,... | collective-permute-start | bytes 153608 | tf_op jit(solution)/shard_map/ppermute | solution.py:104
  82.3 6.3 %collective-permute-start.9 = (f32[10,1280]{1,0:T(8,128)}, f32[10,1280]{1,0:T(8,128)S(1)}, u32[]{:S(2)}, u32[]{:S(2)}) collective-permute-start(f32[10,1280]{1,0:T(8,128)} %dynamic-slice_add_fusion), channel_id=1, source_target_pairs={{0,2},{1,3},{2,0},{3,1},{4,6},{5,7},{6,4},{7,5},{8,10},{9,11},{10,... | collective-permute-start | bytes 153608 | tf_op jit(solution)/shard_map/ppermute | solution.py:104
  84.3 5.5 %collective-permute-start.10 = (f32[10,1280]{1,0:T(8,128)}, f32[10,1280]{1,0:T(8,128)}, u32[]{:S(2)}, u32[]{:S(2)}) collective-permute-start(f32[10,1280]{1,0:T(8,128)} %dynamic-slice_add_fusion), channel_id=1, source_target_pairs={{0,1},{1,0},{2,3},{3,2},{4,5},{5,4},{6,7},{7,6},{8,9},{9,8},{10,11... | collective-permute-start | bytes 153608 | tf_op jit(solution)/shard_map/ppermute | solution.py:104
  90.7 17.6 %collective-permute-start.11 = (f32[10,1280]{1,0:T(8,128)S(1)}, f32[10,1280]{1,0:T(8,128)}, u32[]{:S(2)}, u32[]{:S(2)}) collective-permute-start(f32[10,1280]{1,0:T(8,128)S(1)} %select_add_fusion), channel_id=1, source_target_pairs={{0,8},{1,9},{2,10},{3,11},{4,0},{5,1},{6,2},{7,3},{8,4},{9,5},{10,... | collective-permute-start | bytes 153608 | tf_op jit(solution)/shard_map/ppermute | solution.py:119
  102.5 11.4 %collective-permute-start.12 = (f32[10,1280]{1,0:T(8,128)S(1)}, f32[10,1280]{1,0:T(8,128)}, u32[]{:S(2)}, u32[]{:S(2)}) collective-permute-start(f32[10,1280]{1,0:T(8,128)S(1)} %select_add_fusion), channel_id=1, source_target_pairs={{0,4},{1,5},{2,6},{3,7},{4,8},{5,9},{6,10},{7,11},{8,0},{9,1},{10,... | collective-permute-start | bytes 153608 | tf_op jit(solution)/shard_map/ppermute | solution.py:119
